TPU v7x, 256 devices: a whole 4x4x8 slice. The times are simulated.
256 devices in a mesh: pair: 32 (over y, x, core), lam: 8 (over z).
Axes of the slice: x: 4, y: 4, z: 8, core: 2. Of those that a mesh axis runs over, the one named last changes fastest.
Arguments:
- integrals: bfloat16 [32, 64, 4, 64, 1024], P('pair', 'lam'), may hold values from -0.119628906 to 0.119628906
- tile_pair: int32 [32, 64], P('pair', 'lam'), may hold values from 0 to 15, as said below
- tile_lam: int32 [32, 64], P('pair', 'lam'), may hold values from 0 to 15, as said below
- tile_count: int32 [32, 8], P('pair', 'lam'), may hold values from 1 to 8, as said below
- mu_index: int32 [2048], P('pair'), may hold values from 0 to 1023
- nu_index: int32 [2048], P('pair'), may hold values from 0 to 1023
- occupied_coef: bfloat16 [1024, 16], replicated, may hold values from -1.5 to 1.5
- virtual_coef: bfloat16 [1024, 1280], replicated, may hold values from -1.5 to 1.5
Outputs:
- orbital_integrals: float32 [16, 1280, 20480], P('lam', 'pair')
Inputs may be any that keep to these rules, and one draw needn't show every extreme that they name: On every device the live and dead slots name distinct pairs of (tile_pair, tile_lam); tile_pair lies in 0 to 15. On lam index l every slot's tile_lam lies in l * 2 to (l + 1) * 2 - 1. Slots from tile_count on are dead and their integrals are ignored; some device has all 8 slots live.
All inputs are finite; a program needn't handle non-finite values.
Results may differ from a plain program's by a relative error of at most 0.0049.
Values may be sent and summed in bfloat16 or wider, within the bound.
No kernel may reach another device: no remote copies, remote signals or barrier semaphores. Data moves between devices by JAX's collectives and lax.ppermute only.
A program may use at most 128 MiB of HBM per device.

v0:
```python
import math

import jax
import jax.numpy as jnp
from jax import lax
from jax.sharding import PartitionSpec as P


def tile_pass(partial_value, tile_group, occ_columns):
    tile_data, pair_list, lam_list, live_total = tile_group
    tile_rows = tile_data.shape[1]
    tile_depth = tile_data.shape[2]

    def add_tile(slot_index, running):
        row_start = pair_list[slot_index] * tile_rows
        occ_rows = lax.dynamic_slice_in_dim(
            occ_columns, lam_list[slot_index] * tile_depth, tile_depth, 0
        )
        contrib = jnp.einsum(
            "rls,lj->jrs", tile_data[slot_index], occ_rows, preferred_element_type=jnp.float32
        )
        current = lax.dynamic_slice_in_dim(running, row_start, tile_rows, 1)
        return lax.dynamic_update_slice_in_dim(running, current + contrib, row_start, 1)

    return lax.fori_loop(0, live_total, add_tile, partial_value)


def on_device(
    integrals, tile_pair, tile_lam, tile_count, mu_index, nu_index, occupied_coef, virtual_coef
):
    lam_count = lax.axis_size("lam")
    pair_count = lax.axis_size("pair")
    occ_total = occupied_coef.shape[1]
    vir_total = virtual_coef.shape[1]
    basis_count = occupied_coef.shape[0]
    rows_here = mu_index.shape[0]
    tile_data = integrals[0]
    pair_list = tile_pair[0]
    lam_list = tile_lam[0]
    live_total = tile_count[0, 0]
    tile_groups = (tile_data, pair_list, lam_list, live_total)
    occ_share = occ_total // lam_count
    partial_value = jnp.zeros((occupied_coef.shape[1], rows_here, basis_count), jnp.float32)
    partial_value = tile_pass(partial_value, tile_groups, occupied_coef)
    summed = lax.psum(partial_value, "lam")
    own_half = lax.dynamic_slice_in_dim(summed, lax.axis_index("lam") * occ_share, occ_share, 0)
    vir_share = vir_total // pair_count
    half_low = own_half.astype(jnp.bfloat16).reshape(occ_share * rows_here, basis_count)
    mixed = jnp.dot(half_low, virtual_coef, preferred_element_type=jnp.float32)
    mixed = mixed.astype(jnp.bfloat16).reshape(occ_share, rows_here, pair_count, vir_share)
    first_all, second_all = (
        lax.all_gather(mu_index, "pair", axis=0, tiled=True),
        lax.all_gather(nu_index, "pair", axis=0, tiled=True),
    )
    received = lax.all_to_all(mixed, "pair", split_axis=2, concat_axis=1, tiled=True)
    item_count = received.shape[0]
    total_rows = received.shape[1]
    column_count = received.shape[3]
    mixed_rows = received.reshape(item_count, total_rows, column_count)
    row_block = math.gcd(total_rows, 256)

    def add_rows(running, row_start):
        occ_rows = jnp.take(
            occupied_coef, lax.dynamic_slice_in_dim(first_all, row_start, row_block), axis=0
        ).astype(jnp.float32)
        vir_rows = jnp.take(
            virtual_coef, lax.dynamic_slice_in_dim(second_all, row_start, row_block), axis=0
        ).astype(jnp.float32)
        weights = (
            (occ_rows[:, :, None] * vir_rows[:, None, :])
            .astype(jnp.bfloat16)
            .reshape(row_block, occ_total * vir_total)
        )
        mixed_piece = lax.dynamic_slice_in_dim(mixed_rows, row_start, row_block, 1)
        return (
            running
            + jnp.einsum("qrb,rk->qbk", mixed_piece, weights, preferred_element_type=jnp.float32),
            None,
        )

    start_total = jnp.zeros((item_count, column_count, occ_total * vir_total), jnp.float32)
    result, _ = lax.scan(
        add_rows, start_total, jnp.arange(0, total_rows, row_block, dtype=jnp.int32)
    )
    return result


def solution(mesh):
    placed = (
        P("pair", "lam", None, None, None),
        P("pair", "lam"),
        P("pair", "lam"),
        P("pair", "lam"),
        P("pair"),
        P("pair"),
        P(),
        P(),
    )
    return jax.shard_map(
        on_device, mesh=mesh, in_specs=placed, out_specs=P("lam", "pair", None), check_vma=False
    )
```

profile of v0, /device:TPU:1, one launch (start us, length us, event | category | flops | bytes accessed | tf_op | source)
XLA Modules:
  0.0 600.6 jit_solution(9514965633434375320)
XLA Ops:
  2.5 14.1 %while.21 = (s32[]{:T(128)}, f32[16,64,1024]{2,1,0:T(8,128)}, s32[]{:T(128)}, s32[8]{0:T(128)S(1)}, s32[8]{0:T(128)S(1)}, /*index=5*/bf16[1024,16]{0,1:T(8,128)(...) while((s32[]{:T(128)}, f32[16,64,1024]{2,1,0:T(8,128)}, ...), condition=%wide.region_1.0_spmd, body=%wide.region_0.0_spmd.sunk | while | flops 8454157 | bytes 2101547 | solution.py:25
  16.7 117.0 %all-reduce.4 = bf16[16,64,1024]{2,1,0:T(8,128)(2,1)} all-reduce(f32[16,64,1024]{2,1,0:T(8,128)} %get-tuple-element.85), channel_id=1, replica_groups=mesh['pair'=32,'lam'=8] {'lam'}, use_global_device_ids=true, to_apply=%region_2.0 | all-reduce | flops 1048576 | bytes 6291456 | tf_op jit(solution)/shard_map/psum | solution.py:45
  138.5 22.3 %all-to-all-start = ((bf16[32,2,2560]{2,1,0:T(2,128)(2,1)}), bf16[32,2,2560]{2,1,0:T(2,128)(2,1)}, u32[]{:S(2)}, u32[]{:S(2)}) async-start(bf16[32,2,2560]{2,1,0:T(2,128)(2,1)} %reshape.99), calls=%async_computation | async-start | bytes 655360 | tf_op jit(solution)/shard_map/all_to_all | solution.py:55
  163.5 123.2 %all-reduce.2 = (s32[2048]{0:T(1024)}, s32[2048]{0:T(1024)}) all-reduce(s32[2048]{0:T(1024)S(1)} %dynamic-update-slice, s32[2048]{0:T(1024)S(1)} %dynamic-update-slice.1), channel_id=1, replica_groups=mesh['pair'=32,'lam'=8] {'pair'}, use_global_device_ids=true, to_apply=%add | all-reduce | flops 4096 | bytes 32768
  290.0 310.6 %while.22 = (s32[]{:T(128)}, f32[2,40,20480]{2,1,0:T(8,128)}, s32[8]{0:T(128)S(1)}, bf16[2,2048,40]{1,2,0:T(8,128)(2,1)}, s32[2048]{0:T(1024)}, /*index=5*/bf16[...) while((s32[]{:T(128)}, f32[2,40,20480]{2,1,0:T(8,128)}, ...), condition=%wide.region_4.5_spmd.clone, body=%wide.region_3.4_spmd.clone.sunk | while | flops 853292032 | bytes 59753956 | solution.py:82
  303.7 14.8 %reshape.110 = bf16[256,20480,1]{1,0,2:T(8,128)(2,1)} reshape(bf16[256,16,1280]{2,1,0:T(8,128)(2,1)} %multiply_convert_fusion.2) | data formatting | bytes 20971520 | tf_op jit(solution)/shard_map/while/body/eval_jaxpr/convert_element_type | solution.py:71
  318.4 8.8 %convolution_add_fusion.5 = f32[2,40,20480]{2,1,0:T(8,128)} fusion(bf16[256,20480,1]{1,0,2:T(8,128)(2,1)} %reshape.110, f32[2,40,20480]{2,1,0:T(8,128)} %get-tuple-element.331, pred[]{:T(512)S(6)} %compare.3, bf16[2,2048,40]{1,2,0:T(8,128)(2,1)} %get-tuple-element.344, s32[]{:T(128)S(6)} %select_n.68), kind=kOutput, calls=%fused_computation.10.clone.1 | convolution fusion | flops 842137600 | bytes 23633924 | tf_op jit(solution)/shard_map/while/body/eval_jaxpr/qrb,rk->qbk/dot_general | solution.py:77
  334.2 6.7 %multiply_convert_fusion.2 = bf16[256,16,1280]{2,1,0:T(8,128)(2,1)} fusion(f32[256,1280]{1,0:T(8,128)} %select_convert_fusion.4, f32[256,16]{1,0:T(8,128)S(1)} %select_convert_fusion.5), kind=kLoop, calls=%fused_computation.11.clone.1 | loop fusion | flops 10485760 | bytes 11812864 | tf_op jit(solution)/shard_map/while/body/eval_jaxpr/convert_element_type | solution.py:71
  340.9 14.8 %reshape.110 = bf16[256,20480,1]{1,0,2:T(8,128)(2,1)} reshape(bf16[256,16,1280]{2,1,0:T(8,128)(2,1)} %multiply_convert_fusion.2) | data formatting | bytes 20971520 | tf_op jit(solution)/shard_map/while/body/eval_jaxpr/convert_element_type | solution.py:71
  355.7 10.6 %convolution_add_fusion.5 = f32[2,40,20480]{2,1,0:T(8,128)} fusion(bf16[256,20480,1]{1,0,2:T(8,128)(2,1)} %reshape.110, f32[2,40,20480]{2,1,0:T(8,128)} %get-tuple-element.331, pred[]{:T(512)S(6)} %compare.3, bf16[2,2048,40]{1,2,0:T(8,128)(2,1)} %get-tuple-element.344, s32[]{:T(128)S(6)} %select_n.68), kind=kOutput, calls=%fused_computation.10.clone.1 | convolution fusion | flops 842137600 | bytes 23633924 | tf_op jit(solution)/shard_map/while/body/eval_jaxpr/qrb,rk->qbk/dot_general | solution.py:77
  380.0 14.8 %reshape.110 = bf16[256,20480,1]{1,0,2:T(8,128)(2,1)} reshape(bf16[256,16,1280]{2,1,0:T(8,128)(2,1)} %multiply_convert_fusion.2) | data formatting | bytes 20971520 | tf_op jit(solution)/shard_map/while/body/eval_jaxpr/convert_element_type | solution.py:71
  394.7 10.6 %convolution_add_fusion.5 = f32[2,40,20480]{2,1,0:T(8,128)} fusion(bf16[256,20480,1]{1,0,2:T(8,128)(2,1)} %reshape.110, f32[2,40,20480]{2,1,0:T(8,128)} %get-tuple-element.331, pred[]{:T(512)S(6)} %compare.3, bf16[2,2048,40]{1,2,0:T(8,128)(2,1)} %get-tuple-element.344, s32[]{:T(128)S(6)} %select_n.68), kind=kOutput, calls=%fused_computation.10.clone.1 | convolution fusion | flops 842137600 | bytes 23633924 | tf_op jit(solution)/shard_map/while/body/eval_jaxpr/qrb,rk->qbk/dot_general | solution.py:77
  412.3 6.7 %multiply_convert_fusion.2 = bf16[256,16,1280]{2,1,0:T(8,128)(2,1)} fusion(f32[256,1280]{1,0:T(8,128)} %select_convert_fusion.4, f32[256,16]{1,0:T(8,128)S(1)} %select_convert_fusion.5), kind=kLoop, calls=%fused_computation.11.clone.1 | loop fusion | flops 10485760 | bytes 11812864 | tf_op jit(solution)/shard_map/while/body/eval_jaxpr/convert_element_type | solution.py:71
  419.0 14.8 %reshape.110 = bf16[256,20480,1]{1,0,2:T(8,128)(2,1)} reshape(bf16[256,16,1280]{2,1,0:T(8,128)(2,1)} %multiply_convert_fusion.2) | data formatting | bytes 20971520 | tf_op jit(solution)/shard_map/while/body/eval_jaxpr/convert_element_type | solution.py:71
  433.8 10.6 %convolution_add_fusion.5 = f32[2,40,20480]{2,1,0:T(8,128)} fusion(bf16[256,20480,1]{1,0,2:T(8,128)(2,1)} %reshape.110, f32[2,40,20480]{2,1,0:T(8,128)} %get-tuple-element.331, pred[]{:T(512)S(6)} %compare.3, bf16[2,2048,40]{1,2,0:T(8,128)(2,1)} %get-tuple-element.344, s32[]{:T(128)S(6)} %select_n.68), kind=kOutput, calls=%fused_computation.10.clone.1 | convolution fusion | flops 842137600 | bytes 23633924 | tf_op jit(solution)/shard_map/while/body/eval_jaxpr/qrb,rk->qbk/dot_general | solution.py:77
  458.1 14.8 %reshape.110 = bf16[256,20480,1]{1,0,2:T(8,128)(2,1)} reshape(bf16[256,16,1280]{2,1,0:T(8,128)(2,1)} %multiply_convert_fusion.2) | data formatting | bytes 20971520 | tf_op jit(solution)/shard_map/while/body/eval_jaxpr/convert_element_type | solution.py:71
  472.8 10.6 %convolution_add_fusion.5 = f32[2,40,20480]{2,1,0:T(8,128)} fusion(bf16[256,20480,1]{1,0,2:T(8,128)(2,1)} %reshape.110, f32[2,40,20480]{2,1,0:T(8,128)} %get-tuple-element.331, pred[]{:T(512)S(6)} %compare.3, bf16[2,2048,40]{1,2,0:T(8,128)(2,1)} %get-tuple-element.344, s32[]{:T(128)S(6)} %select_n.68), kind=kOutput, calls=%fused_computation.10.clone.1 | convolution fusion | flops 842137600 | bytes 23633924 | tf_op jit(solution)/shard_map/while/body/eval_jaxpr/qrb,rk->qbk/dot_general | solution.py:77
  490.4 6.7 %multiply_convert_fusion.2 = bf16[256,16,1280]{2,1,0:T(8,128)(2,1)} fusion(f32[256,1280]{1,0:T(8,128)} %select_convert_fusion.4, f32[256,16]{1,0:T(8,128)S(1)} %select_convert_fusion.5), kind=kLoop, calls=%fused_computation.11.clone.1 | loop fusion | flops 10485760 | bytes 11812864 | tf_op jit(solution)/shard_map/while/body/eval_jaxpr/convert_element_type | solution.py:71
  497.1 14.8 %reshape.110 = bf16[256,20480,1]{1,0,2:T(8,128)(2,1)} reshape(bf16[256,16,1280]{2,1,0:T(8,128)(2,1)} %multiply_convert_fusion.2) | data formatting | bytes 20971520 | tf_op jit(solution)/shard_map/while/body/eval_jaxpr/convert_element_type | solution.py:71
  511.9 10.6 %convolution_add_fusion.5 = f32[2,40,20480]{2,1,0:T(8,128)} fusion(bf16[256,20480,1]{1,0,2:T(8,128)(2,1)} %reshape.110, f32[2,40,20480]{2,1,0:T(8,128)} %get-tuple-element.331, pred[]{:T(512)S(6)} %compare.3, bf16[2,2048,40]{1,2,0:T(8,128)(2,1)} %get-tuple-element.344, s32[]{:T(128)S(6)} %select_n.68), kind=kOutput, calls=%fused_computation.10.clone.1 | convolution fusion | flops 842137600 | bytes 23633924 | tf_op jit(solution)/shard_map/while/body/eval_jaxpr/qrb,rk->qbk/dot_general | solution.py:77
  536.1 14.8 %reshape.110 = bf16[256,20480,1]{1,0,2:T(8,128)(2,1)} reshape(bf16[256,16,1280]{2,1,0:T(8,128)(2,1)} %multiply_convert_fusion.2) | data formatting | bytes 20971520 | tf_op jit(solution)/shard_map/while/body/eval_jaxpr/convert_element_type | solution.py:71
  550.9 10.6 %convolution_add_fusion.5 = f32[2,40,20480]{2,1,0:T(8,128)} fusion(bf16[256,20480,1]{1,0,2:T(8,128)(2,1)} %reshape.110, f32[2,40,20480]{2,1,0:T(8,128)} %get-tuple-element.331, pred[]{:T(512)S(6)} %compare.3, bf16[2,2048,40]{1,2,0:T(8,128)(2,1)} %get-tuple-element.344, s32[]{:T(128)S(6)} %select_n.68), kind=kOutput, calls=%fused_computation.10.clone.1 | convolution fusion | flops 842137600 | bytes 23633924 | tf_op jit(solution)/shard_map/while/body/eval_jaxpr/qrb,rk->qbk/dot_general | solution.py:77
  575.2 14.8 %reshape.110 = bf16[256,20480,1]{1,0,2:T(8,128)(2,1)} reshape(bf16[256,16,1280]{2,1,0:T(8,128)(2,1)} %multiply_convert_fusion.2) | data formatting | bytes 20971520 | tf_op jit(solution)/shard_map/while/body/eval_jaxpr/convert_element_type | solution.py:71
  589.9 10.6 %convolution_add_fusion.5 = f32[2,40,20480]{2,1,0:T(8,128)} fusion(bf16[256,20480,1]{1,0,2:T(8,128)(2,1)} %reshape.110, f32[2,40,20480]{2,1,0:T(8,128)} %get-tuple-element.331, pred[]{:T(512)S(6)} %compare.3, bf16[2,2048,40]{1,2,0:T(8,128)(2,1)} %get-tuple-element.344, s32[]{:T(128)S(6)} %select_n.68), kind=kOutput, calls=%fused_computation.10.clone.1 | convolution fusion | flops 842137600 | bytes 23633924 | tf_op jit(solution)/shard_map/while/body/eval_jaxpr/qrb,rk->qbk/dot_general | solution.py:77
  (142 shorter events, 94.6 us)
Async XLA Ops:
  0.0 2.5 copy-start.1
  0.0 2.5 copy-start.2
  16.7 118.0 %copy-start = (bf16[1024,1280]{1,0:T(8,128)(2,1)S(1)}, bf16[1024,1280]{1,0:T(8,128)(2,1)}, u32[]{:S(2)}) copy-start(bf16[1024,1280]{1,0:T(8,128)(2,1)} %param.19) | copy-start | bytes 7864324
  133.6 28.2 %copy-start.5 = (u32[256]{0:T(256)S(1)}, u32[256]{0:T(256)}, u32[]{:S(2)}) copy-start(u32[256]{0:T(256)} %constant.71) | copy-start | bytes 3076
  133.6 29.3 %copy-start.3 = (s32[64]{0:T(128)S(1)}, s32[64]{0:T(128)}, u32[]{:S(2)}) copy-start(s32[64]{0:T(128)} %param.16) | copy-start | bytes 772
  133.6 29.6 %copy-start.4 = (s32[64]{0:T(128)S(1)}, s32[64]{0:T(128)}, u32[]{:S(2)}) copy-start(s32[64]{0:T(128)} %param.17) | copy-start | bytes 772
  138.5 148.2 %all-to-all-start = ((bf16[32,2,2560]{2,1,0:T(2,128)(2,1)}), bf16[32,2,2560]{2,1,0:T(2,128)(2,1)}, u32[]{:S(2)}, u32[]{:S(2)}) async-start(bf16[32,2,2560]{2,1,0:T(2,128)(2,1)} %reshape.99), calls=%async_computation | async-start | bytes 655360 | tf_op jit(solution)/shard_map/all_to_all | solution.py:55
  290.0 3.5 copy-start.6
  318.4 8.8 %copy-start.7 = (s32[8]{0:T(128)S(1)}, s32[8]{0:T(128)}, u32[]{:S(2)}) copy-start(s32[8]{0:T(128)} %copy-done.6) | copy-start | bytes 100 | tf_op jit(solution)/shard_map/while
  327.2 3.5 copy-start.6
  355.7 10.6 %copy-start.7 = (s32[8]{0:T(128)S(1)}, s32[8]{0:T(128)}, u32[]{:S(2)}) copy-start(s32[8]{0:T(128)} %copy-done.6) | copy-start | bytes 100 | tf_op jit(solution)/shard_map/while
  366.3 3.5 copy-start.6
  394.7 10.6 %copy-start.7 = (s32[8]{0:T(128)S(1)}, s32[8]{0:T(128)}, u32[]{:S(2)}) copy-start(s32[8]{0:T(128)} %copy-done.6) | copy-start | bytes 100 | tf_op jit(solution)/shard_map/while
  405.4 3.5 copy-start.6
  433.8 10.6 %copy-start.7 = (s32[8]{0:T(128)S(1)}, s32[8]{0:T(128)}, u32[]{:S(2)}) copy-start(s32[8]{0:T(128)} %copy-done.6) | copy-start | bytes 100 | tf_op jit(solution)/shard_map/while
  444.4 3.5 copy-start.6
  472.8 10.6 %copy-start.7 = (s32[8]{0:T(128)S(1)}, s32[8]{0:T(128)}, u32[]{:S(2)}) copy-start(s32[8]{0:T(128)} %copy-done.6) | copy-start | bytes 100 | tf_op jit(solution)/shard_map/while
  483.5 3.5 copy-start.6
  511.9 10.6 %copy-start.7 = (s32[8]{0:T(128)S(1)}, s32[8]{0:T(128)}, u32[]{:S(2)}) copy-start(s32[8]{0:T(128)} %copy-done.6) | copy-start | bytes 100 | tf_op jit(solution)/shard_map/while
  522.5 3.5 copy-start.6
  550.9 10.6 %copy-start.7 = (s32[8]{0:T(128)S(1)}, s32[8]{0:T(128)}, u32[]{:S(2)}) copy-start(s32[8]{0:T(128)} %copy-done.6) | copy-start | bytes 100 | tf_op jit(solution)/shard_map/while
  561.5 3.5 copy-start.6
  589.9 10.6 %copy-start.7 = (s32[8]{0:T(128)S(1)}, s32[8]{0:T(128)}, u32[]{:S(2)}) copy-start(s32[8]{0:T(128)} %copy-done.6) | copy-start | bytes 100 | tf_op jit(solution)/shard_map/while
where the time goes:
time: 609 us; the launch traced here: 601 us
  blocking collectives  240 us (39%)
  local copies, waits for them, and re-layouts  159 us (26%)
  matrix products  86.4 us (14%)
  other arithmetic  70.6 us (12%)
  starting transfers between devices  22.3 us (4%)
  loops' own time  21.4 us (4%)
    unnamed x1, blocking collectives  123 us
    convert_element_type x8, local copies, waits for them, and re-layouts, add_rows(): weights = (occ_rows[:, :, None] * vir_rows[:, None, :]).astype(jnp.bfloat...  118 us
    psum x1, blocking collectives, on_device(): summed = lax.psum(partial_value, 'lam')  117 us
    dot_general x8, matrix products, add_rows(): jnp.einsum('qrb,rk->qbk', mixed_piece, weights, preferred_element_type=jn...  83.1 us
    convert_element_type x8, other arithmetic, add_rows(): weights = (occ_rows[:, :, None] * vir_rows[:, None, :]).astype(jnp.bfloat...  53.6 us
    all_to_all x1, starting transfers between devices, on_device(): lax.all_to_all(mixed, 'pair', split_axis=2, concat_axis=1, tiled=True)  22.3 us
    another operation x1, loops' own time, on_device(): lax.scan(add_rows, start_total, jnp.arange(0, total_rows, row_block, dtyp...  16.6 us
  transfers between devices with their start and end apart: 1, of which 0 were waited for; matrix products, arithmetic and copies ran while one was open for 0% of the time, Pallas kernels for 0%

commit v1 on v0

v1 whole, which is shorter than its diff:
```python
import jax
import jax.numpy as jnp
from jax import lax
from jax.sharding import PartitionSpec as P


def on_device(
    integrals, tile_pair, tile_lam, tile_count, mu_index, nu_index, occupied_coef, virtual_coef
):
    lam_count = lax.axis_size("lam")
    pair_count = lax.axis_size("pair")
    basis_count, occ_total = occupied_coef.shape
    vir_total = virtual_coef.shape[1]
    rows_here = mu_index.shape[0]

    both_index = lax.all_gather(
        jnp.stack([mu_index, nu_index]), "pair", axis=1, tiled=True
    )

    tile_data = integrals[0]
    slot_count, tile_rows, tile_depth, _ = tile_data.shape
    block_count = rows_here // tile_rows
    pair_list = tile_pair[0]
    lam_list = tile_lam[0]
    live = jnp.arange(slot_count) < tile_count[0, 0]
    occ_blocks = occupied_coef.reshape(basis_count // tile_depth, tile_depth, occ_total)
    occ_slot = jnp.take(occ_blocks, lam_list, axis=0)
    hit = (pair_list[:, None] == jnp.arange(block_count)[None, :]) & live[:, None]
    mask = jnp.where(hit[:, :, None, None], occ_slot[:, None, :, :], jnp.zeros((), occ_slot.dtype))
    partial_value = jnp.einsum(
        "tgmj,tkms->jgks", mask, tile_data, preferred_element_type=jnp.float32
    ).reshape(occ_total, rows_here, basis_count)

    own_half = lax.psum_scatter(partial_value, "lam", scatter_dimension=0, tiled=True)
    occ_share = own_half.shape[0]
    vir_share = vir_total // pair_count
    half_low = own_half.astype(jnp.bfloat16).reshape(occ_share * rows_here, basis_count)
    mixed = jnp.dot(half_low, virtual_coef, preferred_element_type=jnp.float32)
    mixed = mixed.astype(jnp.bfloat16).reshape(occ_share, rows_here, pair_count, vir_share)
    received = lax.all_to_all(mixed, "pair", split_axis=2, concat_axis=1, tiled=True)
    total_rows = received.shape[1]
    mixed_rows = received.reshape(occ_share, total_rows, vir_share)

    occ_rows = jnp.take(occupied_coef, both_index[0], axis=0)
    vir_rows = jnp.take(virtual_coef, both_index[1], axis=0)
    scaled = (
        mixed_rows.astype(jnp.float32)[:, :, :, None]
        * occ_rows.astype(jnp.float32)[None, :, None, :]
    ).astype(jnp.bfloat16)
    result = jnp.einsum("qrbi,ra->qbia", scaled, vir_rows, preferred_element_type=jnp.float32)
    return result.reshape(occ_share, vir_share, occ_total * vir_total)


def solution(mesh):
    placed = (
        P("pair", "lam", None, None, None),
        P("pair", "lam"),
        P("pair", "lam"),
        P("pair", "lam"),
        P("pair"),
        P("pair"),
        P(),
        P(),
    )
    return jax.shard_map(
        on_device, mesh=mesh, in_specs=placed, out_specs=P("lam", "pair", None), check_vma=False
    )
```

time: 609 us -> 133 us (0.22); the launches traced: 601 us -> 132 us
  blocking collectives: 240 us -> 25.8 us
  local copies, waits for them, and re-layouts: 159 us -> 38.8 us
  matrix products: 86.4 us -> 15.7 us
  other arithmetic: 70.6 us -> 3.82 us
  waiting for transfers between devices: 0.01 us -> 26 us
  loops' own time: 21.4 us -> 0 us
  starting transfers between devices: 22.3 us -> 7.56 us
  between operations: 0.69 us -> 14.2 us
    unnamed x1 -> x0, blocking collectives: 123 us -> none
    psum x1 -> x0, blocking collectives: 117 us -> none  [on_device(): summed = lax.psum(partial_value, 'lam')]
    convert_element_type x9 -> x2, local copies, waits for them, and re-layouts: 119 us -> 3.21 us  [on_device(): mixed_rows.astype(jnp.float32)[:, :, :, None]]
    dot_general x10 -> x2, matrix products: 85.9 us -> 15.2 us  [the longest x1 11.6 us: on_device(): jnp.einsum('qrbi,ra->qbia', scaled, vir_rows, preferred_element_type=jnp....]
    convert_element_type x24 -> x3, other arithmetic: 64.2 us -> 1.54 us  [the longest x1 1.07 us: on_device(): own_half.astype(jnp.bfloat16).reshape(occ_share * rows_here, basis_count)]
    reduce_scatter x0 -> x1, waiting for transfers between devices: none -> 26 us  [on_device(): lax.psum_scatter(partial_value, 'lam', scatter_dimension=0, tiled=True)]
    all_gather x0 -> x1, blocking collectives: none -> 25.8 us  [on_device(): lax.all_gather(jnp.stack([mu_index, nu_index]), 'pair', axis=1, tiled=True)]
    another operation x2 -> x0, loops' own time: 21.4 us -> none  [the longest x1 16.6 us: on_device(): lax.scan(add_rows, start_total, jnp.arange(0, total_rows, row_block, dtyp...]
  transfers between devices with their start and end apart: 1 -> 2, of which waited for: 0 -> 1; matrix products, arithmetic and copies ran while one was open for 0% -> 13% of each run, Pallas kernels for 0% -> 0%
where the time goes in v1:
time: 133 us; the launch traced here: 132 us
  local copies, waits for them, and re-layouts  38.8 us (29%)
  waiting for transfers between devices  26 us (20%)
  blocking collectives  25.8 us (19%)
  matrix products  15.7 us (12%)
  between operations  14.2 us (11%)
  starting transfers between devices  7.56 us (6%)
  other arithmetic  3.82 us (3%)
    reduce_scatter x1, waiting for transfers between devices, on_device(): lax.psum_scatter(partial_value, 'lam', scatter_dimension=0, tiled=True)  26 us
    all_gather x1, blocking collectives, on_device(): lax.all_gather(jnp.stack([mu_index, nu_index]), 'pair', axis=1, tiled=True)  25.8 us
    dot_general x1, matrix products, on_device(): jnp.einsum('qrbi,ra->qbia', scaled, vir_rows, preferred_element_type=jnp....  11.6 us
    gather x1, local copies, waits for them, and re-layouts, on_device(): vir_rows = jnp.take(virtual_coef, both_index[1], axis=0)  9.85 us
    reshape x1, local copies, waits for them, and re-layouts, on_device(): return result.reshape(occ_share, vir_share, occ_total * vir_total)  7.69 us
    all_to_all x1, starting transfers between devices, on_device(): lax.all_to_all(mixed, 'pair', split_axis=2, concat_axis=1, tiled=True)  7.55 us
    gather x2, local copies, waits for them, and re-layouts, on_device(): occ_rows = jnp.take(occupied_coef, both_index[0], axis=0)  6.36 us
    reshape x1, local copies, waits for them, and re-layouts, on_device(): partial_value = jnp.einsum('tgmj,tkms->jgks', mask, tile_data, preferred_...  4.44 us
  transfers between devices with their start and end apart: 2, of which 1 were waited for; matrix products, arithmetic and copies ran while one was open for 13% of the time, Pallas kernels for 0%

profile of v1, /device:TPU:1, one launch (start us, length us, event | category | flops | bytes accessed | tf_op | source)
XLA Modules:
  0.0 131.9 jit_solution(3602176303495265358)
XLA Ops:
  6.5 0.8 fusion.16
  7.3 0.7 compare_and_fusion.2
  8.7 0.9 reshape.187
  9.6 0.7 fusion.15
  10.3 0.6 gather_fusion
  10.9 3.6 %fusion.6 = f32[16,16,4,1024,1]{3,1,4,2,0:T(8,128)S(1)} fusion(pred[8,16]{0,1:T(8,128)(4,1)S(1)} %fusion.15, bf16[8,64,16]{1,2,0:T(8,128)(2,1)S(1)} %broadcast_select_fusion, bf16[1,8,4,64,1024]{4,3,2,1,0:T(8,128)(2,1)} %param.8), kind=kOutput, calls=%fused_computation.10 | convolution fusion | flops 1073872896 | bytes 8405120 | tf_op jit(solution)/shard_map/tgmj,tkms->jgks/dot_general | solution.py:30
  14.5 4.4 %copy.38 = f32[16,64,1024]{2,1,0:T(8,128)} copy(f32[16,64,1024]{2,0,1:T(8,128)S(1)} %bitcast.70) | data formatting | bytes 8388608 | tf_op jit(solution)/shard_map/reshape | solution.py:32
  19.0 0.7 copy-done.1
  20.0 25.8 %all-gather = s32[32,64,2]{1,2,0:T(2,128)S(1)} all-gather(s32[1,64,2]{1,2,0:T(2,128)S(1)} %add_bitcast_fusion), channel_id=1, replica_groups=mesh['pair'=32,'lam'=8] {'pair'}, dimensions={0}, use_global_device_ids=true | all-gather | bytes 16896 | tf_op jit(solution)/shard_map/all_gather | solution.py:16
  45.9 6.2 %gather_fusion.1 = bf16[2048,16]{1,0:T(8,128)(2,1)S(1)} fusion(bf16[1024,16]{1,0:T(8,128)(2,1)S(1)} %copy.42, s32[2048]{0:T(1024)S(1)} %broadcast_clamp_fusion.1), kind=kCustom, calls=%fused_computation.1 | custom fusion | bytes 139264 | tf_op jit(solution)/shard_map/jit(_take)/gather | solution.py:44
  52.3 26.0 %reduce-scatter.2.cloned.1.call-done = f32[2,64,1024]{2,1,0:T(8,128)} async-done(((f32[16,64,1024]{2,1,0:T(8,128)}), f32[2,64,1024]{2,1,0:T(8,128)}) %reduce-scatter.2.cloned.1.call-update) | async-done | bytes 524304 | tf_op jit(solution)/shard_map/reduce_scatter | solution.py:34
  78.3 1.1 convert_element_type.32
  79.4 0.5 convolution_convert_fusion
  79.9 0.9 copy.39
  80.8 1.3 reshape.190
  82.1 1.1 reshape.224
  83.2 7.6 %all-to-all-start = ((bf16[32,2,2560]{2,1,0:T(2,128)(2,1)}), bf16[32,2,2560]{2,1,0:T(2,128)(2,1)}, u32[]{:S(2)}, u32[]{:S(2)}) async-start(bf16[32,2,2560]{2,1,0:T(2,128)(2,1)} %reshape.224), calls=%async_computation.1 | async-start | bytes 655360 | tf_op jit(solution)/shard_map/all_to_all | solution.py:40
  90.8 9.9 %gather_fusion.2 = bf16[2048,1280]{1,0:T(8,128)(2,1)} fusion(bf16[1024,1280]{1,0:T(8,128)(2,1)S(1)} %copy-done, s32[2048]{0:T(1024)S(1)} %broadcast_clamp_fusion), kind=kCustom, calls=%fused_computation.2 | custom fusion | bytes 10493952 | tf_op jit(solution)/shard_map/jit(_take)/gather | solution.py:45
  100.7 1.4 %reshape.225 = bf16[32,40,2,64]{3,2,1,0:T(2,128)(2,1)S(1)} reshape(bf16[32,2,2560]{2,1,0:T(2,128)(2,1)} %all-to-all-done) | data formatting | bytes 655360
  102.1 0.5 convert_bitcast_fusion
  102.6 1.5 %copy.40 = f32[2,32,64,1,40]{2,1,4,0,3:T(8,128)} copy(f32[2,32,64,1,40]{2,0,4,1,3:T(2,128)S(1)} %convert_bitcast_fusion) | data formatting | bytes 1310720 | tf_op jit(solution)/shard_map/convert_element_type | solution.py:47
  104.0 1.7 %reshape.192 = f32[2,2048,40]{1,2,0:T(8,128)S(1)} reshape(f32[2,32,64,1,40]{2,1,4,0,3:T(8,128)} %copy.40) | data formatting | bytes 1310720 | tf_op jit(solution)/shard_map/convert_element_type | solution.py:47
  105.8 11.6 %fusion = f32[2,40,16,1280]{3,2,1,0:T(8,128)} fusion(bf16[2048,1280]{1,0:T(8,128)(2,1)} %gather_fusion.2, f32[2048,16]{0,1:T(8,128)S(1)} %select_convert_fusion, f32[2,2048,40]{1,2,0:T(8,128)S(1)} %reshape.192, pred[2048]{0:T(1024)(128)(4,1)S(1)} %compare_and_fusion), kind=kOutput, calls=%fused_computation.4 | convolution fusion | flops 6718750720 | bytes 12584960 | tf_op jit(solution)/shard_map/qrbi,ra->qbia/dot_general | solution.py:50
  117.4 7.7 %reshape.191 = f32[2,40,20480]{2,1,0:T(8,128)} reshape(f32[2,40,16,1280]{3,2,1,0:T(8,128)} %fusion) | data formatting | bytes 13107200 | tf_op jit(solution)/shard_map/reshape | solution.py:51
  (26 shorter events, 0.7 us)
Async XLA Ops:
  6.5 72.9 %copy-start = (bf16[1024,1280]{1,0:T(8,128)(2,1)S(1)}, bf16[1024,1280]{1,0:T(8,128)(2,1)}, u32[]{:S(2)}) copy-start(bf16[1024,1280]{1,0:T(8,128)(2,1)} %param.15) | copy-start | bytes 7864324
  6.5 71.8 %reduce-scatter.2.cloned.1.call-start = ((), (), s32[]{:S(2)}) async-start(), calls=%async_computation.2 | async-start | bytes 4718592 | tf_op jit(solution)/shard_map/reduce_scatter | solution.py:34
  19.0 0.8 copy-start.1
  19.0 0.9 copy-start.2
  19.0 0.9 copy-start.3
  83.2 17.4 %all-to-all-start = ((bf16[32,2,2560]{2,1,0:T(2,128)(2,1)}), bf16[32,2,2560]{2,1,0:T(2,128)(2,1)}, u32[]{:S(2)}, u32[]{:S(2)}) async-start(bf16[32,2,2560]{2,1,0:T(2,128)(2,1)} %reshape.224), calls=%async_computation.1 | async-start | bytes 655360 | tf_op jit(solution)/shard_map/all_to_all | solution.py:40
Sparse Core Ops, SparseCore 0:
  19.1 59.1 reduce-scatter.1

commit v2 on v1

--- a/solution.py
+++ b/solution.py
@@ -13,9 +13,11 @@
     vir_total = virtual_coef.shape[1]
     rows_here = mu_index.shape[0]
 
-    both_index = lax.all_gather(
-        jnp.stack([mu_index, nu_index]), "pair", axis=1, tiled=True
+    index_copies = jnp.broadcast_to(
+        jnp.stack([mu_index, nu_index])[None], (pair_count, 2, rows_here)
     )
+    both_index = lax.all_to_all(index_copies, "pair", split_axis=0, concat_axis=0, tiled=True)
+    both_index = jnp.transpose(both_index, (1, 0, 2)).reshape(2, pair_count * rows_here)
 
     tile_data = integrals[0]
     slot_count, tile_rows, tile_depth, _ = tile_data.shape
@@ -31,7 +33,9 @@
         "tgmj,tkms->jgks", mask, tile_data, preferred_element_type=jnp.float32
     ).reshape(occ_total, rows_here, basis_count)
 
-    own_half = lax.psum_scatter(partial_value, "lam", scatter_dimension=0, tiled=True)
+    own_half = lax.psum_scatter(
+        partial_value.astype(jnp.bfloat16), "lam", scatter_dimension=0, tiled=True
+    )
     occ_share = own_half.shape[0]
     vir_share = vir_total // pair_count
     half_low = own_half.astype(jnp.bfloat16).reshape(occ_share * rows_here, basis_count)

time: 133 us -> 118 us (0.89)
  blocking collectives: 25.8 us -> 0 us
  starting transfers between devices: 7.56 us -> 20.4 us
  waiting for transfers between devices: 26 us -> 24.4 us
    all_gather x1 -> x0, blocking collectives: 25.8 us -> none  [on_device(): lax.all_gather(jnp.stack([mu_index, nu_index]), 'pair', axis=1, tiled=True)]
    all_to_all x0 -> x1, starting transfers between devices: none -> 8.59 us  [on_device(): lax.all_to_all(index_copies, 'pair', split_axis=0, concat_axis=0, tiled=T...]
    reduce_scatter x1, waiting for transfers between devices: 26 us -> 17.6 us  [on_device(): lax.psum_scatter(partial_value.astype(jnp.bfloat16), 'lam', scatter_dimen...]
    all_to_all x0 -> x1, waiting for transfers between devices: none -> 6.75 us  [on_device(): lax.all_to_all(index_copies, 'pair', split_axis=0, concat_axis=0, tiled=T...]
    reshape x1 -> x0, local copies, waits for them, and re-layouts: 4.44 us -> none  [on_device(): partial_value = jnp.einsum('tgmj,tkms->jgks', mask, tile_data, preferred_...]
    all_to_all x1, starting transfers between devices: 7.55 us -> 11.8 us  [on_device(): lax.all_to_all(mixed, 'pair', split_axis=2, concat_axis=1, tiled=True)]
    convert_element_type x0 -> x1, local copies, waits for them, and re-layouts: none -> 2.47 us  [on_device(): partial_value.astype(jnp.bfloat16)]
    unnamed x12 -> x13, local copies, waits for them, and re-layouts: 3.56 us -> 3.54 us
  transfers between devices with their start and end apart: 2 -> 3, of which waited for: 1 -> 2; matrix products, arithmetic and copies ran while one was open for 13% -> 16% of each run, Pallas kernels for 0% -> 0%
where the time goes in v2:
time: 118 us; the launch traced here: 117 us
  local copies, waits for them, and re-layouts  37.7 us (32%)
  waiting for transfers between devices  24.4 us (21%)
  starting transfers between devices  20.4 us (17%)
  matrix products  16.7 us (14%)
  between operations  14.3 us (12%)
  other arithmetic  3.42 us (3%)
    reduce_scatter x1, waiting for transfers between devices, on_device(): lax.psum_scatter(partial_value.astype(jnp.bfloat16), 'lam', scatter_dimen...  17.6 us
    all_to_all x1, starting transfers between devices, on_device(): lax.all_to_all(mixed, 'pair', split_axis=2, concat_axis=1, tiled=True)  11.8 us
    dot_general x1, matrix products, on_device(): jnp.einsum('qrbi,ra->qbia', scaled, vir_rows, preferred_element_type=jnp....  11.6 us
    gather x1, local copies, waits for them, and re-layouts, on_device(): vir_rows = jnp.take(virtual_coef, both_index[1], axis=0)  9.85 us
    all_to_all x1, starting transfers between devices, on_device(): lax.all_to_all(index_copies, 'pair', split_axis=0, concat_axis=0, tiled=T...  8.59 us
    reshape x1, local copies, waits for them, and re-layouts, on_device(): return result.reshape(occ_share, vir_share, occ_total * vir_total)  7.69 us
    all_to_all x1, waiting for transfers between devices, on_device(): lax.all_to_all(index_copies, 'pair', split_axis=0, concat_axis=0, tiled=T...  6.75 us
    gather x2, local copies, waits for them, and re-layouts, on_device(): occ_rows = jnp.take(occupied_coef, both_index[0], axis=0)  6.36 us
  transfers between devices with their start and end apart: 3, of which 2 were waited for; matrix products, arithmetic and copies ran while one was open for 16% of the time, Pallas kernels for 0%

profile of v2, /device:TPU:1, one launch (start us, length us, event | category | flops | bytes accessed | tf_op | source)
XLA Modules:
  0.0 116.9 jit_solution(2812479855992214328)
XLA Ops:
  6.5 0.8 fusion.18
  7.3 0.7 compare_and_fusion.2
  8.7 0.9 reshape.192
  9.6 0.7 fusion.17
  10.3 0.6 gather_fusion
  10.9 3.6 %bitcast_convert_fusion = bf16[16,16,4,1024]{3,1,2,0:T(8,128)(2,1)S(1)} fusion(pred[8,16]{0,1:T(8,128)(4,1)S(1)} %fusion.17, bf16[8,64,16]{1,2,0:T(8,128)(2,1)S(1)} %broadcast_select_fusion, bf16[1,8,4,64,1024]{4,3,2,1,0:T(8,128)(2,1)} %param.8), kind=kOutput, calls=%fused_computation.10 | convolution fusion | flops 1074921472 | bytes 6307968 | tf_op jit(solution)/shard_map/tgmj,tkms->jgks/dot_general | solution.py:32
  14.6 2.5 %copy.28 = bf16[16,64,1024]{2,1,0:T(8,128)(2,1)} copy(bf16[16,64,1024]{2,0,1:T(8,128)(2,1)S(1)} %bitcast.63) | data formatting | bytes 4194304 | tf_op jit(solution)/shard_map/convert_element_type | solution.py:37
  17.1 0.7 reshape.244
  17.8 8.6 %all-to-all-start.1 = ((s32[32,1,128]{2,1,0:T(1,128)}), s32[32,1,128]{2,1,0:T(1,128)S(1)}, u32[]{:S(2)}, u32[]{:S(2)}) async-start(s32[32,1,128]{2,1,0:T(1,128)} %reshape.244), calls=%async_computation.2 | async-start | bytes 32768 | tf_op jit(solution)/shard_map/all_to_all | solution.py:19
  26.6 6.8 %all-to-all-done.1 = s32[32,1,128]{2,1,0:T(1,128)S(1)} async-done(((s32[32,1,128]{2,1,0:T(1,128)}), s32[32,1,128]{2,1,0:T(1,128)S(1)}, u32[]{:S(2)}, u32[]{:S(2)}) %all-to-all-start.1) | async-done | bytes 16416 | tf_op jit(solution)/shard_map/all_to_all | solution.py:19
  33.9 0.7 reduce.12
  35.0 6.2 %gather_fusion.1 = bf16[2048,16]{1,0:T(8,128)(2,1)S(1)} fusion(bf16[1024,16]{1,0:T(8,128)(2,1)S(1)} %copy.31, s32[2048]{0:T(1024)S(1)} %broadcast_clamp_fusion.1), kind=kCustom, calls=%fused_computation.1 | custom fusion | bytes 139264 | tf_op jit(solution)/shard_map/jit(_take)/gather | solution.py:48
  41.5 17.6 %reduce-scatter.2.cloned.1.call-done = bf16[2,64,1024]{2,1,0:T(8,128)(2,1)} async-done(((bf16[16,64,1024]{2,1,0:T(8,128)(2,1)}), bf16[2,64,1024]{2,1,0:T(8,128)(2,1)}) %reduce-scatter.2.cloned.1.call-update) | async-done | bytes 262160 | tf_op jit(solution)/shard_map/reduce_scatter | solution.py:36
  59.1 1.5 %convolution_convert_fusion = bf16[128,1280]{1,0:T(8,128)(2,1)S(1)} fusion(bf16[128,1024]{1,0:T(8,128)(2,1)} %bitcast.64, bf16[1024,1280]{1,0:T(8,128)(2,1)S(1)} %copy-done), kind=kOutput, calls=%fused_computation.15 | convolution fusion | flops 335708160 | bytes 3211264 | tf_op jit(solution)/shard_map/dot_general | solution.py:42
  60.6 0.9 copy.29
  61.5 1.3 %reshape.194 = bf16[2,64,32,40]{1,0,3,2:T(2,128)(2,1)S(1)} reshape(bf16[128,1280]{0,1:T(8,128)(2,1)} %copy.29) | data formatting | bytes 655360 | tf_op jit(solution)/shard_map/reshape | solution.py:43
  62.8 1.1 reshape.246
  63.9 11.8 %all-to-all-start = ((bf16[32,2,2560]{2,1,0:T(2,128)(2,1)}), bf16[32,2,2560]{2,1,0:T(2,128)(2,1)}, u32[]{:S(2)}, u32[]{:S(2)}) async-start(bf16[32,2,2560]{2,1,0:T(2,128)(2,1)} %reshape.246), calls=%async_computation.1 | async-start | bytes 655360 | tf_op jit(solution)/shard_map/all_to_all | solution.py:44
  75.8 9.8 %gather_fusion.2 = bf16[2048,1280]{1,0:T(8,128)(2,1)} fusion(bf16[1024,1280]{1,0:T(8,128)(2,1)S(1)} %copy-done, s32[2048]{0:T(1024)S(1)} %broadcast_clamp_fusion), kind=kCustom, calls=%fused_computation.2 | custom fusion | bytes 10493952 | tf_op jit(solution)/shard_map/jit(_take)/gather | solution.py:49
  85.7 1.4 %reshape.247 = bf16[32,40,2,64]{3,2,1,0:T(2,128)(2,1)S(1)} reshape(bf16[32,2,2560]{2,1,0:T(2,128)(2,1)} %all-to-all-done) | data formatting | bytes 655360
  87.6 1.5 %copy.30 = f32[2,32,64,1,40]{2,1,4,0,3:T(8,128)} copy(f32[2,32,64,1,40]{2,0,4,1,3:T(2,128)S(1)} %convert_bitcast_fusion) | data formatting | bytes 1310720 | tf_op jit(solution)/shard_map/convert_element_type | solution.py:51
  89.0 1.7 %reshape.196 = f32[2,2048,40]{1,2,0:T(8,128)S(1)} reshape(f32[2,32,64,1,40]{2,1,4,0,3:T(8,128)} %copy.30) | data formatting | bytes 1310720 | tf_op jit(solution)/shard_map/convert_element_type | solution.py:51
  90.8 11.6 %fusion = f32[2,40,16,1280]{3,2,1,0:T(8,128)} fusion(bf16[2048,1280]{1,0:T(8,128)(2,1)} %gather_fusion.2, f32[2048,16]{0,1:T(8,128)S(1)} %select_convert_fusion, f32[2,2048,40]{1,2,0:T(8,128)S(1)} %reshape.196, pred[2048]{0:T(1024)(128)(4,1)S(1)} %compare_and_fusion), kind=kOutput, calls=%fused_computation.4 | convolution fusion | flops 6718750720 | bytes 12584960 | tf_op jit(solution)/shard_map/qrbi,ra->qbia/dot_general | solution.py:54
  102.4 7.7 %reshape.195 = f32[2,40,20480]{2,1,0:T(8,128)} reshape(f32[2,40,16,1280]{3,2,1,0:T(8,128)} %fusion) | data formatting | bytes 13107200 | tf_op jit(solution)/shard_map/reshape | solution.py:55
  (34 shorter events, 2.1 us)
Async XLA Ops:
  6.5 52.6 %copy-start = (bf16[1024,1280]{1,0:T(8,128)(2,1)S(1)}, bf16[1024,1280]{1,0:T(8,128)(2,1)}, u32[]{:S(2)}) copy-start(bf16[1024,1280]{1,0:T(8,128)(2,1)} %param.15) | copy-start | bytes 7864324
  6.5 52.6 %reduce-scatter.2.cloned.1.call-start = ((), (), s32[]{:S(2)}) async-start(), calls=%async_computation.3 | async-start | bytes 2359296 | tf_op jit(solution)/shard_map/reduce_scatter | solution.py:36
  14.5 2.5 %copy-start.2 = (s32[64]{0:T(128)S(1)}, s32[64]{0:T(128)}, u32[]{:S(2)}) copy-start(s32[64]{0:T(128)} %param.13) | copy-start | bytes 772
  14.6 2.5 %copy-start.3 = (s32[64]{0:T(128)S(1)}, s32[64]{0:T(128)}, u32[]{:S(2)}) copy-start(s32[64]{0:T(128)} %param.12) | copy-start | bytes 772
  14.6 11.9 %copy-start.1 = (bf16[1024,16]{0,1:T(8,128)(2,1)S(1)}, bf16[1024,16]{0,1:T(8,128)(2,1)}, u32[]{:S(2)}) copy-start(bf16[1024,16]{0,1:T(8,128)(2,1)} %param.14) | copy-start | bytes 98308
  17.8 15.5 %all-to-all-start.1 = ((s32[32,1,128]{2,1,0:T(1,128)}), s32[32,1,128]{2,1,0:T(1,128)S(1)}, u32[]{:S(2)}, u32[]{:S(2)}) async-start(s32[32,1,128]{2,1,0:T(1,128)} %reshape.244), calls=%async_computation.2 | async-start | bytes 32768 | tf_op jit(solution)/shard_map/all_to_all | solution.py:19
  63.9 21.8 %all-to-all-start = ((bf16[32,2,2560]{2,1,0:T(2,128)(2,1)}), bf16[32,2,2560]{2,1,0:T(2,128)(2,1)}, u32[]{:S(2)}, u32[]{:S(2)}) async-start(bf16[32,2,2560]{2,1,0:T(2,128)(2,1)} %reshape.246), calls=%async_computation.1 | async-start | bytes 655360 | tf_op jit(solution)/shard_map/all_to_all | solution.py:44
Sparse Core Ops, SparseCore 0:
  17.2 41.8 reduce-scatter.1

commit v3 on v2

--- a/solution.py
+++ b/solution.py
@@ -27,16 +27,20 @@
     live = jnp.arange(slot_count) < tile_count[0, 0]
     occ_blocks = occupied_coef.reshape(basis_count // tile_depth, tile_depth, occ_total)
     occ_slot = jnp.take(occ_blocks, lam_list, axis=0)
-    hit = (pair_list[:, None] == jnp.arange(block_count)[None, :]) & live[:, None]
-    mask = jnp.where(hit[:, :, None, None], occ_slot[:, None, :, :], jnp.zeros((), occ_slot.dtype))
-    partial_value = jnp.einsum(
-        "tgmj,tkms->jgks", mask, tile_data, preferred_element_type=jnp.float32
-    ).reshape(occ_total, rows_here, basis_count)
-
-    own_half = lax.psum_scatter(
-        partial_value.astype(jnp.bfloat16), "lam", scatter_dimension=0, tiled=True
+    occ_slot = jnp.where(live[:, None, None], occ_slot, jnp.zeros((), occ_slot.dtype))
+    contrib = jnp.einsum("tmj,tkms->jtks", occ_slot, tile_data, preferred_element_type=jnp.float32)
+    occ_share = occ_total // lam_count
+    contrib = contrib.astype(jnp.bfloat16).reshape(
+        lam_count, occ_share, slot_count, tile_rows, basis_count
     )
-    occ_share = own_half.shape[0]
+    pair_or_dead = jnp.where(live, pair_list, -1)
+    pair_copies = jnp.broadcast_to(pair_or_dead[None], (lam_count, slot_count))
+    pair_all = lax.all_to_all(pair_copies, "lam", split_axis=0, concat_axis=0, tiled=True)
+    got = lax.all_to_all(contrib, "lam", split_axis=0, concat_axis=0, tiled=True)
+    hit = (pair_all[:, :, None] == jnp.arange(block_count)[None, None, :]).astype(jnp.bfloat16)
+    own_half = jnp.einsum(
+        "ptg,pjtks->jgks", hit, got, preferred_element_type=jnp.float32
+    ).reshape(occ_share, rows_here, basis_count)
     vir_share = vir_total // pair_count
     half_low = own_half.astype(jnp.bfloat16).reshape(occ_share * rows_here, basis_count)
     mixed = jnp.dot(half_low, virtual_coef, preferred_element_type=jnp.float32)

time: 118 us -> 116 us (0.983)
  between operations: 14.3 us -> 0.86 us
  starting transfers between devices: 20.4 us -> 28.3 us
    all_to_all x0 -> x2, waiting for transfers between devices: none -> 22.5 us  [the longest x1 22.5 us: on_device(): lax.all_to_all(contrib, 'lam', split_axis=0, concat_axis=0, tiled=True)]
    reduce_scatter x1 -> x0, waiting for transfers between devices: 17.6 us -> none  [on_device(): lax.psum_scatter(partial_value.astype(jnp.bfloat16), 'lam', scatter_dimen...]
    all_to_all x0 -> x2, starting transfers between devices: none -> 14.8 us  [the longest x1 8.19 us: on_device(): lax.all_to_all(pair_copies, 'lam', split_axis=0, concat_axis=0, tiled=True)]
    all_to_all x1, starting transfers between devices: 11.8 us -> 4.84 us  [on_device(): lax.all_to_all(mixed, 'pair', split_axis=2, concat_axis=1, tiled=True)]
    all_to_all x1, waiting for transfers between devices: 6.75 us -> 2.74 us  [on_device(): lax.all_to_all(index_copies, 'pair', split_axis=0, concat_axis=0, tiled=T...]
    reshape x0 -> x1, local copies, waits for them, and re-layouts: none -> 2.78 us  [on_device(): contrib.astype(jnp.bfloat16)]
    convert_element_type x1 -> x2, local copies, waits for them, and re-layouts: 2.47 us -> 0.27 us  [on_device(): own_half.astype(jnp.bfloat16).reshape(occ_share * rows_here, basis_count)]
    dot_general x1 -> x2, matrix products: 3.64 us -> 5.49 us  [the longest x1 3.89 us: on_device(): jnp.einsum('tmj,tkms->jtks', occ_slot, tile_data, preferred_element_type=...]
  transfers between devices with their start and end apart: 3 -> 4, of which waited for: 2 -> 2; matrix products, arithmetic and copies ran while one was open for 16% -> 25% of each run, Pallas kernels for 0% -> 0%
where the time goes in v3:
time: 116 us; the launch traced here: 115 us
  local copies, waits for them, and re-layouts  38.8 us (33%)
  starting transfers between devices  28.3 us (24%)
  waiting for transfers between devices  25.2 us (22%)
  matrix products  17.6 us (15%)
  other arithmetic  4.03 us (3%)
    all_to_all x1, waiting for transfers between devices, on_device(): lax.all_to_all(contrib, 'lam', split_axis=0, concat_axis=0, tiled=True)  22.5 us
    dot_general x1, matrix products, on_device(): jnp.einsum('qrbi,ra->qbia', scaled, vir_rows, preferred_element_type=jnp....  11.6 us
    gather x1, local copies, waits for them, and re-layouts, on_device(): vir_rows = jnp.take(virtual_coef, both_index[1], axis=0)  9.85 us
    all_to_all x1, starting transfers between devices, on_device(): lax.all_to_all(index_copies, 'pair', split_axis=0, concat_axis=0, tiled=T...  8.59 us
    all_to_all x1, starting transfers between devices, on_device(): lax.all_to_all(pair_copies, 'lam', split_axis=0, concat_axis=0, tiled=True)  8.19 us
    reshape x1, local copies, waits for them, and re-layouts, on_device(): return result.reshape(occ_share, vir_share, occ_total * vir_total)  7.69 us
    all_to_all x1, starting transfers between devices, on_device(): lax.all_to_all(contrib, 'lam', split_axis=0, concat_axis=0, tiled=True)  6.66 us
    gather x2, local copies, waits for them, and re-layouts, on_device(): occ_rows = jnp.take(occupied_coef, both_index[0], axis=0)  6.36 us
  transfers between devices with their start and end apart: 4, of which 2 were waited for; matrix products, arithmetic and copies ran while one was open for 25% of the time, Pallas kernels for 0%

profile of v3, /device:TPU:1, one launch (start us, length us, event | category | flops | bytes accessed | tf_op | source)
XLA Modules:
  0.0 114.8 jit_solution(4605337708380835397)
XLA Ops:
  0.0 0.8 pad_add_fusion
  0.9 0.7 reshape.219
  1.6 8.6 %all-to-all-start.3 = ((s32[32,1,128]{2,1,0:T(1,128)}), s32[32,1,128]{2,1,0:T(1,128)S(1)}, u32[]{:S(2)}, u32[]{:S(2)}) async-start(s32[32,1,128]{2,1,0:T(1,128)} %reshape.219), calls=%async_computation.3 | async-start | bytes 32768 | tf_op jit(solution)/shard_map/all_to_all | solution.py:19
  12.1 0.7 fusion.27
  12.8 0.9 reshape.167
  14.3 2.7 %all-to-all-done.3 = s32[32,1,128]{2,1,0:T(1,128)S(1)} async-done(((s32[32,1,128]{2,1,0:T(1,128)}), s32[32,1,128]{2,1,0:T(1,128)S(1)}, u32[]{:S(2)}, u32[]{:S(2)}) %all-to-all-start.3) | async-done | bytes 16416 | tf_op jit(solution)/shard_map/all_to_all | solution.py:19
  17.6 8.2 %all-to-all-start.1 = ((s32[8,1,8]{2,1,0:T(1,128)}), s32[8,1,8]{2,1,0:T(1,128)S(1)}, u32[]{:S(2)}, u32[]{:S(2)}) async-start(s32[8,1,8]{2,1,0:T(1,128)} %broadcast_in_dim.68), calls=%async_computation.1 | async-start | bytes 8192 | tf_op jit(solution)/shard_map/all_to_all | solution.py:38
  25.8 3.9 %fusion.12 = bf16[16,8,4,1024]{3,0,2,1:T(8,128)(2,1)} fusion(bf16[1,8,4,64,1024]{4,3,2,1,0:T(8,128)(2,1)} %param.8, bf16[8,64,16]{1,2,0:T(8,128)(2,1)S(1)} %gather_fusion, pred[8]{0:T(512)(128)(4,1)S(1)} %compare_and_fusion.2, pred[8]{0:T(512)(128)(4,1)S(1)} %iota_compare_fusion.1), kind=kOutput, calls=%fused_computation.15 | convolution fusion | flops 67649536 | bytes 5259280 | tf_op jit(solution)/shard_map/tmj,tkms->jtks/dot_general | solution.py:31
  29.9 2.8 %copy.46 = bf16[16,8,4,1024]{3,1,2,0:T(8,128)(2,1)} copy(bf16[16,8,4,1024]{3,0,2,1:T(8,128)(2,1)} %fusion.12) | data formatting | bytes 2097152 | tf_op jit(solution)/shard_map/reshape | solution.py:33
  33.2 0.7 reduce.12
  33.9 6.7 %all-to-all-start = ((bf16[8,2,8,4,1024]{4,2,3,1,0:T(8,128)(2,1)}), bf16[8,2,8,4,1024]{4,2,3,1,0:T(8,128)(2,1)}, u32[]{:S(2)}, u32[]{:S(2)}) async-start(bf16[8,2,8,4,1024]{4,2,3,1,0:T(8,128)(2,1)} %bitcast.73), calls=%async_computation | async-start | bytes 2097152 | tf_op jit(solution)/shard_map/all_to_all | solution.py:39
  41.0 6.2 %gather_fusion.1 = bf16[2048,16]{1,0:T(8,128)(2,1)S(1)} fusion(bf16[1024,16]{1,0:T(8,128)(2,1)S(1)} %copy.39, s32[2048]{0:T(1024)S(1)} %broadcast_clamp_fusion.1), kind=kCustom, calls=%fused_computation.1 | custom fusion | bytes 139264 | tf_op jit(solution)/shard_map/jit(_take)/gather | solution.py:52
  47.4 22.5 %all-to-all-done = bf16[8,2,8,4,1024]{4,2,3,1,0:T(8,128)(2,1)} async-done(((bf16[8,2,8,4,1024]{4,2,3,1,0:T(8,128)(2,1)}), bf16[8,2,8,4,1024]{4,2,3,1,0:T(8,128)(2,1)}, u32[]{:S(2)}, u32[]{:S(2)}) %all-to-all-start) | async-done | bytes 1048608 | tf_op jit(solution)/shard_map/all_to_all | solution.py:39
  69.9 1.6 %fusion.22 = bf16[2,4,1024,16,1]{2,3,1,0,4:T(8,128)(2,1)S(1)} fusion(bf16[8,2,8,4,1024]{4,2,3,1,0:T(8,128)(2,1)} %all-to-all-done, s32[8,8]{1,0:T(8,128)S(1)} %bitcast.81), kind=kOutput, calls=%fused_computation.29 | convolution fusion | flops 16778240 | bytes 1310976 | tf_op jit(solution)/shard_map/ptg,pjtks->jgks/dot_general | solution.py:41
  72.4 0.9 copy.37
  73.3 1.3 %reshape.169 = bf16[2,64,32,40]{1,0,3,2:T(2,128)(2,1)S(1)} reshape(bf16[128,1280]{0,1:T(8,128)(2,1)} %copy.37) | data formatting | bytes 655360 | tf_op jit(solution)/shard_map/reshape | solution.py:47
  74.5 1.1 reshape.221
  75.7 4.8 %all-to-all-start.2 = ((bf16[32,2,2560]{2,1,0:T(2,128)(2,1)}), bf16[32,2,2560]{2,1,0:T(2,128)(2,1)}, u32[]{:S(2)}, u32[]{:S(2)}) async-start(bf16[32,2,2560]{2,1,0:T(2,128)(2,1)} %reshape.221), calls=%async_computation.2 | async-start | bytes 655360 | tf_op jit(solution)/shard_map/all_to_all | solution.py:48
  80.6 9.8 %gather_fusion.2 = bf16[2048,1280]{1,0:T(8,128)(2,1)} fusion(bf16[1024,1280]{1,0:T(8,128)(2,1)S(1)} %copy-done, s32[2048]{0:T(1024)S(1)} %broadcast_clamp_fusion), kind=kCustom, calls=%fused_computation.2 | custom fusion | bytes 10493952 | tf_op jit(solution)/shard_map/jit(_take)/gather | solution.py:53
  90.4 1.4 %reshape.222 = bf16[32,40,2,64]{3,2,1,0:T(2,128)(2,1)S(1)} reshape(bf16[32,2,2560]{2,1,0:T(2,128)(2,1)} %all-to-all-done.2) | data formatting | bytes 655360
  92.3 1.5 %copy.38 = f32[2,32,64,1,40]{2,1,4,0,3:T(8,128)} copy(f32[2,32,64,1,40]{2,0,4,1,3:T(2,128)S(1)} %convert_bitcast_fusion) | data formatting | bytes 1310720 | tf_op jit(solution)/shard_map/convert_element_type | solution.py:55
  93.8 1.7 %reshape.171 = f32[2,2048,40]{1,2,0:T(8,128)S(1)} reshape(f32[2,32,64,1,40]{2,1,4,0,3:T(8,128)} %copy.38) | data formatting | bytes 1310720 | tf_op jit(solution)/shard_map/convert_element_type | solution.py:55
  95.5 11.6 %fusion = f32[2,40,16,1280]{3,2,1,0:T(8,128)} fusion(bf16[2048,1280]{1,0:T(8,128)(2,1)} %gather_fusion.2, f32[2048,16]{0,1:T(8,128)S(1)} %select_convert_fusion, f32[2,2048,40]{1,2,0:T(8,128)S(1)} %reshape.171, pred[2048]{0:T(1024)(128)(4,1)S(1)} %compare_and_fusion), kind=kOutput, calls=%fused_computation.4 | convolution fusion | flops 6718750720 | bytes 12584960 | tf_op jit(solution)/shard_map/qrbi,ra->qbia/dot_general | solution.py:58
  107.1 7.7 %reshape.170 = f32[2,40,20480]{2,1,0:T(8,128)} reshape(f32[2,40,16,1280]{3,2,1,0:T(8,128)} %fusion) | data formatting | bytes 13107200 | tf_op jit(solution)/shard_map/reshape | solution.py:59
  (35 shorter events, 5.2 us)
Async XLA Ops:
  0.0 71.8 %copy-start = (bf16[1024,1280]{1,0:T(8,128)(2,1)S(1)}, bf16[1024,1280]{1,0:T(8,128)(2,1)}, u32[]{:S(2)}) copy-start(bf16[1024,1280]{1,0:T(8,128)(2,1)} %param.15) | copy-start | bytes 7864324
  0.0 29.7 %copy-start.1 = (bf16[1024,16]{0,1:T(8,128)(2,1)S(1)}, bf16[1024,16]{0,1:T(8,128)(2,1)}, u32[]{:S(2)}) copy-start(bf16[1024,16]{0,1:T(8,128)(2,1)} %param.14) | copy-start | bytes 98308
  1.6 15.5 %all-to-all-start.3 = ((s32[32,1,128]{2,1,0:T(1,128)}), s32[32,1,128]{2,1,0:T(1,128)S(1)}, u32[]{:S(2)}, u32[]{:S(2)}) async-start(s32[32,1,128]{2,1,0:T(1,128)} %reshape.219), calls=%async_computation.3 | async-start | bytes 32768 | tf_op jit(solution)/shard_map/all_to_all | solution.py:19
  17.6 16.3 %all-to-all-start.1 = ((s32[8,1,8]{2,1,0:T(1,128)}), s32[8,1,8]{2,1,0:T(1,128)S(1)}, u32[]{:S(2)}, u32[]{:S(2)}) async-start(s32[8,1,8]{2,1,0:T(1,128)} %broadcast_in_dim.68), calls=%async_computation.1 | async-start | bytes 8192 | tf_op jit(solution)/shard_map/all_to_all | solution.py:38
  33.9 36.0 %all-to-all-start = ((bf16[8,2,8,4,1024]{4,2,3,1,0:T(8,128)(2,1)}), bf16[8,2,8,4,1024]{4,2,3,1,0:T(8,128)(2,1)}, u32[]{:S(2)}, u32[]{:S(2)}) async-start(bf16[8,2,8,4,1024]{4,2,3,1,0:T(8,128)(2,1)} %bitcast.73), calls=%async_computation | async-start | bytes 2097152 | tf_op jit(solution)/shard_map/all_to_all | solution.py:39
  75.7 14.8 %all-to-all-start.2 = ((bf16[32,2,2560]{2,1,0:T(2,128)(2,1)}), bf16[32,2,2560]{2,1,0:T(2,128)(2,1)}, u32[]{:S(2)}, u32[]{:S(2)}) async-start(bf16[32,2,2560]{2,1,0:T(2,128)(2,1)} %reshape.221), calls=%async_computation.2 | async-start | bytes 655360 | tf_op jit(solution)/shard_map/all_to_all | solution.py:48

commit v4 on v2

--- a/solution.py
+++ b/solution.py
@@ -29,29 +29,33 @@
     occ_slot = jnp.take(occ_blocks, lam_list, axis=0)
     hit = (pair_list[:, None] == jnp.arange(block_count)[None, :]) & live[:, None]
     mask = jnp.where(hit[:, :, None, None], occ_slot[:, None, :, :], jnp.zeros((), occ_slot.dtype))
+    occ_share = occ_total // lam_count
+    mask = mask.reshape(slot_count, block_count, tile_depth, lam_count, occ_share)
     partial_value = jnp.einsum(
-        "tgmj,tkms->jgks", mask, tile_data, preferred_element_type=jnp.float32
-    ).reshape(occ_total, rows_here, basis_count)
+        "tgmlc,tkms->clgks", mask, tile_data, preferred_element_type=jnp.float32
+    ).reshape(occ_share, lam_count, rows_here, basis_count)
 
-    own_half = lax.psum_scatter(
-        partial_value.astype(jnp.bfloat16), "lam", scatter_dimension=0, tiled=True
-    )
-    occ_share = own_half.shape[0]
+    occ_rows = jnp.take(occupied_coef, both_index[0], axis=0).astype(jnp.float32)
+    vir_rows = jnp.take(virtual_coef, both_index[1], axis=0)
     vir_share = vir_total // pair_count
-    half_low = own_half.astype(jnp.bfloat16).reshape(occ_share * rows_here, basis_count)
-    mixed = jnp.dot(half_low, virtual_coef, preferred_element_type=jnp.float32)
-    mixed = mixed.astype(jnp.bfloat16).reshape(occ_share, rows_here, pair_count, vir_share)
-    received = lax.all_to_all(mixed, "pair", split_axis=2, concat_axis=1, tiled=True)
-    total_rows = received.shape[1]
-    mixed_rows = received.reshape(occ_share, total_rows, vir_share)
 
-    occ_rows = jnp.take(occupied_coef, both_index[0], axis=0)
-    vir_rows = jnp.take(virtual_coef, both_index[1], axis=0)
-    scaled = (
-        mixed_rows.astype(jnp.float32)[:, :, :, None]
-        * occ_rows.astype(jnp.float32)[None, :, None, :]
-    ).astype(jnp.bfloat16)
-    result = jnp.einsum("qrbi,ra->qbia", scaled, vir_rows, preferred_element_type=jnp.float32)
+    pieces = []
+    for part in range(occ_share):
+        own_half = lax.psum_scatter(partial_value[part], "lam", scatter_dimension=0, tiled=True)
+        if pieces:
+            pieces[-1], own_half = lax.optimization_barrier((pieces[-1], own_half))
+        half_low = own_half.astype(jnp.bfloat16).reshape(rows_here, basis_count)
+        mixed = jnp.dot(half_low, virtual_coef, preferred_element_type=jnp.float32)
+        mixed = mixed.astype(jnp.bfloat16).reshape(rows_here, pair_count, vir_share)
+        received = lax.all_to_all(mixed, "pair", split_axis=1, concat_axis=0, tiled=True)
+        mixed_rows = received.reshape(pair_count * rows_here, vir_share)
+        scaled = (
+            mixed_rows.astype(jnp.float32)[:, :, None] * occ_rows[:, None, :]
+        ).astype(jnp.bfloat16)
+        pieces.append(
+            jnp.einsum("rbi,ra->bia", scaled, vir_rows, preferred_element_type=jnp.float32)
+        )
+    result = jnp.stack(pieces)
     return result.reshape(occ_share, vir_share, occ_total * vir_total)
 
 

time: 118 us -> 154 us (1.31)
  starting transfers between devices: 20.4 us -> 31.6 us
  waiting for transfers between devices: 24.4 us -> 33.8 us
  matrix products: 16.7 us -> 22.7 us
  other arithmetic: 3.42 us -> 9.32 us
  local copies, waits for them, and re-layouts: 37.7 us -> 41.2 us
    all_to_all x1 -> x2, waiting for transfers between devices: 0.01 us -> 11.7 us  [on_device(): lax.all_to_all(mixed, 'pair', split_axis=1, concat_axis=0, tiled=True)]
    all_to_all x1 -> x2, starting transfers between devices: 11.8 us -> 23 us  [on_device(): lax.all_to_all(mixed, 'pair', split_axis=1, concat_axis=0, tiled=True)]
    reshape x2 -> x0, local copies, waits for them, and re-layouts: 8.95 us -> none  [the longest x1 7.69 us: on_device(): return result.reshape(occ_share, vir_share, occ_total * vir_total)]
    another operation x0 -> x2, local copies, waits for them, and re-layouts: none -> 8.34 us  [on_device(): result = jnp.stack(pieces)]
    squeeze x2 -> x4, local copies, waits for them, and re-layouts: 0.15 us -> 6.82 us  [the longest x2 6.67 us: on_device(): partial_value[part]]
    another operation x0 -> x1, other arithmetic: none -> 6.22 us  [on_device(): result = jnp.stack(pieces)]
    dot_general x2 -> x3, matrix products: 15.2 us -> 19.7 us  [the longest x2 16.1 us: on_device(): jnp.einsum('rbi,ra->bia', scaled, vir_rows, preferred_element_type=jnp.fl...]
    convert_element_type x4 -> x6, local copies, waits for them, and re-layouts: 6.58 us -> 2.63 us  [the longest x4 2.19 us: on_device(): mixed_rows.astype(jnp.float32)[:, :, None] * occ_rows[:, None, :]]
  transfers between devices with their start and end apart: 3 -> 5, of which waited for: 2 -> 5; matrix products, arithmetic and copies ran while one was open for 16% -> 26% of each run, Pallas kernels for 0% -> 0%
where the time goes in v4:
time: 154 us; the launch traced here: 153 us
  local copies, waits for them, and re-layouts  41.2 us (27%)
  waiting for transfers between devices  33.8 us (22%)
  starting transfers between devices  31.6 us (21%)
  matrix products  22.7 us (15%)
  between operations  14.3 us (9%)
  other arithmetic  9.32 us (6%)
    all_to_all x2, starting transfers between devices, on_device(): lax.all_to_all(mixed, 'pair', split_axis=1, concat_axis=0, tiled=True)  23 us
    dot_general x2, matrix products, on_device(): jnp.einsum('rbi,ra->bia', scaled, vir_rows, preferred_element_type=jnp.fl...  16.1 us
    reduce_scatter x2, waiting for transfers between devices, on_device(): lax.psum_scatter(partial_value[part], 'lam', scatter_dimension=0, tiled=T...  15.4 us
    all_to_all x2, waiting for transfers between devices, on_device(): lax.all_to_all(mixed, 'pair', split_axis=1, concat_axis=0, tiled=True)  11.7 us
    gather x1, local copies, waits for them, and re-layouts, on_device(): vir_rows = jnp.take(virtual_coef, both_index[1], axis=0)  9.85 us
    all_to_all x1, starting transfers between devices, on_device(): lax.all_to_all(index_copies, 'pair', split_axis=0, concat_axis=0, tiled=T...  8.59 us
    another operation x2, local copies, waits for them, and re-layouts, on_device(): result = jnp.stack(pieces)  8.34 us
    all_to_all x1, waiting for transfers between devices, on_device(): lax.all_to_all(index_copies, 'pair', split_axis=0, concat_axis=0, tiled=T...  6.68 us
  transfers between devices with their start and end apart: 5, of which 5 were waited for; matrix products, arithmetic and copies ran while one was open for 26% of the time, Pallas kernels for 0%

profile of v4, /device:TPU:1, one launch (start us, length us, event | category | flops | bytes accessed | tf_op | source)
XLA Modules:
  0.0 153.0 jit_solution(12065404693373480224)
XLA Ops:
  10.9 3.6 %fusion.10 = f32[2,8,16,4,1024]{4,1,3,0,2:T(8,128)S(1)} fusion(bf16[1,8,4,64,1024]{4,3,2,1,0:T(8,128)(2,1)} %param.8, pred[8,16]{0,1:T(8,128)(4,1)S(1)} %fusion.22, bf16[8,64,8,2]{1,2,0,3:T(8,128)(2,1)S(1)} %copy.35), kind=kOutput, calls=%fused_computation.19 | convolution fusion | flops 1073872896 | bytes 8405120 | tf_op jit(solution)/shard_map/tgmlc,tkms->clgks/dot_general | solution.py:34
  14.6 1.8 %fusion.27 = (f32[1,8,16,4,1024]{4,1,3,0,2:T(8,128)}, f32[1,8,16,4,1024]{4,1,3,0,2:T(8,128)S(1)}) fusion(f32[2,8,16,4,1024]{4,1,3,0,2:T(8,128)S(1)} %fusion.10), kind=kLoop, calls=%fused_computation.55 | loop fusion | bytes 8388608 | tf_op jit(solution)/shard_map/slice | solution.py:44
  16.3 2.5 %copy.37 = f32[8,64,1024]{2,1,0:T(8,128)} copy(f32[8,64,1024]{2,0,1:T(8,128)S(1)} %bitcast.82) | data formatting | bytes 4194304 | tf_op jit(solution)/shard_map/squeeze | solution.py:44
  18.9 4.1 %copy.42 = f32[8,64,1024]{2,1,0:T(8,128)} copy(f32[8,64,1024]{2,0,1:T(8,128)} %bitcast.81) | data formatting | bytes 4194304 | tf_op jit(solution)/shard_map/squeeze | solution.py:44
  23.9 8.6 %all-to-all-start.1 = ((s32[32,1,128]{2,1,0:T(1,128)}), s32[32,1,128]{2,1,0:T(1,128)S(1)}, u32[]{:S(2)}, u32[]{:S(2)}) async-start(s32[32,1,128]{2,1,0:T(1,128)} %reshape.273), calls=%async_computation.2 | async-start | bytes 32768 | tf_op jit(solution)/shard_map/all_to_all | solution.py:19
  32.6 6.7 %all-to-all-done.1 = s32[32,1,128]{2,1,0:T(1,128)S(1)} async-done(((s32[32,1,128]{2,1,0:T(1,128)}), s32[32,1,128]{2,1,0:T(1,128)S(1)}, u32[]{:S(2)}, u32[]{:S(2)}) %all-to-all-start.1) | async-done | bytes 16416 | tf_op jit(solution)/shard_map/all_to_all | solution.py:19
  41.1 6.2 %gather_fusion.1 = bf16[2048,16]{1,0:T(8,128)(2,1)S(1)} fusion(bf16[1024,16]{1,0:T(8,128)(2,1)S(1)} %copy.40, s32[2048]{0:T(1024)S(1)} %broadcast_clamp_fusion.1), kind=kCustom, calls=%fused_computation.1 | custom fusion | bytes 139264 | tf_op jit(solution)/shard_map/jit(_take)/gather | solution.py:38
  47.5 9.9 %gather_fusion.2 = bf16[2048,1280]{1,0:T(8,128)(2,1)} fusion(bf16[1024,1280]{1,0:T(8,128)(2,1)S(1)} %copy-done, s32[2048]{0:T(1024)S(1)} %broadcast_clamp_fusion), kind=kCustom, calls=%fused_computation.2 | custom fusion | bytes 10493952 | tf_op jit(solution)/shard_map/jit(_take)/gather | solution.py:39
  57.4 3.3 %reduce-scatter.3.cloned.1.call-done = f32[1,64,1024]{2,1,0:T(8,128)} async-done(((f32[8,64,1024]{2,1,0:T(8,128)}), f32[1,64,1024]{2,1,0:T(8,128)}) %reduce-scatter.3.cloned.1.call-update) | async-done | bytes 262160 | tf_op jit(solution)/shard_map/reduce_scatter | solution.py:44
  60.7 1.5 convolution_convert_fusion.1
  63.3 11.6 %all-to-all-start = ((bf16[32,2,1280]{2,1,0:T(2,128)(2,1)}), bf16[32,2,1280]{2,1,0:T(2,128)(2,1)S(1)}, u32[]{:S(2)}, u32[]{:S(2)}) async-start(bf16[32,2,1280]{2,1,0:T(2,128)(2,1)} %reshape.275), calls=%async_computation.1 | async-start | bytes 327680 | tf_op jit(solution)/shard_map/all_to_all | solution.py:50
  74.9 7.9 %all-to-all-done = bf16[32,2,1280]{2,1,0:T(2,128)(2,1)S(1)} async-done(((bf16[32,2,1280]{2,1,0:T(2,128)(2,1)}), bf16[32,2,1280]{2,1,0:T(2,128)(2,1)S(1)}, u32[]{:S(2)}, u32[]{:S(2)}) %all-to-all-start) | async-done | bytes 163872 | tf_op jit(solution)/shard_map/all_to_all | solution.py:50
  83.3 1.0 reshape.223
  84.3 8.1 %fusion.2 = f32[40,16,1280]{2,1,0:T(8,128)} fusion(f32[2048,16]{0,1:T(8,128)S(1)} %select_convert_fusion, f32[2048,40]{0,1:T(8,128)} %reshape.223, bf16[2048,1280]{1,0:T(8,128)(2,1)} %gather_fusion.2, pred[2048]{0:T(1024)(128)(4,1)S(1)} %compare_and_fusion), kind=kOutput, calls=%fused_computation.6 | convolution fusion | flops 3360686080 | bytes 8980480 | tf_op jit(solution)/shard_map/rbi,ra->bia/dot_general | solution.py:56
  92.3 12.1 %reduce-scatter.5.cloned.1.call-done = f32[1,64,1024]{2,1,0:T(8,128)} async-done(((f32[8,64,1024]{2,1,0:T(8,128)}), f32[1,64,1024]{2,1,0:T(8,128)}) %reduce-scatter.5.cloned.1.call-update) | async-done | bytes 262160 | tf_op jit(solution)/shard_map/reduce_scatter | solution.py:44
  104.4 1.5 convolution_convert_fusion
  106.1 0.9 reshape.277
  107.0 11.4 %all-to-all-start.2 = ((bf16[32,2,1280]{2,1,0:T(2,128)(2,1)}), bf16[32,2,1280]{2,1,0:T(2,128)(2,1)S(1)}, u32[]{:S(2)}, u32[]{:S(2)}) async-start(bf16[32,2,1280]{2,1,0:T(2,128)(2,1)} %reshape.277), calls=%async_computation.4 | async-start | bytes 327680 | tf_op jit(solution)/shard_map/all_to_all | solution.py:50
  118.4 4.2 %stack.21 = f32[1,40,20480]{2,1,0:T(8,128)} reshape(f32[40,16,1280]{2,1,0:T(8,128)} %fusion.2) | data formatting | bytes 6553600 | tf_op jit(solution)/shard_map/stack | solution.py:58
  122.6 3.8 %all-to-all-done.2 = bf16[32,2,1280]{2,1,0:T(2,128)(2,1)S(1)} async-done(((bf16[32,2,1280]{2,1,0:T(2,128)(2,1)}), bf16[32,2,1280]{2,1,0:T(2,128)(2,1)S(1)}, u32[]{:S(2)}, u32[]{:S(2)}) %all-to-all-start.2) | async-done | bytes 163872 | tf_op jit(solution)/shard_map/all_to_all | solution.py:50
  126.8 1.0 reshape.224
  127.8 8.0 %fusion = f32[40,16,1280]{2,1,0:T(8,128)} fusion(f32[2048,40]{0,1:T(8,128)} %reshape.224, f32[2048,16]{0,1:T(8,128)S(1)} %select_convert_fusion, bf16[2048,1280]{1,0:T(8,128)(2,1)} %gather_fusion.2, pred[2048]{0:T(1024)(128)(4,1)S(1)} %compare_and_fusion), kind=kOutput, calls=%fused_computation.4 | convolution fusion | flops 3360686080 | bytes 8980480 | tf_op jit(solution)/shard_map/rbi,ra->bia/dot_general | solution.py:56
  135.8 4.2 %stack.22 = f32[1,40,20480]{2,1,0:T(8,128)} reshape(f32[40,16,1280]{2,1,0:T(8,128)} %fusion) | data formatting | bytes 6553600 | tf_op jit(solution)/shard_map/stack | solution.py:58
  139.9 6.2 %pad_maximum_fusion = f32[2,40,20480]{2,1,0:T(8,128)} fusion(f32[1,40,20480]{2,1,0:T(8,128)} %stack.22, f32[1,40,20480]{2,1,0:T(8,128)} %stack.21), kind=kLoop, calls=%fused_computation.3 | loop fusion | flops 1638400 | bytes 13107200 | tf_op jit(solution)/shard_map/stack | solution.py:58
  (51 shorter events, 8.8 us)
Async XLA Ops:
  6.5 40.9 %copy-start = (bf16[1024,1280]{1,0:T(8,128)(2,1)S(1)}, bf16[1024,1280]{1,0:T(8,128)(2,1)}, u32[]{:S(2)}) copy-start(bf16[1024,1280]{1,0:T(8,128)(2,1)} %param.15) | copy-start | bytes 7864324
  6.5 54.1 %reduce-scatter.3.cloned.1.call-start = ((), (), s32[]{:S(2)}) async-start(), calls=%async_computation.5 | async-start | bytes 2359296 | tf_op jit(solution)/shard_map/reduce_scatter | solution.py:44
  18.9 4.2 %copy-start.2 = (s32[64]{0:T(128)S(1)}, s32[64]{0:T(128)}, u32[]{:S(2)}) copy-start(s32[64]{0:T(128)} %param.13) | copy-start | bytes 772
  18.9 4.3 %copy-start.3 = (s32[64]{0:T(128)S(1)}, s32[64]{0:T(128)}, u32[]{:S(2)}) copy-start(s32[64]{0:T(128)} %param.12) | copy-start | bytes 772
  18.9 13.6 %copy-start.1 = (bf16[1024,16]{0,1:T(8,128)(2,1)S(1)}, bf16[1024,16]{0,1:T(8,128)(2,1)}, u32[]{:S(2)}) copy-start(bf16[1024,16]{0,1:T(8,128)(2,1)} %param.14) | copy-start | bytes 98308
  18.9 85.5 %reduce-scatter.5.cloned.1.call-start = ((), (), s32[]{:S(2)}) async-start(), calls=%async_computation.6 | async-start | bytes 2359296 | tf_op jit(solution)/shard_map/reduce_scatter | solution.py:44
  23.9 15.5 %all-to-all-start.1 = ((s32[32,1,128]{2,1,0:T(1,128)}), s32[32,1,128]{2,1,0:T(1,128)S(1)}, u32[]{:S(2)}, u32[]{:S(2)}) async-start(s32[32,1,128]{2,1,0:T(1,128)} %reshape.273), calls=%async_computation.2 | async-start | bytes 32768 | tf_op jit(solution)/shard_map/all_to_all | solution.py:19
  63.3 19.6 %all-to-all-start = ((bf16[32,2,1280]{2,1,0:T(2,128)(2,1)}), bf16[32,2,1280]{2,1,0:T(2,128)(2,1)S(1)}, u32[]{:S(2)}, u32[]{:S(2)}) async-start(bf16[32,2,1280]{2,1,0:T(2,128)(2,1)} %reshape.275), calls=%async_computation.1 | async-start | bytes 327680 | tf_op jit(solution)/shard_map/all_to_all | solution.py:50
  107.0 19.3 %all-to-all-start.2 = ((bf16[32,2,1280]{2,1,0:T(2,128)(2,1)}), bf16[32,2,1280]{2,1,0:T(2,128)(2,1)S(1)}, u32[]{:S(2)}, u32[]{:S(2)}) async-start(bf16[32,2,1280]{2,1,0:T(2,128)(2,1)} %reshape.277), calls=%async_computation.4 | async-start | bytes 327680 | tf_op jit(solution)/shard_map/all_to_all | solution.py:50
Sparse Core Ops, SparseCore 0:
  19.0 41.6 reduce-scatter.2
  63.2 41.1 reduce-scatter.4

commit v5 on v3

--- a/solution.py
+++ b/solution.py
@@ -12,12 +12,8 @@
     basis_count, occ_total = occupied_coef.shape
     vir_total = virtual_coef.shape[1]
     rows_here = mu_index.shape[0]
-
-    index_copies = jnp.broadcast_to(
-        jnp.stack([mu_index, nu_index])[None], (pair_count, 2, rows_here)
-    )
-    both_index = lax.all_to_all(index_copies, "pair", split_axis=0, concat_axis=0, tiled=True)
-    both_index = jnp.transpose(both_index, (1, 0, 2)).reshape(2, pair_count * rows_here)
+    occ_share = occ_total // lam_count
+    vir_share = vir_total // pair_count
 
     tile_data = integrals[0]
     slot_count, tile_rows, tile_depth, _ = tile_data.shape
@@ -29,19 +25,42 @@
     occ_slot = jnp.take(occ_blocks, lam_list, axis=0)
     occ_slot = jnp.where(live[:, None, None], occ_slot, jnp.zeros((), occ_slot.dtype))
     contrib = jnp.einsum("tmj,tkms->jtks", occ_slot, tile_data, preferred_element_type=jnp.float32)
-    occ_share = occ_total // lam_count
-    contrib = contrib.astype(jnp.bfloat16).reshape(
+
+    peak = jnp.maximum(jnp.max(jnp.abs(contrib)), 1e-30)
+    exponent = jnp.clip(jnp.floor(jnp.log2(peak)), -100.0, 100.0)
+    scale = jnp.exp2(13.0 - exponent)
+    payload = (contrib * scale).astype(jnp.float16).reshape(
         lam_count, occ_share, slot_count, tile_rows, basis_count
     )
-    pair_or_dead = jnp.where(live, pair_list, -1)
-    pair_copies = jnp.broadcast_to(pair_or_dead[None], (lam_count, slot_count))
-    pair_all = lax.all_to_all(pair_copies, "lam", split_axis=0, concat_axis=0, tiled=True)
-    got = lax.all_to_all(contrib, "lam", split_axis=0, concat_axis=0, tiled=True)
-    hit = (pair_all[:, :, None] == jnp.arange(block_count)[None, None, :]).astype(jnp.bfloat16)
+    hit = (pair_list[:, None] == jnp.arange(block_count)[None, :]) & live[:, None]
+    info = jnp.zeros((slot_count, 128), jnp.float32)
+    info = info.at[:, :block_count].set(hit.astype(jnp.float32))
+    info = info.at[:, block_count].set(exponent)
+    info = jnp.broadcast_to(
+        info.astype(jnp.float16)[None, None, :, None, :],
+        (lam_count, occ_share, slot_count, tile_rows, 128),
+    )
+    payload = jnp.concatenate([payload, info], axis=4)
+
+    index_copies = jnp.broadcast_to(
+        jnp.stack([mu_index, nu_index])[None], (pair_count, 2, rows_here)
+    )
+    payload, index_copies = lax.optimization_barrier((payload, index_copies))
+    got = lax.all_to_all(payload, "lam", split_axis=0, concat_axis=0, tiled=True)
+    both_index = lax.all_to_all(index_copies, "pair", split_axis=0, concat_axis=0, tiled=True)
+    both_index = jnp.transpose(both_index, (1, 0, 2)).reshape(2, pair_count * rows_here)
+
+    got_info = got[:, 0, :, 0, basis_count:].astype(jnp.float32)
+    unscale = jnp.exp2(got_info[:, 0, block_count] - 13.0)
+    got_hit = got_info[:, :, :block_count] * unscale[:, None, None]
     own_half = jnp.einsum(
-        "ptg,pjtks->jgks", hit, got, preferred_element_type=jnp.float32
+        "ptg,pjtks->jgks",
+        got_hit,
+        got[..., :basis_count].astype(jnp.float32),
+        precision=lax.Precision.HIGHEST,
+        preferred_element_type=jnp.float32,
     ).reshape(occ_share, rows_here, basis_count)
-    vir_share = vir_total // pair_count
+
     half_low = own_half.astype(jnp.bfloat16).reshape(occ_share * rows_here, basis_count)
     mixed = jnp.dot(half_low, virtual_coef, preferred_element_type=jnp.float32)
     mixed = mixed.astype(jnp.bfloat16).reshape(occ_share, rows_here, pair_count, vir_share)

time: 116 us -> 121 us (1.043)
  starting transfers between devices: 28.3 us -> 12.9 us
  blocking collectives: 0 us -> 15.3 us
  other arithmetic: 4.03 us -> 9.99 us
  local copies, waits for them, and re-layouts: 38.8 us -> 36.6 us
  matrix products: 17.6 us -> 19.2 us
  waiting for transfers between devices: 25.2 us -> 23.8 us
  between operations: 0.86 us -> 2.2 us
    all_to_all x0 -> x1, blocking collectives: none -> 15.3 us  [on_device(): lax.all_to_all(index_copies, 'pair', split_axis=0, concat_axis=0, tiled=T...]
    all_to_all x3 -> x1, starting transfers between devices: 23.4 us -> 8.19 us  [on_device(): lax.all_to_all(payload, 'lam', split_axis=0, concat_axis=0, tiled=True)]
    convert_element_type x0 -> x3, other arithmetic: none -> 2.6 us  [the longest x1 1.87 us: on_device(): (contrib * scale).astype(jnp.float16)]
    concatenate x0 -> x1, other arithmetic: none -> 2.55 us  [on_device(): payload = jnp.concatenate([payload, info], axis=4)]
    another operation x0 -> x3, other arithmetic: none -> 2.11 us
    all_to_all x3 -> x1, waiting for transfers between devices: 25.2 us -> 23.8 us  [on_device(): lax.all_to_all(payload, 'lam', split_axis=0, concat_axis=0, tiled=True)]
    unnamed x9 -> x15, local copies, waits for them, and re-layouts: 3.52 us -> 2.94 us
  transfers between devices with their start and end apart: 4 -> 2, of which waited for: 2 -> 1; matrix products, arithmetic and copies ran while one was open for 25% -> 15% of each run, Pallas kernels for 0% -> 0%
where the time goes in v5:
time: 121 us; the launch traced here: 120 us
  local copies, waits for them, and re-layouts  36.6 us (30%)
  waiting for transfers between devices  23.8 us (20%)
  matrix products  19.2 us (16%)
  blocking collectives  15.3 us (13%)
  starting transfers between devices  12.9 us (11%)
  other arithmetic  9.99 us (8%)
  between operations  2.2 us (2%)
    all_to_all x1, waiting for transfers between devices, on_device(): lax.all_to_all(payload, 'lam', split_axis=0, concat_axis=0, tiled=True)  23.8 us
    all_to_all x1, blocking collectives, on_device(): lax.all_to_all(index_copies, 'pair', split_axis=0, concat_axis=0, tiled=T...  15.3 us
    dot_general x1, matrix products, on_device(): jnp.einsum('qrbi,ra->qbia', scaled, vir_rows, preferred_element_type=jnp....  11.6 us
    gather x1, local copies, waits for them, and re-layouts, on_device(): vir_rows = jnp.take(virtual_coef, both_index[1], axis=0)  9.85 us
    all_to_all x1, starting transfers between devices, on_device(): lax.all_to_all(payload, 'lam', split_axis=0, concat_axis=0, tiled=True)  8.19 us
    reshape x1, local copies, waits for them, and re-layouts, on_device(): return result.reshape(occ_share, vir_share, occ_total * vir_total)  7.69 us
    gather x2, local copies, waits for them, and re-layouts, on_device(): occ_rows = jnp.take(occupied_coef, both_index[0], axis=0)  6.36 us
    dot_general x1, matrix products, on_device(): jnp.einsum('tmj,tkms->jtks', occ_slot, tile_data, preferred_element_type=...  4.87 us
  transfers between devices with their start and end apart: 2, of which 1 were waited for; matrix products, arithmetic and copies ran while one was open for 15% of the time, Pallas kernels for 0%

profile of v5, /device:TPU:1, one launch (start us, length us, event | category | flops | bytes accessed | tf_op | source)
XLA Modules:
  0.0 120.0 jit_solution(17618433454761629591)
XLA Ops:
  0.0 0.7 compare_reduce_fusion.1
  2.7 0.7 compare_and_fusion.2
  3.3 0.9 reshape.206
  4.8 4.9 %abs_reduce_fusion = (f32[]{:T(128)}, f32[8,16,4,1024]{3,1,2,0:T(8,128)}) fusion(bf16[1,8,4,64,1024]{4,3,2,1,0:T(8,128)(2,1)} %param.12, bf16[8,64,16]{1,2,0:T(8,128)(2,1)S(1)} %gather_fusion, pred[8]{0:T(512)(128)(4,1)S(1)} %get-tuple-element.39, pred[8]{0:T(512)(128)(4,1)S(1)} %get-tuple-element.40), kind=kOutput, calls=%fused_computation.15 | convolution fusion | flops 68173824 | bytes 6307860 | tf_op jit(solution)/shard_map/tmj,tkms->jtks/dot_general | solution.py:27
  10.4 0.8 convert_select_fusion
  11.8 1.9 %fusion.11 = f16[16,8,4,1024]{3,0,2,1:T(8,128)(2,1)S(1)} fusion(f32[8,16,4,1024]{3,1,2,0:T(8,128)} %get-tuple-element.38, f32[]{:T(128)S(6)} %exp2.15), kind=kLoop, calls=%fused_computation.21 | loop fusion | flops 1048576 | bytes 3145732 | tf_op jit(solution)/shard_map/convert_element_type | solution.py:32
  13.7 1.6 %copy.45 = f16[16,8,4,1024]{3,1,2,0:T(8,128)(2,1)} copy(f16[16,8,4,1024]{3,0,2,1:T(8,128)(2,1)S(1)} %fusion.11) | data formatting | bytes 2097152 | tf_op jit(solution)/shard_map/reshape | solution.py:32
  15.4 2.6 %pad_maximum_fusion = f16[8,2,8,4,1152]{4,2,3,1,0:T(8,128)(2,1)} fusion(f16[8,2,8,4,128]{4,2,3,1,0:T(8,128)(2,1)S(1)} %broadcast_in_dim.66, f16[8,2,8,4,1024]{4,2,3,1,0:T(8,128)(2,1)} %bitcast.79), kind=kLoop, calls=%fused_computation.19 | loop fusion | flops 589824 | bytes 2359296 | tf_op jit(solution)/shard_map/concatenate | solution.py:43
  18.1 15.3 %all_to_all.19 = s32[32,1,128]{2,1,0:T(1,128)S(1)} all-to-all(s32[32,1,128]{2,1,0:T(1,128)S(1)} %reshape.260), channel_id=1, replica_groups=mesh['pair'=32,'lam'=8] {'pair'}, dimensions={0} | all-to-all | bytes 32768 | tf_op jit(solution)/shard_map/all_to_all | solution.py:50
  33.4 8.2 %all-to-all-start = ((f16[8,2,8,4,1152]{4,2,3,1,0:T(8,128)(2,1)}), f16[8,2,8,4,1152]{4,2,3,1,0:T(8,128)(2,1)}, u32[]{:S(2)}, u32[]{:S(2)}) async-start(f16[8,2,8,4,1152]{4,2,3,1,0:T(8,128)(2,1)} %pad_maximum_fusion), calls=%async_computation | async-start | bytes 2359296 | tf_op jit(solution)/shard_map/all_to_all | solution.py:49
  43.5 6.2 %gather_fusion.1 = bf16[2048,16]{1,0:T(8,128)(2,1)S(1)} fusion(bf16[1024,16]{1,0:T(8,128)(2,1)S(1)} %copy.39, s32[2048]{0:T(1024)S(1)} %broadcast_clamp_fusion.1), kind=kCustom, calls=%fused_computation.1 | custom fusion | bytes 139264 | tf_op jit(solution)/shard_map/jit(_take)/gather | solution.py:71
  49.9 23.8 %all-to-all-done = f16[8,2,8,4,1152]{4,2,3,1,0:T(8,128)(2,1)} async-done(((f16[8,2,8,4,1152]{4,2,3,1,0:T(8,128)(2,1)}), f16[8,2,8,4,1152]{4,2,3,1,0:T(8,128)(2,1)}, u32[]{:S(2)}, u32[]{:S(2)}) %all-to-all-start) | async-done | bytes 1179680 | tf_op jit(solution)/shard_map/all_to_all | solution.py:49
  73.8 0.7 fusion.20
  74.7 2.2 %fusion.10 = bf16[2,16,4,1024]{3,1,2,0:T(8,128)(2,1)S(1)} fusion(f16[8,2,8,4,1152]{4,2,3,1,0:T(8,128)(2,1)} %all-to-all-done, f32[8,8,128]{2,1,0:T(8,128)S(1)} %fusion.20, f32[8]{0:T(128)S(1)} %fusion.26), kind=kOutput, calls=%fused_computation.20 | convolution fusion | flops 100795392 | bytes 1343520 | tf_op jit(solution)/shard_map/ptg,pjtks->jgks/dot_general | solution.py:56
  77.7 0.9 copy.37
  78.6 1.3 %reshape.208 = bf16[2,64,32,40]{1,0,3,2:T(2,128)(2,1)S(1)} reshape(bf16[128,1280]{0,1:T(8,128)(2,1)} %copy.37) | data formatting | bytes 655360 | tf_op jit(solution)/shard_map/reshape | solution.py:66
  79.9 1.1 reshape.262
  81.0 4.7 %all-to-all-start.1 = ((bf16[32,2,2560]{2,1,0:T(2,128)(2,1)}), bf16[32,2,2560]{2,1,0:T(2,128)(2,1)}, u32[]{:S(2)}, u32[]{:S(2)}) async-start(bf16[32,2,2560]{2,1,0:T(2,128)(2,1)} %reshape.262), calls=%async_computation.1 | async-start | bytes 655360 | tf_op jit(solution)/shard_map/all_to_all | solution.py:67
  85.8 9.8 %gather_fusion.2 = bf16[2048,1280]{1,0:T(8,128)(2,1)} fusion(bf16[1024,1280]{1,0:T(8,128)(2,1)S(1)} %copy-done, s32[2048]{0:T(1024)S(1)} %broadcast_clamp_fusion), kind=kCustom, calls=%fused_computation.2 | custom fusion | bytes 10493952 | tf_op jit(solution)/shard_map/jit(_take)/gather | solution.py:72
  95.7 1.4 %reshape.263 = bf16[32,40,2,64]{3,2,1,0:T(2,128)(2,1)S(1)} reshape(bf16[32,2,2560]{2,1,0:T(2,128)(2,1)} %all-to-all-done.1) | data formatting | bytes 655360
  97.5 1.5 %copy.38 = f32[2,32,64,1,40]{2,1,4,0,3:T(8,128)} copy(f32[2,32,64,1,40]{2,0,4,1,3:T(2,128)S(1)} %convert_bitcast_fusion) | data formatting | bytes 1310720 | tf_op jit(solution)/shard_map/convert_element_type | solution.py:74
  99.0 1.7 %reshape.211 = f32[2,2048,40]{1,2,0:T(8,128)S(1)} reshape(f32[2,32,64,1,40]{2,1,4,0,3:T(8,128)} %copy.38) | data formatting | bytes 1310720 | tf_op jit(solution)/shard_map/convert_element_type | solution.py:74
  100.7 11.6 %fusion = f32[2,40,16,1280]{3,2,1,0:T(8,128)} fusion(bf16[2048,1280]{1,0:T(8,128)(2,1)} %gather_fusion.2, f32[2048,16]{0,1:T(8,128)S(1)} %select_convert_fusion, f32[2,2048,40]{1,2,0:T(8,128)S(1)} %reshape.211, pred[2048]{0:T(1024)(128)(4,1)S(1)} %compare_and_fusion), kind=kOutput, calls=%fused_computation.4 | convolution fusion | flops 6718750720 | bytes 12584960 | tf_op jit(solution)/shard_map/qrbi,ra->qbia/dot_general | solution.py:77
  112.3 7.7 %reshape.209 = f32[2,40,20480]{2,1,0:T(8,128)} reshape(f32[2,40,16,1280]{3,2,1,0:T(8,128)} %fusion) | data formatting | bytes 13107200 | tf_op jit(solution)/shard_map/reshape | solution.py:78
  (46 shorter events, 5.7 us)
Async XLA Ops:
  0.0 77.2 %copy-start = (bf16[1024,1280]{1,0:T(8,128)(2,1)S(1)}, bf16[1024,1280]{1,0:T(8,128)(2,1)}, u32[]{:S(2)}) copy-start(bf16[1024,1280]{1,0:T(8,128)(2,1)} %param.19) | copy-start | bytes 7864324
  4.8 5.6 %copy-start.4 = (s32[1,8]{1,0:T(1,128)S(1)}, s32[1,8]{1,0:T(1,128)}, u32[]{:S(2)}) copy-start(s32[1,8]{1,0:T(1,128)} %param.13) | copy-start | bytes 100
  11.8 3.6 %copy-start.2 = (s32[64]{0:T(128)S(1)}, s32[64]{0:T(128)}, u32[]{:S(2)}) copy-start(s32[64]{0:T(128)} %param.17) | copy-start | bytes 772
  11.8 3.6 %copy-start.3 = (s32[64]{0:T(128)S(1)}, s32[64]{0:T(128)}, u32[]{:S(2)}) copy-start(s32[64]{0:T(128)} %param.16) | copy-start | bytes 772
  15.3 26.3 %copy-start.1 = (bf16[1024,16]{0,1:T(8,128)(2,1)S(1)}, bf16[1024,16]{0,1:T(8,128)(2,1)}, u32[]{:S(2)}) copy-start(bf16[1024,16]{0,1:T(8,128)(2,1)} %param.18) | copy-start | bytes 98308
  33.4 40.3 %all-to-all-start = ((f16[8,2,8,4,1152]{4,2,3,1,0:T(8,128)(2,1)}), f16[8,2,8,4,1152]{4,2,3,1,0:T(8,128)(2,1)}, u32[]{:S(2)}, u32[]{:S(2)}) async-start(f16[8,2,8,4,1152]{4,2,3,1,0:T(8,128)(2,1)} %pad_maximum_fusion), calls=%async_computation | async-start | bytes 2359296 | tf_op jit(solution)/shard_map/all_to_all | solution.py:49
  81.0 14.6 %all-to-all-start.1 = ((bf16[32,2,2560]{2,1,0:T(2,128)(2,1)}), bf16[32,2,2560]{2,1,0:T(2,128)(2,1)}, u32[]{:S(2)}, u32[]{:S(2)}) async-start(bf16[32,2,2560]{2,1,0:T(2,128)(2,1)} %reshape.262), calls=%async_computation.1 | async-start | bytes 655360 | tf_op jit(solution)/shard_map/all_to_all | solution.py:67

commit v6 on v5

--- a/solution.py
+++ b/solution.py
@@ -42,13 +42,12 @@
     )
     payload = jnp.concatenate([payload, info], axis=4)
 
-    index_copies = jnp.broadcast_to(
-        jnp.stack([mu_index, nu_index])[None], (pair_count, 2, rows_here)
+    own_rows = jnp.zeros((2, pair_count, rows_here), jnp.float32)
+    own_rows = lax.dynamic_update_index_in_dim(
+        own_rows, jnp.stack([mu_index, nu_index]).astype(jnp.float32)[:, None], lax.axis_index("pair"), 1
     )
-    payload, index_copies = lax.optimization_barrier((payload, index_copies))
+    both_index = lax.psum(own_rows, "pair").astype(jnp.int32).reshape(2, pair_count * rows_here)
     got = lax.all_to_all(payload, "lam", split_axis=0, concat_axis=0, tiled=True)
-    both_index = lax.all_to_all(index_copies, "pair", split_axis=0, concat_axis=0, tiled=True)
-    both_index = jnp.transpose(both_index, (1, 0, 2)).reshape(2, pair_count * rows_here)
 
     got_info = got[:, 0, :, 0, basis_count:].astype(jnp.float32)
     unscale = jnp.exp2(got_info[:, 0, block_count] - 13.0)

time: 121 us -> 210 us (1.74)
  blocking collectives: 15.3 us -> 124 us
  waiting for transfers between devices: 23.8 us -> 0.01 us
  starting transfers between devices: 12.9 us -> 18.8 us
    psum x0 -> x1, blocking collectives: none -> 124 us  [on_device(): lax.psum(own_rows, 'pair').astype(jnp.int32)]
    all_to_all x1, waiting for transfers between devices: 23.8 us -> 0.01 us  [on_device(): lax.all_to_all(payload, 'lam', split_axis=0, concat_axis=0, tiled=True)]
    all_to_all x1 -> x0, blocking collectives: 15.3 us -> none  [on_device(): lax.all_to_all(index_copies, 'pair', split_axis=0, concat_axis=0, tiled=T...]
    all_to_all x1, starting transfers between devices: 4.67 us -> 9.83 us  [on_device(): lax.all_to_all(mixed, 'pair', split_axis=2, concat_axis=1, tiled=True)]
  transfers between devices with their start and end apart: 2 -> 2, of which waited for: 1 -> 0; matrix products, arithmetic and copies ran while one was open for 15% -> 8% of each run, Pallas kernels for 0% -> 0%
where the time goes in v6:
time: 210 us; the launch traced here: 209 us
  blocking collectives  124 us (59%)
  local copies, waits for them, and re-layouts  35.8 us (17%)
  matrix products  19.2 us (9%)
  starting transfers between devices  18.8 us (9%)
  other arithmetic  9.33 us (4%)
  between operations  2.18 us (1%)
    psum x1, blocking collectives, on_device(): lax.psum(own_rows, 'pair').astype(jnp.int32)  124 us
    dot_general x1, matrix products, on_device(): jnp.einsum('qrbi,ra->qbia', scaled, vir_rows, preferred_element_type=jnp....  11.6 us
    gather x1, local copies, waits for them, and re-layouts, on_device(): vir_rows = jnp.take(virtual_coef, both_index[1], axis=0)  9.85 us
    all_to_all x1, starting transfers between devices, on_device(): lax.all_to_all(mixed, 'pair', split_axis=2, concat_axis=1, tiled=True)  9.83 us
    all_to_all x1, starting transfers between devices, on_device(): lax.all_to_all(payload, 'lam', split_axis=0, concat_axis=0, tiled=True)  9.01 us
    reshape x1, local copies, waits for them, and re-layouts, on_device(): return result.reshape(occ_share, vir_share, occ_total * vir_total)  7.69 us
    gather x2, local copies, waits for them, and re-layouts, on_device(): occ_rows = jnp.take(occupied_coef, both_index[0], axis=0)  6.36 us
    dot_general x1, matrix products, on_device(): jnp.einsum('tmj,tkms->jtks', occ_slot, tile_data, preferred_element_type=...  4.87 us
  transfers between devices with their start and end apart: 2, of which 0 were waited for; matrix products, arithmetic and copies ran while one was open for 8% of the time, Pallas kernels for 0%

profile of v6, /device:TPU:1, one launch (start us, length us, event | category | flops | bytes accessed | tf_op | source)
XLA Modules:
  0.0 209.2 jit_solution(5575800816990912734)
XLA Ops:
  0.0 0.7 compare_reduce_fusion.1
  2.0 0.7 fusion.28
  2.7 0.7 compare_and_fusion.2
  3.3 0.9 reshape.236
  4.8 4.9 %abs_reduce_fusion = (f32[]{:T(128)}, f32[8,16,4,1024]{3,1,2,0:T(8,128)}) fusion(bf16[1,8,4,64,1024]{4,3,2,1,0:T(8,128)(2,1)} %param.12, bf16[8,64,16]{1,2,0:T(8,128)(2,1)S(1)} %gather_fusion, pred[8]{0:T(512)(128)(4,1)S(1)} %get-tuple-element.33, pred[8]{0:T(512)(128)(4,1)S(1)} %get-tuple-element.34), kind=kOutput, calls=%fused_computation.15 | convolution fusion | flops 68173824 | bytes 6307860 | tf_op jit(solution)/shard_map/tmj,tkms->jtks/dot_general | solution.py:27
  10.4 0.8 convert_select_fusion
  11.8 1.9 fusion.11
  13.6 1.6 copy.45
  15.4 2.6 %pad_maximum_fusion = f16[8,2,8,4,1152]{4,2,3,1,0:T(8,128)(2,1)} fusion(f16[8,2,8,4,128]{4,2,3,1,0:T(8,128)(2,1)S(1)} %broadcast_in_dim.64, f16[8,2,8,4,1024]{4,2,3,1,0:T(8,128)(2,1)} %bitcast.76), kind=kLoop, calls=%fused_computation.19 | loop fusion | flops 589824 | bytes 2359296 | tf_op jit(solution)/shard_map/concatenate | solution.py:43
  17.9 9.0 %all-to-all-start = ((f16[8,2,8,4,1152]{4,2,3,1,0:T(8,128)(2,1)}), f16[8,2,8,4,1152]{4,2,3,1,0:T(8,128)(2,1)}, u32[]{:S(2)}, u32[]{:S(2)}) async-start(f16[8,2,8,4,1152]{4,2,3,1,0:T(8,128)(2,1)} %pad_maximum_fusion), calls=%async_computation | async-start | bytes 2359296 | tf_op jit(solution)/shard_map/all_to_all | solution.py:50
  27.0 123.8 %psum.7 = f32[2,32,64]{2,1,0:T(8,128)S(1)} all-reduce(f32[2,32,64]{2,1,0:T(8,128)S(1)} %dynamic_update_slice.4), channel_id=1, replica_groups=mesh['pair'=32,'lam'=8] {'pair'}, use_global_device_ids=true, to_apply=%region_3.4 | all-reduce | flops 4096 | bytes 32768 | tf_op jit(solution)/shard_map/psum | solution.py:49
  151.3 6.2 %gather_fusion.1 = bf16[2048,16]{1,0:T(8,128)(2,1)S(1)} fusion(bf16[1024,16]{1,0:T(8,128)(2,1)S(1)} %copy.39, s32[2048]{0:T(1024)S(1)} %broadcast_clamp_fusion.1), kind=kCustom, calls=%fused_computation.1 | custom fusion | bytes 139264 | tf_op jit(solution)/shard_map/jit(_take)/gather | solution.py:70
  157.8 0.7 fusion.20
  158.7 2.2 %fusion.10 = bf16[2,16,4,1024]{3,1,2,0:T(8,128)(2,1)S(1)} fusion(f16[8,2,8,4,1152]{4,2,3,1,0:T(8,128)(2,1)} %all-to-all-done, f32[8,8,128]{2,1,0:T(8,128)S(1)} %fusion.20, f32[8]{0:T(128)S(1)} %fusion.26), kind=kOutput, calls=%fused_computation.20 | convolution fusion | flops 100795392 | bytes 1343520 | tf_op jit(solution)/shard_map/ptg,pjtks->jgks/dot_general | solution.py:55
  161.7 0.9 copy.37
  162.6 1.3 reshape.238
  163.9 1.1 reshape.272
  165.0 9.8 %all-to-all-start.1 = ((bf16[32,2,2560]{2,1,0:T(2,128)(2,1)}), bf16[32,2,2560]{2,1,0:T(2,128)(2,1)}, u32[]{:S(2)}, u32[]{:S(2)}) async-start(bf16[32,2,2560]{2,1,0:T(2,128)(2,1)} %reshape.272), calls=%async_computation.1 | async-start | bytes 655360 | tf_op jit(solution)/shard_map/all_to_all | solution.py:66
  174.9 9.8 %gather_fusion.2 = bf16[2048,1280]{1,0:T(8,128)(2,1)} fusion(bf16[1024,1280]{1,0:T(8,128)(2,1)S(1)} %copy-done, s32[2048]{0:T(1024)S(1)} %broadcast_clamp_fusion), kind=kCustom, calls=%fused_computation.2 | custom fusion | bytes 10493952 | tf_op jit(solution)/shard_map/jit(_take)/gather | solution.py:71
  184.8 1.4 reshape.273
  186.7 1.5 copy.38
  188.2 1.7 reshape.241
  189.9 11.6 %fusion = f32[2,40,16,1280]{3,2,1,0:T(8,128)} fusion(bf16[2048,1280]{1,0:T(8,128)(2,1)} %gather_fusion.2, f32[2048,16]{0,1:T(8,128)S(1)} %select_convert_fusion, f32[2,2048,40]{1,2,0:T(8,128)S(1)} %reshape.241, pred[2048]{0:T(1024)(128)(4,1)S(1)} %compare_and_fusion), kind=kOutput, calls=%fused_computation.4 | convolution fusion | flops 6718750720 | bytes 12584960 | tf_op jit(solution)/shard_map/qrbi,ra->qbia/dot_general | solution.py:76
  201.5 7.7 %reshape.239 = f32[2,40,20480]{2,1,0:T(8,128)} reshape(f32[2,40,16,1280]{3,2,1,0:T(8,128)} %fusion) | data formatting | bytes 13107200 | tf_op jit(solution)/shard_map/reshape | solution.py:77
  (44 shorter events, 3.6 us)
Async XLA Ops:
  0.0 161.2 %copy-start = (bf16[1024,1280]{1,0:T(8,128)(2,1)S(1)}, bf16[1024,1280]{1,0:T(8,128)(2,1)}, u32[]{:S(2)}) copy-start(bf16[1024,1280]{1,0:T(8,128)(2,1)} %param.19) | copy-start | bytes 7864324
  4.8 5.6 %copy-start.4 = (s32[1,8]{1,0:T(1,128)S(1)}, s32[1,8]{1,0:T(1,128)}, u32[]{:S(2)}) copy-start(s32[1,8]{1,0:T(1,128)} %param.13) | copy-start | bytes 100
  15.2 11.7 %copy-start.2 = (s32[64]{0:T(128)S(1)}, s32[64]{0:T(128)}, u32[]{:S(2)}) copy-start(s32[64]{0:T(128)} %param.17) | copy-start | bytes 772
  15.2 11.7 %copy-start.3 = (s32[64]{0:T(128)S(1)}, s32[64]{0:T(128)}, u32[]{:S(2)}) copy-start(s32[64]{0:T(128)} %param.16) | copy-start | bytes 772
  15.2 135.8 %copy-start.1 = (bf16[1024,16]{0,1:T(8,128)(2,1)S(1)}, bf16[1024,16]{0,1:T(8,128)(2,1)}, u32[]{:S(2)}) copy-start(bf16[1024,16]{0,1:T(8,128)(2,1)} %param.18) | copy-start | bytes 98308
  17.9 139.8 %all-to-all-start = ((f16[8,2,8,4,1152]{4,2,3,1,0:T(8,128)(2,1)}), f16[8,2,8,4,1152]{4,2,3,1,0:T(8,128)(2,1)}, u32[]{:S(2)}, u32[]{:S(2)}) async-start(f16[8,2,8,4,1152]{4,2,3,1,0:T(8,128)(2,1)} %pad_maximum_fusion), calls=%async_computation | async-start | bytes 2359296 | tf_op jit(solution)/shard_map/all_to_all | solution.py:50
  165.0 19.8 %all-to-all-start.1 = ((bf16[32,2,2560]{2,1,0:T(2,128)(2,1)}), bf16[32,2,2560]{2,1,0:T(2,128)(2,1)}, u32[]{:S(2)}, u32[]{:S(2)}) async-start(bf16[32,2,2560]{2,1,0:T(2,128)(2,1)} %reshape.272), calls=%async_computation.1 | async-start | bytes 655360 | tf_op jit(solution)/shard_map/all_to_all | solution.py:66

commit v7 on v6

--- a/solution.py
+++ b/solution.py
@@ -14,6 +14,12 @@
     rows_here = mu_index.shape[0]
     occ_share = occ_total // lam_count
     vir_share = vir_total // pair_count
+
+    index_copies = jnp.broadcast_to(
+        jnp.stack([mu_index, nu_index])[None], (pair_count, 2, rows_here)
+    )
+    both_index = lax.all_to_all(index_copies, "pair", split_axis=0, concat_axis=0, tiled=True)
+    both_index = jnp.transpose(both_index, (1, 0, 2)).reshape(2, pair_count * rows_here)
 
     tile_data = integrals[0]
     slot_count, tile_rows, tile_depth, _ = tile_data.shape
@@ -42,11 +48,6 @@
     )
     payload = jnp.concatenate([payload, info], axis=4)
 
-    own_rows = jnp.zeros((2, pair_count, rows_here), jnp.float32)
-    own_rows = lax.dynamic_update_index_in_dim(
-        own_rows, jnp.stack([mu_index, nu_index]).astype(jnp.float32)[:, None], lax.axis_index("pair"), 1
-    )
-    both_index = lax.psum(own_rows, "pair").astype(jnp.int32).reshape(2, pair_count * rows_here)
     got = lax.all_to_all(payload, "lam", split_axis=0, concat_axis=0, tiled=True)
 
     got_info = got[:, 0, :, 0, basis_count:].astype(jnp.float32)

time: 210 us -> 118 us (0.56)
  blocking collectives: 124 us -> 0 us
  waiting for transfers between devices: 0.01 us -> 23.8 us
  starting transfers between devices: 18.8 us -> 24.4 us
    psum x1 -> x0, blocking collectives: 124 us -> none  [on_device(): lax.psum(own_rows, 'pair').astype(jnp.int32)]
    all_to_all x1, waiting for transfers between devices: 0.01 us -> 23.8 us  [on_device(): lax.all_to_all(payload, 'lam', split_axis=0, concat_axis=0, tiled=True)]
    all_to_all x0 -> x1, starting transfers between devices: none -> 8.59 us  [on_device(): lax.all_to_all(index_copies, 'pair', split_axis=0, concat_axis=0, tiled=T...]
    all_to_all x1, starting transfers between devices: 9.83 us -> 7.61 us  [on_device(): lax.all_to_all(mixed, 'pair', split_axis=2, concat_axis=1, tiled=True)]
  transfers between devices with their start and end apart: 2 -> 3, of which waited for: 0 -> 1; matrix products, arithmetic and copies ran while one was open for 8% -> 29% of each run, Pallas kernels for 0% -> 0%
where the time goes in v7:
time: 118 us
  local copies, waits for them, and re-layouts  37.2 us (32%)
  starting transfers between devices  24.4 us (21%)
  waiting for transfers between devices  23.8 us (20%)
  matrix products  19.2 us (16%)
  other arithmetic  10.8 us (9%)
  between operations  2.17 us (2%)
    all_to_all x1, waiting for transfers between devices, on_device(): lax.all_to_all(payload, 'lam', split_axis=0, concat_axis=0, tiled=True)  23.8 us
    dot_general x1, matrix products, on_device(): jnp.einsum('qrbi,ra->qbia', scaled, vir_rows, preferred_element_type=jnp....  11.6 us
    gather x1, local copies, waits for them, and re-layouts, on_device(): vir_rows = jnp.take(virtual_coef, both_index[1], axis=0)  9.85 us
    all_to_all x1, starting transfers between devices, on_device(): lax.all_to_all(index_copies, 'pair', split_axis=0, concat_axis=0, tiled=T...  8.59 us
    all_to_all x1, starting transfers between devices, on_device(): lax.all_to_all(payload, 'lam', split_axis=0, concat_axis=0, tiled=True)  8.19 us
    reshape x1, local copies, waits for them, and re-layouts, on_device(): return result.reshape(occ_share, vir_share, occ_total * vir_total)  7.69 us
    all_to_all x1, starting transfers between devices, on_device(): lax.all_to_all(mixed, 'pair', split_axis=2, concat_axis=1, tiled=True)  7.61 us
    gather x2, local copies, waits for them, and re-layouts, on_device(): occ_rows = jnp.take(occupied_coef, both_index[0], axis=0)  6.36 us
  transfers between devices with their start and end apart: 3, of which 1 were waited for; matrix products, arithmetic and copies ran while one was open for 29% of the time, Pallas kernels for 0%

profile of v7, /device:TPU:1, one launch (start us, length us, event | category | flops | bytes accessed | tf_op | source)
XLA Modules:
  0.0 117.6 jit_solution(13312044808587423349)
XLA Ops:
  0.0 0.8 pad_add_fusion
  1.5 8.6 %all-to-all-start.2 = ((s32[32,1,128]{2,1,0:T(1,128)}), s32[32,1,128]{2,1,0:T(1,128)S(1)}, u32[]{:S(2)}, u32[]{:S(2)}) async-start(s32[32,1,128]{2,1,0:T(1,128)} %reshape.260), calls=%async_computation.2 | async-start | bytes 32768 | tf_op jit(solution)/shard_map/all_to_all | solution.py:21
  10.1 0.7 compare_reduce_fusion.1
  13.5 0.9 reshape.206
  15.0 4.9 %abs_reduce_fusion = (f32[]{:T(128)}, f32[8,16,4,1024]{3,1,2,0:T(8,128)}) fusion(bf16[1,8,4,64,1024]{4,3,2,1,0:T(8,128)(2,1)} %param.12, bf16[8,64,16]{1,2,0:T(8,128)(2,1)S(1)} %gather_fusion, pred[8]{0:T(512)(128)(4,1)S(1)} %get-tuple-element.35, pred[8]{0:T(512)(128)(4,1)S(1)} %get-tuple-element.36), kind=kOutput, calls=%fused_computation.15 | convolution fusion | flops 68173824 | bytes 6307860 | tf_op jit(solution)/shard_map/tmj,tkms->jtks/dot_general | solution.py:33
  20.5 0.8 convert_select_fusion
  21.9 1.9 %fusion.11 = f16[16,8,4,1024]{3,0,2,1:T(8,128)(2,1)S(1)} fusion(f32[8,16,4,1024]{3,1,2,0:T(8,128)} %get-tuple-element.34, f32[]{:T(128)S(6)} %exp2.15), kind=kLoop, calls=%fused_computation.21 | loop fusion | flops 1048576 | bytes 3145732 | tf_op jit(solution)/shard_map/convert_element_type | solution.py:38
  23.8 1.6 %copy.45 = f16[16,8,4,1024]{3,1,2,0:T(8,128)(2,1)} copy(f16[16,8,4,1024]{3,0,2,1:T(8,128)(2,1)S(1)} %fusion.11) | data formatting | bytes 2097152 | tf_op jit(solution)/shard_map/reshape | solution.py:38
  25.5 2.6 %pad_maximum_fusion = f16[8,2,8,4,1152]{4,2,3,1,0:T(8,128)(2,1)} fusion(f16[8,2,8,4,128]{4,2,3,1,0:T(8,128)(2,1)S(1)} %broadcast_in_dim.66, f16[8,2,8,4,1024]{4,2,3,1,0:T(8,128)(2,1)} %bitcast.79), kind=kLoop, calls=%fused_computation.19 | loop fusion | flops 589824 | bytes 2359296 | tf_op jit(solution)/shard_map/concatenate | solution.py:49
  28.1 8.2 %all-to-all-start = ((f16[8,2,8,4,1152]{4,2,3,1,0:T(8,128)(2,1)}), f16[8,2,8,4,1152]{4,2,3,1,0:T(8,128)(2,1)}, u32[]{:S(2)}, u32[]{:S(2)}) async-start(f16[8,2,8,4,1152]{4,2,3,1,0:T(8,128)(2,1)} %pad_maximum_fusion), calls=%async_computation | async-start | bytes 2359296 | tf_op jit(solution)/shard_map/all_to_all | solution.py:51
  38.1 6.2 %gather_fusion.1 = bf16[2048,16]{1,0:T(8,128)(2,1)S(1)} fusion(bf16[1024,16]{1,0:T(8,128)(2,1)S(1)} %copy.39, s32[2048]{0:T(1024)S(1)} %broadcast_clamp_fusion.1), kind=kCustom, calls=%fused_computation.1 | custom fusion | bytes 139264 | tf_op jit(solution)/shard_map/jit(_take)/gather | solution.py:71
  44.6 23.8 %all-to-all-done = f16[8,2,8,4,1152]{4,2,3,1,0:T(8,128)(2,1)} async-done(((f16[8,2,8,4,1152]{4,2,3,1,0:T(8,128)(2,1)}), f16[8,2,8,4,1152]{4,2,3,1,0:T(8,128)(2,1)}, u32[]{:S(2)}, u32[]{:S(2)}) %all-to-all-start) | async-done | bytes 1179680 | tf_op jit(solution)/shard_map/all_to_all | solution.py:51
  68.4 0.7 fusion.20
  69.3 2.2 %fusion.10 = bf16[2,16,4,1024]{3,1,2,0:T(8,128)(2,1)S(1)} fusion(f16[8,2,8,4,1152]{4,2,3,1,0:T(8,128)(2,1)} %all-to-all-done, f32[8,8,128]{2,1,0:T(8,128)S(1)} %fusion.20, f32[8]{0:T(128)S(1)} %fusion.26), kind=kOutput, calls=%fused_computation.20 | convolution fusion | flops 100795392 | bytes 1343520 | tf_op jit(solution)/shard_map/ptg,pjtks->jgks/dot_general | solution.py:56
  72.4 0.9 copy.37
  73.3 1.3 %reshape.208 = bf16[2,64,32,40]{1,0,3,2:T(2,128)(2,1)S(1)} reshape(bf16[128,1280]{0,1:T(8,128)(2,1)} %copy.37) | data formatting | bytes 655360 | tf_op jit(solution)/shard_map/reshape | solution.py:66
  74.5 1.1 reshape.262
  75.7 7.6 %all-to-all-start.1 = ((bf16[32,2,2560]{2,1,0:T(2,128)(2,1)}), bf16[32,2,2560]{2,1,0:T(2,128)(2,1)}, u32[]{:S(2)}, u32[]{:S(2)}) async-start(bf16[32,2,2560]{2,1,0:T(2,128)(2,1)} %reshape.262), calls=%async_computation.1 | async-start | bytes 655360 | tf_op jit(solution)/shard_map/all_to_all | solution.py:67
  83.4 9.8 %gather_fusion.2 = bf16[2048,1280]{1,0:T(8,128)(2,1)} fusion(bf16[1024,1280]{1,0:T(8,128)(2,1)S(1)} %copy-done, s32[2048]{0:T(1024)S(1)} %broadcast_clamp_fusion), kind=kCustom, calls=%fused_computation.2 | custom fusion | bytes 10493952 | tf_op jit(solution)/shard_map/jit(_take)/gather | solution.py:72
  93.2 1.4 %reshape.263 = bf16[32,40,2,64]{3,2,1,0:T(2,128)(2,1)S(1)} reshape(bf16[32,2,2560]{2,1,0:T(2,128)(2,1)} %all-to-all-done.1) | data formatting | bytes 655360
  95.1 1.5 %copy.38 = f32[2,32,64,1,40]{2,1,4,0,3:T(8,128)} copy(f32[2,32,64,1,40]{2,0,4,1,3:T(2,128)S(1)} %convert_bitcast_fusion) | data formatting | bytes 1310720 | tf_op jit(solution)/shard_map/convert_element_type | solution.py:74
  96.6 1.7 %reshape.211 = f32[2,2048,40]{1,2,0:T(8,128)S(1)} reshape(f32[2,32,64,1,40]{2,1,4,0,3:T(8,128)} %copy.38) | data formatting | bytes 1310720 | tf_op jit(solution)/shard_map/convert_element_type | solution.py:74
  98.3 11.6 %fusion = f32[2,40,16,1280]{3,2,1,0:T(8,128)} fusion(bf16[2048,1280]{1,0:T(8,128)(2,1)} %gather_fusion.2, f32[2048,16]{0,1:T(8,128)S(1)} %select_convert_fusion, f32[2,2048,40]{1,2,0:T(8,128)S(1)} %reshape.211, pred[2048]{0:T(1024)(128)(4,1)S(1)} %compare_and_fusion), kind=kOutput, calls=%fused_computation.4 | convolution fusion | flops 6718750720 | bytes 12584960 | tf_op jit(solution)/shard_map/qrbi,ra->qbia/dot_general | solution.py:77
  109.9 7.7 %reshape.209 = f32[2,40,20480]{2,1,0:T(8,128)} reshape(f32[2,40,16,1280]{3,2,1,0:T(8,128)} %fusion) | data formatting | bytes 13107200 | tf_op jit(solution)/shard_map/reshape | solution.py:78
  (43 shorter events, 7.0 us)
Async XLA Ops:
  0.0 71.8 %copy-start = (bf16[1024,1280]{1,0:T(8,128)(2,1)S(1)}, bf16[1024,1280]{1,0:T(8,128)(2,1)}, u32[]{:S(2)}) copy-start(bf16[1024,1280]{1,0:T(8,128)(2,1)} %param.19) | copy-start | bytes 7864324
  1.5 26.5 %all-to-all-start.2 = ((s32[32,1,128]{2,1,0:T(1,128)}), s32[32,1,128]{2,1,0:T(1,128)S(1)}, u32[]{:S(2)}, u32[]{:S(2)}) async-start(s32[32,1,128]{2,1,0:T(1,128)} %reshape.260), calls=%async_computation.2 | async-start | bytes 32768 | tf_op jit(solution)/shard_map/all_to_all | solution.py:21
  14.9 5.6 %copy-start.2 = (s32[1,8]{1,0:T(1,128)S(1)}, s32[1,8]{1,0:T(1,128)}, u32[]{:S(2)}) copy-start(s32[1,8]{1,0:T(1,128)} %param.13) | copy-start | bytes 100
  25.4 10.9 %copy-start.1 = (bf16[1024,16]{0,1:T(8,128)(2,1)S(1)}, bf16[1024,16]{0,1:T(8,128)(2,1)}, u32[]{:S(2)}) copy-start(bf16[1024,16]{0,1:T(8,128)(2,1)} %param.18) | copy-start | bytes 98308
  28.1 40.3 %all-to-all-start = ((f16[8,2,8,4,1152]{4,2,3,1,0:T(8,128)(2,1)}), f16[8,2,8,4,1152]{4,2,3,1,0:T(8,128)(2,1)}, u32[]{:S(2)}, u32[]{:S(2)}) async-start(f16[8,2,8,4,1152]{4,2,3,1,0:T(8,128)(2,1)} %pad_maximum_fusion), calls=%async_computation | async-start | bytes 2359296 | tf_op jit(solution)/shard_map/all_to_all | solution.py:51
  75.7 17.6 %all-to-all-start.1 = ((bf16[32,2,2560]{2,1,0:T(2,128)(2,1)}), bf16[32,2,2560]{2,1,0:T(2,128)(2,1)}, u32[]{:S(2)}, u32[]{:S(2)}) async-start(bf16[32,2,2560]{2,1,0:T(2,128)(2,1)} %reshape.262), calls=%async_computation.1 | async-start | bytes 655360 | tf_op jit(solution)/shard_map/all_to_all | solution.py:67

commit v8 on v7

--- a/solution.py
+++ b/solution.py
@@ -1,7 +1,44 @@
 import jax
 import jax.numpy as jnp
 from jax import lax
+from jax.experimental import pallas as pl
+from jax.experimental.pallas import tpu as pltpu
 from jax.sharding import PartitionSpec as P
+
+
+def contract_kernel(mixed_ref, occ_ref, vir_ref, out_ref, stack_ref):
+    vir_share = mixed_ref.shape[1]
+    occ_total = occ_ref.shape[0]
+    vir_total = vir_ref.shape[1]
+    mixed_block = mixed_ref[0]
+    for i in range(occ_total):
+        stack_ref[i * vir_share : (i + 1) * vir_share, :] = mixed_block * occ_ref[i : i + 1, :]
+    product = jnp.dot(
+        stack_ref[...].astype(jnp.bfloat16), vir_ref[...], preferred_element_type=jnp.float32
+    )
+    for i in range(occ_total):
+        out_ref[0, :, i * vir_total : (i + 1) * vir_total] = product[
+            i * vir_share : (i + 1) * vir_share, :
+        ]
+
+
+def final_contract(mixed_t, occ_t, vir_rows, interpret=False):
+    occ_share, vir_share, total_rows = mixed_t.shape
+    occ_total = occ_t.shape[0]
+    vir_total = vir_rows.shape[1]
+    return pl.pallas_call(
+        contract_kernel,
+        grid=(occ_share,),
+        in_specs=[
+            pl.BlockSpec((1, vir_share, total_rows), lambda n: (n, 0, 0)),
+            pl.BlockSpec((occ_total, total_rows), lambda n: (0, 0)),
+            pl.BlockSpec((total_rows, vir_total), lambda n: (0, 0)),
+        ],
+        out_specs=pl.BlockSpec((1, vir_share, occ_total * vir_total), lambda n: (n, 0, 0)),
+        out_shape=jax.ShapeDtypeStruct((occ_share, vir_share, occ_total * vir_total), jnp.float32),
+        scratch_shapes=[pltpu.VMEM((occ_total * vir_share, total_rows), jnp.float32)],
+        interpret=interpret,
+    )(mixed_t, occ_t, vir_rows)
 
 
 def on_device(
@@ -70,13 +107,9 @@
 
     occ_rows = jnp.take(occupied_coef, both_index[0], axis=0)
     vir_rows = jnp.take(virtual_coef, both_index[1], axis=0)
-    scaled = (
-        mixed_rows.astype(jnp.float32)[:, :, :, None]
-        * occ_rows.astype(jnp.float32)[None, :, None, :]
-    ).astype(jnp.bfloat16)
-    result = jnp.einsum("qrbi,ra->qbia", scaled, vir_rows, preferred_element_type=jnp.float32)
-    return result.reshape(occ_share, vir_share, occ_total * vir_total)
-
+    mixed_t = jnp.transpose(mixed_rows, (0, 2, 1)).astype(jnp.float32)
+    occ_t = jnp.transpose(occ_rows).astype(jnp.float32)
+    return final_contract(mixed_t, occ_t, vir_rows)
 
 def solution(mesh):
     placed = (

time: 118 us -> 111 us (0.941)
  matrix products: 19.2 us -> 7.62 us
  Pallas kernels: 0 us -> 11.5 us
  local copies, waits for them, and re-layouts: 37.2 us -> 30.3 us
  waiting for transfers between devices: 23.8 us -> 17.7 us
  other arithmetic: 10.8 us -> 16.7 us
    all_to_all x1, waiting for transfers between devices: 23.8 us -> 8.79 us  [on_device(): lax.all_to_all(payload, 'lam', split_axis=0, concat_axis=0, tiled=True)]
    dot_general x1 -> x0, matrix products: 11.6 us -> none  [on_device(): jnp.einsum('qrbi,ra->qbia', scaled, vir_rows, preferred_element_type=jnp....]
    pallas_call x0 -> x1, Pallas kernels: none -> 11.5 us  [final_contract(): pl.pallas_call(contract_kernel, grid=(occ_share,), in_specs=[pl.BlockSpec...]
    all_to_all x1, waiting for transfers between devices: 0.01 us -> 8.92 us  [on_device(): lax.all_to_all(mixed, 'pair', split_axis=2, concat_axis=1, tiled=True)]
    reshape x1 -> x0, local copies, waits for them, and re-layouts: 7.69 us -> none  [on_device(): return result.reshape(occ_share, vir_share, occ_total * vir_total)]
    select_n x1 -> x2, other arithmetic: 0.01 us -> 5.38 us  [on_device(): vir_rows = jnp.take(virtual_coef, both_index[1], axis=0)]
  transfers between devices with their start and end apart: 3 -> 3, of which waited for: 1 -> 2; matrix products, arithmetic and copies ran while one was open for 29% -> 36% of each run, Pallas kernels for 0% -> 0%
where the time goes in v8:
time: 111 us; the launch traced here: 110 us
  local copies, waits for them, and re-layouts  30.3 us (27%)
  starting transfers between devices  24.4 us (22%)
  waiting for transfers between devices  17.7 us (16%)
  other arithmetic  16.7 us (15%)
  Pallas kernels  11.5 us (10%)
  matrix products  7.62 us (7%)
  between operations  2.23 us (2%)
    pallas_call x1, Pallas kernels, final_contract(): pl.pallas_call(contract_kernel, grid=(occ_share,), in_specs=[pl.BlockSpec...  11.5 us
    gather x1, local copies, waits for them, and re-layouts, on_device(): vir_rows = jnp.take(virtual_coef, both_index[1], axis=0)  9.86 us
    all_to_all x1, waiting for transfers between devices, on_device(): lax.all_to_all(mixed, 'pair', split_axis=2, concat_axis=1, tiled=True)  8.92 us
    all_to_all x1, waiting for transfers between devices, on_device(): lax.all_to_all(payload, 'lam', split_axis=0, concat_axis=0, tiled=True)  8.79 us
    all_to_all x1, starting transfers between devices, on_device(): lax.all_to_all(index_copies, 'pair', split_axis=0, concat_axis=0, tiled=T...  8.59 us
    all_to_all x1, starting transfers between devices, on_device(): lax.all_to_all(payload, 'lam', split_axis=0, concat_axis=0, tiled=True)  8.2 us
    all_to_all x1, starting transfers between devices, on_device(): lax.all_to_all(mixed, 'pair', split_axis=2, concat_axis=1, tiled=True)  7.6 us
    gather x2, local copies, waits for them, and re-layouts, on_device(): occ_rows = jnp.take(occupied_coef, both_index[0], axis=0)  6.36 us
  transfers between devices with their start and end apart: 3, of which 2 were waited for; matrix products, arithmetic and copies ran while one was open for 36% of the time, Pallas kernels for 0%

profile of v8, /device:TPU:1, one launch (start us, length us, event | category | flops | bytes accessed | tf_op | source)
XLA Modules:
  0.0 110.4 jit_solution(11439808898343530314)
XLA Ops:
  0.0 0.8 pad_add_fusion
  0.8 0.7 reshape.239
  1.5 8.6 %all-to-all-start.2 = ((s32[32,1,128]{2,1,0:T(1,128)}), s32[32,1,128]{2,1,0:T(1,128)S(1)}, u32[]{:S(2)}, u32[]{:S(2)}) async-start(s32[32,1,128]{2,1,0:T(1,128)} %reshape.239), calls=%async_computation.2 | async-start | bytes 32768 | tf_op jit(solution)/shard_map/all_to_all | solution.py:58
  13.4 0.9 reshape.185
  14.9 4.9 %abs_reduce_fusion = (f32[]{:T(128)}, f32[8,16,4,1024]{3,1,2,0:T(8,128)}) fusion(bf16[1,8,4,64,1024]{4,3,2,1,0:T(8,128)(2,1)} %param.12, bf16[8,64,16]{1,2,0:T(8,128)(2,1)S(1)} %gather_fusion, pred[8]{0:T(512)(128)(4,1)S(1)} %get-tuple-element.35, pred[8]{0:T(512)(128)(4,1)S(1)} %get-tuple-element.36), kind=kOutput, calls=%fused_computation.8 | convolution fusion | flops 68173824 | bytes 6307860 | tf_op jit(solution)/shard_map/tmj,tkms->jtks/dot_general | solution.py:70
  21.8 1.9 %fusion.4 = f16[16,8,4,1024]{3,0,2,1:T(8,128)(2,1)S(1)} fusion(f32[8,16,4,1024]{3,1,2,0:T(8,128)} %get-tuple-element.34, f32[]{:T(128)S(6)} %exp2.15), kind=kLoop, calls=%fused_computation.14 | loop fusion | flops 1048576 | bytes 3145732 | tf_op jit(solution)/shard_map/convert_element_type | solution.py:75
  23.7 1.6 %copy.37 = f16[16,8,4,1024]{3,1,2,0:T(8,128)(2,1)} copy(f16[16,8,4,1024]{3,0,2,1:T(8,128)(2,1)S(1)} %fusion.4) | data formatting | bytes 2097152 | tf_op jit(solution)/shard_map/reshape | solution.py:75
  25.4 2.6 %pad_maximum_fusion = f16[8,2,8,4,1152]{4,2,3,1,0:T(8,128)(2,1)} fusion(f16[8,2,8,4,128]{4,2,3,1,0:T(8,128)(2,1)S(1)} %broadcast_in_dim.64, f16[8,2,8,4,1024]{4,2,3,1,0:T(8,128)(2,1)} %bitcast.75), kind=kLoop, calls=%fused_computation.12 | loop fusion | flops 589824 | bytes 2359296 | tf_op jit(solution)/shard_map/concatenate | solution.py:86
  28.2 8.2 %all-to-all-start = ((f16[8,2,8,4,1152]{4,2,3,1,0:T(8,128)(2,1)}), f16[8,2,8,4,1152]{4,2,3,1,0:T(8,128)(2,1)}, u32[]{:S(2)}, u32[]{:S(2)}) async-start(f16[8,2,8,4,1152]{4,2,3,1,0:T(8,128)(2,1)} %pad_maximum_fusion), calls=%async_computation | async-start | bytes 2359296 | tf_op jit(solution)/shard_map/all_to_all | solution.py:88
  38.1 6.2 %gather_fusion.1 = bf16[2048,16]{1,0:T(8,128)(2,1)S(1)} fusion(bf16[1024,16]{1,0:T(8,128)(2,1)S(1)} %copy.32, s32[2048]{0:T(1024)S(1)} %broadcast_clamp_fusion.1), kind=kCustom, calls=%fused_computation.1 | custom fusion | bytes 139264 | tf_op jit(solution)/shard_map/jit(_take)/gather | solution.py:108
  44.5 9.9 %gather_fusion.2 = bf16[2048,1280]{1,0:T(8,128)(2,1)} fusion(bf16[1024,1280]{1,0:T(8,128)(2,1)S(1)} %copy-done, s32[2048]{0:T(1024)S(1)} %broadcast_clamp_fusion), kind=kCustom, calls=%fused_computation.2 | custom fusion | bytes 10493952 | tf_op jit(solution)/shard_map/jit(_take)/gather | solution.py:109
  54.4 5.4 %broadcast_select_fusion.vir_ref = bf16[2048,1280]{1,0:T(8,128)(2,1)} fusion(bf16[2048,1280]{1,0:T(8,128)(2,1)} %gather_fusion.2, pred[2048]{0:T(1024)(128)(4,1)S(1)} %compare_and_fusion), kind=kLoop, calls=%fused_computation.3 | loop fusion | flops 2621440 | bytes 10487808 | tf_op jit(solution)/shard_map/jit(_take)/select_n | solution.py:109
  59.8 8.8 %all-to-all-done = f16[8,2,8,4,1152]{4,2,3,1,0:T(8,128)(2,1)} async-done(((f16[8,2,8,4,1152]{4,2,3,1,0:T(8,128)(2,1)}), f16[8,2,8,4,1152]{4,2,3,1,0:T(8,128)(2,1)}, u32[]{:S(2)}, u32[]{:S(2)}) %all-to-all-start) | async-done | bytes 1179680 | tf_op jit(solution)/shard_map/all_to_all | solution.py:88
  68.5 0.7 fusion.13
  69.5 2.2 %fusion.3 = bf16[2,16,4,1024]{3,1,2,0:T(8,128)(2,1)S(1)} fusion(f16[8,2,8,4,1152]{4,2,3,1,0:T(8,128)(2,1)} %all-to-all-done, f32[8,8,128]{2,1,0:T(8,128)S(1)} %fusion.13, f32[8]{0:T(128)S(1)} %fusion.19), kind=kOutput, calls=%fused_computation.13 | convolution fusion | flops 100795392 | bytes 1343520 | tf_op jit(solution)/shard_map/ptg,pjtks->jgks/dot_general | solution.py:93
  72.5 0.9 copy.30
  73.4 1.3 %reshape.187 = bf16[2,64,32,40]{1,0,3,2:T(2,128)(2,1)S(1)} reshape(bf16[128,1280]{0,1:T(8,128)(2,1)} %copy.30) | data formatting | bytes 655360 | tf_op jit(solution)/shard_map/reshape | solution.py:103
  74.7 1.1 %reshape.237 = bf16[32,2,2560]{2,1,0:T(2,128)(2,1)} reshape(bf16[32,40,2,64]{3,2,1,0:T(2,128)(2,1)S(1)} %bitcast.77) | data formatting | bytes 655360
  75.8 7.6 %all-to-all-start.1 = ((bf16[32,2,2560]{2,1,0:T(2,128)(2,1)}), bf16[32,2,2560]{2,1,0:T(2,128)(2,1)}, u32[]{:S(2)}, u32[]{:S(2)}) async-start(bf16[32,2,2560]{2,1,0:T(2,128)(2,1)} %reshape.237), calls=%async_computation.1 | async-start | bytes 655360 | tf_op jit(solution)/shard_map/all_to_all | solution.py:104
  84.1 8.9 %all-to-all-done.1 = bf16[32,2,2560]{2,1,0:T(2,128)(2,1)} async-done(((bf16[32,2,2560]{2,1,0:T(2,128)(2,1)}), bf16[32,2,2560]{2,1,0:T(2,128)(2,1)}, u32[]{:S(2)}, u32[]{:S(2)}) %all-to-all-start.1) | async-done | bytes 327712 | tf_op jit(solution)/shard_map/all_to_all | solution.py:104
  93.0 1.4 %reshape.238 = bf16[32,40,2,64]{3,2,1,0:T(2,128)(2,1)S(1)} reshape(bf16[32,2,2560]{2,1,0:T(2,128)(2,1)} %all-to-all-done.1) | data formatting | bytes 655360
  94.9 1.5 %copy.31 = f32[2,32,64,1,40]{2,1,4,0,3:T(8,128)} copy(f32[2,32,64,1,40]{2,0,4,1,3:T(2,128)S(1)} %convert_bitcast_fusion) | data formatting | bytes 1310720 | tf_op jit(solution)/shard_map/convert_element_type | solution.py:110
  96.3 2.6 %reshape.189 = f32[2,2048,40]{1,2,0:T(8,128)} reshape(f32[2,32,64,1,40]{2,1,4,0,3:T(8,128)} %copy.31) | data formatting | bytes 1310720 | tf_op jit(solution)/shard_map/convert_element_type | solution.py:110
  98.9 11.5 %shard_map.82 = f32[2,40,20480]{2,1,0:T(8,128)} custom-call(f32[2,40,2048]{2,1,0:T(8,128)} %bitcast.76, f32[16,2048]{1,0:T(8,128)} %convert_bitcast_fusion.1.occ_ref, bf16[2048,1280]{1,0:T(8,128)(2,1)} %broadcast_select_fusion.vir_ref), custom_call_target="tpu_custom_call" | custom-call | tf_op jit(solution)/shard_map/pallas_call | solution.py:29
  (43 shorter events, 8.2 us)
Async XLA Ops:
  0.0 44.5 %copy-start = (bf16[1024,1280]{1,0:T(8,128)(2,1)S(1)}, bf16[1024,1280]{1,0:T(8,128)(2,1)}, u32[]{:S(2)}) copy-start(bf16[1024,1280]{1,0:T(8,128)(2,1)} %param.19) | copy-start | bytes 7864324
  1.5 26.6 %all-to-all-start.2 = ((s32[32,1,128]{2,1,0:T(1,128)}), s32[32,1,128]{2,1,0:T(1,128)S(1)}, u32[]{:S(2)}, u32[]{:S(2)}) async-start(s32[32,1,128]{2,1,0:T(1,128)} %reshape.239), calls=%async_computation.2 | async-start | bytes 32768 | tf_op jit(solution)/shard_map/all_to_all | solution.py:58
  14.9 5.6 %copy-start.2 = (s32[1,8]{1,0:T(1,128)S(1)}, s32[1,8]{1,0:T(1,128)}, u32[]{:S(2)}) copy-start(s32[1,8]{1,0:T(1,128)} %param.13) | copy-start | bytes 100
  23.7 4.3 %copy-start.1 = (bf16[1024,16]{0,1:T(8,128)(2,1)S(1)}, bf16[1024,16]{0,1:T(8,128)(2,1)}, u32[]{:S(2)}) copy-start(bf16[1024,16]{0,1:T(8,128)(2,1)} %param.18) | copy-start | bytes 98308
  28.2 40.4 %all-to-all-start = ((f16[8,2,8,4,1152]{4,2,3,1,0:T(8,128)(2,1)}), f16[8,2,8,4,1152]{4,2,3,1,0:T(8,128)(2,1)}, u32[]{:S(2)}, u32[]{:S(2)}) async-start(f16[8,2,8,4,1152]{4,2,3,1,0:T(8,128)(2,1)} %pad_maximum_fusion), calls=%async_computation | async-start | bytes 2359296 | tf_op jit(solution)/shard_map/all_to_all | solution.py:88
  75.8 17.2 %all-to-all-start.1 = ((bf16[32,2,2560]{2,1,0:T(2,128)(2,1)}), bf16[32,2,2560]{2,1,0:T(2,128)(2,1)}, u32[]{:S(2)}, u32[]{:S(2)}) async-start(bf16[32,2,2560]{2,1,0:T(2,128)(2,1)} %reshape.237), calls=%async_computation.1 | async-start | bytes 655360 | tf_op jit(solution)/shard_map/all_to_all | solution.py:104

commit v9 on v8

--- a/solution.py
+++ b/solution.py
@@ -10,7 +10,7 @@
     vir_share = mixed_ref.shape[1]
     occ_total = occ_ref.shape[0]
     vir_total = vir_ref.shape[1]
-    mixed_block = mixed_ref[0]
+    mixed_block = mixed_ref[0].astype(jnp.float32)
     for i in range(occ_total):
         stack_ref[i * vir_share : (i + 1) * vir_share, :] = mixed_block * occ_ref[i : i + 1, :]
     product = jnp.dot(
@@ -107,7 +107,7 @@
 
     occ_rows = jnp.take(occupied_coef, both_index[0], axis=0)
     vir_rows = jnp.take(virtual_coef, both_index[1], axis=0)
-    mixed_t = jnp.transpose(mixed_rows, (0, 2, 1)).astype(jnp.float32)
+    mixed_t = jnp.transpose(mixed_rows, (0, 2, 1))
     occ_t = jnp.transpose(occ_rows).astype(jnp.float32)
     return final_contract(mixed_t, occ_t, vir_rows)
 

time: 111 us -> 108 us (0.973)
  local copies, waits for them, and re-layouts: 30.3 us -> 28.1 us
    convert_element_type x2 -> x0, local copies, waits for them, and re-layouts: 4.05 us -> none  [on_device(): mixed_t = jnp.transpose(mixed_rows, (0, 2, 1)).astype(jnp.float32)]
    reshape x0 -> x1, local copies, waits for them, and re-layouts: none -> 1.25 us  [on_device(): mixed_rows = received.reshape(occ_share, total_rows, vir_share)]
  transfers between devices with their start and end apart: 3 -> 3, of which waited for: 2 -> 2; matrix products, arithmetic and copies ran while one was open for 36% -> 37% of each run, Pallas kernels for 0% -> 0%
where the time goes in v9:
time: 108 us
  local copies, waits for them, and re-layouts  28.1 us (26%)
  starting transfers between devices  24.4 us (23%)
  waiting for transfers between devices  17.7 us (16%)
  other arithmetic  16.2 us (15%)
  Pallas kernels  11.5 us (11%)
  matrix products  7.62 us (7%)
  between operations  2.24 us (2%)
    pallas_call x1, Pallas kernels, final_contract(): pl.pallas_call(contract_kernel, grid=(occ_share,), in_specs=[pl.BlockSpec...  11.5 us
    gather x1, local copies, waits for them, and re-layouts, on_device(): vir_rows = jnp.take(virtual_coef, both_index[1], axis=0)  9.85 us
    all_to_all x1, waiting for transfers between devices, on_device(): lax.all_to_all(mixed, 'pair', split_axis=2, concat_axis=1, tiled=True)  8.92 us
    all_to_all x1, waiting for transfers between devices, on_device(): lax.all_to_all(payload, 'lam', split_axis=0, concat_axis=0, tiled=True)  8.79 us
    all_to_all x1, starting transfers between devices, on_device(): lax.all_to_all(index_copies, 'pair', split_axis=0, concat_axis=0, tiled=T...  8.59 us
    all_to_all x1, starting transfers between devices, on_device(): lax.all_to_all(payload, 'lam', split_axis=0, concat_axis=0, tiled=True)  8.2 us
    all_to_all x1, starting transfers between devices, on_device(): lax.all_to_all(mixed, 'pair', split_axis=2, concat_axis=1, tiled=True)  7.6 us
    gather x2, local copies, waits for them, and re-layouts, on_device(): occ_rows = jnp.take(occupied_coef, both_index[0], axis=0)  6.36 us
  transfers between devices with their start and end apart: 3, of which 2 were waited for; matrix products, arithmetic and copies ran while one was open for 37% of the time, Pallas kernels for 0%

profile of v9, /device:TPU:1, one launch (start us, length us, event | category | flops | bytes accessed | tf_op | source)
XLA Modules:
  0.0 107.8 jit_solution(5113812566268063783)
XLA Ops:
  0.0 0.8 pad_add_fusion
  0.8 0.7 reshape.236
  1.5 8.6 %all-to-all-start.2 = ((s32[32,1,128]{2,1,0:T(1,128)}), s32[32,1,128]{2,1,0:T(1,128)S(1)}, u32[]{:S(2)}, u32[]{:S(2)}) async-start(s32[32,1,128]{2,1,0:T(1,128)} %reshape.236), calls=%async_computation.2 | async-start | bytes 32768 | tf_op jit(solution)/shard_map/all_to_all | solution.py:58
  13.4 0.9 reshape.183
  14.9 4.9 %abs_reduce_fusion = (f32[]{:T(128)}, f32[8,16,4,1024]{3,1,2,0:T(8,128)}) fusion(bf16[1,8,4,64,1024]{4,3,2,1,0:T(8,128)(2,1)} %param.12, bf16[8,64,16]{1,2,0:T(8,128)(2,1)S(1)} %gather_fusion, pred[8]{0:T(512)(128)(4,1)S(1)} %get-tuple-element.35, pred[8]{0:T(512)(128)(4,1)S(1)} %get-tuple-element.36), kind=kOutput, calls=%fused_computation.8 | convolution fusion | flops 68173824 | bytes 6307860 | tf_op jit(solution)/shard_map/tmj,tkms->jtks/dot_general | solution.py:70
  21.8 1.9 %fusion.4 = f16[16,8,4,1024]{3,0,2,1:T(8,128)(2,1)S(1)} fusion(f32[8,16,4,1024]{3,1,2,0:T(8,128)} %get-tuple-element.34, f32[]{:T(128)S(6)} %exp2.15), kind=kLoop, calls=%fused_computation.13 | loop fusion | flops 1048576 | bytes 3145732 | tf_op jit(solution)/shard_map/convert_element_type | solution.py:75
  23.7 1.6 %copy.37 = f16[16,8,4,1024]{3,1,2,0:T(8,128)(2,1)} copy(f16[16,8,4,1024]{3,0,2,1:T(8,128)(2,1)S(1)} %fusion.4) | data formatting | bytes 2097152 | tf_op jit(solution)/shard_map/reshape | solution.py:75
  25.4 2.6 %pad_maximum_fusion = f16[8,2,8,4,1152]{4,2,3,1,0:T(8,128)(2,1)} fusion(f16[8,2,8,4,128]{4,2,3,1,0:T(8,128)(2,1)S(1)} %broadcast_in_dim.64, f16[8,2,8,4,1024]{4,2,3,1,0:T(8,128)(2,1)} %bitcast.74), kind=kLoop, calls=%fused_computation.11 | loop fusion | flops 589824 | bytes 2359296 | tf_op jit(solution)/shard_map/concatenate | solution.py:86
  28.2 8.2 %all-to-all-start = ((f16[8,2,8,4,1152]{4,2,3,1,0:T(8,128)(2,1)}), f16[8,2,8,4,1152]{4,2,3,1,0:T(8,128)(2,1)}, u32[]{:S(2)}, u32[]{:S(2)}) async-start(f16[8,2,8,4,1152]{4,2,3,1,0:T(8,128)(2,1)} %pad_maximum_fusion), calls=%async_computation | async-start | bytes 2359296 | tf_op jit(solution)/shard_map/all_to_all | solution.py:88
  36.9 0.7 reduce.31
  38.1 6.2 %gather_fusion.1 = bf16[2048,16]{1,0:T(8,128)(2,1)S(1)} fusion(bf16[1024,16]{1,0:T(8,128)(2,1)S(1)} %copy.32, s32[2048]{0:T(1024)S(1)} %broadcast_clamp_fusion.1), kind=kCustom, calls=%fused_computation.1 | custom fusion | bytes 139264 | tf_op jit(solution)/shard_map/jit(_take)/gather | solution.py:108
  44.5 9.9 %gather_fusion.2 = bf16[2048,1280]{1,0:T(8,128)(2,1)} fusion(bf16[1024,1280]{1,0:T(8,128)(2,1)S(1)} %copy-done, s32[2048]{0:T(1024)S(1)} %broadcast_clamp_fusion), kind=kCustom, calls=%fused_computation.2 | custom fusion | bytes 10493952 | tf_op jit(solution)/shard_map/jit(_take)/gather | solution.py:109
  54.4 5.4 %broadcast_select_fusion.vir_ref = bf16[2048,1280]{1,0:T(8,128)(2,1)} fusion(bf16[2048,1280]{1,0:T(8,128)(2,1)} %gather_fusion.2, pred[2048]{0:T(1024)(128)(4,1)S(1)} %compare_and_fusion), kind=kLoop, calls=%fused_computation.3 | loop fusion | flops 2621440 | bytes 10487808 | tf_op jit(solution)/shard_map/jit(_take)/select_n | solution.py:109
  59.8 8.8 %all-to-all-done = f16[8,2,8,4,1152]{4,2,3,1,0:T(8,128)(2,1)} async-done(((f16[8,2,8,4,1152]{4,2,3,1,0:T(8,128)(2,1)}), f16[8,2,8,4,1152]{4,2,3,1,0:T(8,128)(2,1)}, u32[]{:S(2)}, u32[]{:S(2)}) %all-to-all-start) | async-done | bytes 1179680 | tf_op jit(solution)/shard_map/all_to_all | solution.py:88
  68.5 0.7 fusion.13
  69.5 2.2 %fusion.3 = bf16[2,16,4,1024]{3,1,2,0:T(8,128)(2,1)S(1)} fusion(f16[8,2,8,4,1152]{4,2,3,1,0:T(8,128)(2,1)} %all-to-all-done, f32[8,8,128]{2,1,0:T(8,128)S(1)} %fusion.13, f32[8]{0:T(128)S(1)} %fusion.19), kind=kOutput, calls=%fused_computation.12 | convolution fusion | flops 100795392 | bytes 1343520 | tf_op jit(solution)/shard_map/ptg,pjtks->jgks/dot_general | solution.py:93
  72.5 0.9 copy.30
  73.4 1.3 %reshape.185 = bf16[2,64,32,40]{1,0,3,2:T(2,128)(2,1)S(1)} reshape(bf16[128,1280]{0,1:T(8,128)(2,1)} %copy.30) | data formatting | bytes 655360 | tf_op jit(solution)/shard_map/reshape | solution.py:103
  74.7 1.1 %reshape.234 = bf16[32,2,2560]{2,1,0:T(2,128)(2,1)} reshape(bf16[32,40,2,64]{3,2,1,0:T(2,128)(2,1)S(1)} %bitcast.75) | data formatting | bytes 655360
  75.8 7.6 %all-to-all-start.1 = ((bf16[32,2,2560]{2,1,0:T(2,128)(2,1)}), bf16[32,2,2560]{2,1,0:T(2,128)(2,1)}, u32[]{:S(2)}, u32[]{:S(2)}) async-start(bf16[32,2,2560]{2,1,0:T(2,128)(2,1)} %reshape.234), calls=%async_computation.1 | async-start | bytes 655360 | tf_op jit(solution)/shard_map/all_to_all | solution.py:104
  84.1 8.9 %all-to-all-done.1 = bf16[32,2,2560]{2,1,0:T(2,128)(2,1)} async-done(((bf16[32,2,2560]{2,1,0:T(2,128)(2,1)}), bf16[32,2,2560]{2,1,0:T(2,128)(2,1)}, u32[]{:S(2)}, u32[]{:S(2)}) %all-to-all-start.1) | async-done | bytes 327712 | tf_op jit(solution)/shard_map/all_to_all | solution.py:104
  93.0 1.4 %reshape.235 = bf16[32,40,2,64]{3,2,1,0:T(2,128)(2,1)S(1)} reshape(bf16[32,2,2560]{2,1,0:T(2,128)(2,1)} %all-to-all-done.1) | data formatting | bytes 655360
  95.1 1.3 %reshape.186 = bf16[2,2048,40]{1,2,0:T(8,128)(2,1)} reshape(bf16[2,32,64,1,40]{2,1,4,0,3:T(8,128)(2,1)S(1)} %copy.31) | data formatting | bytes 655360 | tf_op jit(solution)/shard_map/reshape | solution.py:106
  96.3 11.5 %shard_map.82 = f32[2,40,20480]{2,1,0:T(8,128)} custom-call(bf16[2,40,2048]{2,1,0:T(8,128)(2,1)} %bitcast.76, f32[16,2048]{1,0:T(8,128)} %convert_bitcast_fusion.occ_ref, bf16[2048,1280]{1,0:T(8,128)(2,1)} %broadcast_select_fusion.vir_ref), custom_call_target="tpu_custom_call" | custom-call | tf_op jit(solution)/shard_map/pallas_call | solution.py:29
  (43 shorter events, 7.7 us)
Async XLA Ops:
  0.0 44.5 %copy-start = (bf16[1024,1280]{1,0:T(8,128)(2,1)S(1)}, bf16[1024,1280]{1,0:T(8,128)(2,1)}, u32[]{:S(2)}) copy-start(bf16[1024,1280]{1,0:T(8,128)(2,1)} %param.19) | copy-start | bytes 7864324
  1.5 26.6 %all-to-all-start.2 = ((s32[32,1,128]{2,1,0:T(1,128)}), s32[32,1,128]{2,1,0:T(1,128)S(1)}, u32[]{:S(2)}, u32[]{:S(2)}) async-start(s32[32,1,128]{2,1,0:T(1,128)} %reshape.236), calls=%async_computation.2 | async-start | bytes 32768 | tf_op jit(solution)/shard_map/all_to_all | solution.py:58
  14.9 5.6 %copy-start.2 = (s32[1,8]{1,0:T(1,128)S(1)}, s32[1,8]{1,0:T(1,128)}, u32[]{:S(2)}) copy-start(s32[1,8]{1,0:T(1,128)} %param.13) | copy-start | bytes 100
  23.7 4.3 %copy-start.1 = (bf16[1024,16]{0,1:T(8,128)(2,1)S(1)}, bf16[1024,16]{0,1:T(8,128)(2,1)}, u32[]{:S(2)}) copy-start(bf16[1024,16]{0,1:T(8,128)(2,1)} %param.18) | copy-start | bytes 98308
  28.2 40.4 %all-to-all-start = ((f16[8,2,8,4,1152]{4,2,3,1,0:T(8,128)(2,1)}), f16[8,2,8,4,1152]{4,2,3,1,0:T(8,128)(2,1)}, u32[]{:S(2)}, u32[]{:S(2)}) async-start(f16[8,2,8,4,1152]{4,2,3,1,0:T(8,128)(2,1)} %pad_maximum_fusion), calls=%async_computation | async-start | bytes 2359296 | tf_op jit(solution)/shard_map/all_to_all | solution.py:88
  75.8 17.2 %all-to-all-start.1 = ((bf16[32,2,2560]{2,1,0:T(2,128)(2,1)}), bf16[32,2,2560]{2,1,0:T(2,128)(2,1)}, u32[]{:S(2)}, u32[]{:S(2)}) async-start(bf16[32,2,2560]{2,1,0:T(2,128)(2,1)} %reshape.234), calls=%async_computation.1 | async-start | bytes 655360 | tf_op jit(solution)/shard_map/all_to_all | solution.py:104

commit v10 on v9

--- a/solution.py
+++ b/solution.py
@@ -85,7 +85,13 @@
     )
     payload = jnp.concatenate([payload, info], axis=4)
 
-    got = lax.all_to_all(payload, "lam", split_axis=0, concat_axis=0, tiled=True)
+    lam_here = lax.axis_index("lam")
+    arrived = [lax.dynamic_index_in_dim(payload, lam_here, 0, keepdims=False)]
+    for shift in range(1, lam_count):
+        outgoing = lax.dynamic_index_in_dim(payload, (lam_here + shift) % lam_count, 0, keepdims=False)
+        ring = [(source, (source + shift) % lam_count) for source in range(lam_count)]
+        arrived.append(lax.ppermute(outgoing, "lam", ring))
+    got = jnp.stack(arrived)
 
     got_info = got[:, 0, :, 0, basis_count:].astype(jnp.float32)
     unscale = jnp.exp2(got_info[:, 0, block_count] - 13.0)

time: 108 us -> 129 us (1.19)
  starting transfers between devices: 24.4 us -> 33.3 us
  local copies, waits for them, and re-layouts: 28.1 us -> 36.6 us
  waiting for transfers between devices: 17.7 us -> 19.8 us
  other arithmetic: 16.2 us -> 18.2 us
    ppermute x0 -> x7, starting transfers between devices: none -> 15.6 us  [on_device(): arrived.append(lax.ppermute(outgoing, 'lam', ring))]
    ppermute x0 -> x7, waiting for transfers between devices: none -> 10.9 us  [on_device(): arrived.append(lax.ppermute(outgoing, 'lam', ring))]
    all_to_all x1 -> x0, waiting for transfers between devices: 8.79 us -> none  [on_device(): lax.all_to_all(payload, 'lam', split_axis=0, concat_axis=0, tiled=True)]
    all_to_all x1 -> x0, starting transfers between devices: 8.2 us -> none  [on_device(): lax.all_to_all(payload, 'lam', split_axis=0, concat_axis=0, tiled=True)]
    squeeze x0 -> x2, other arithmetic: none -> 4.01 us  [on_device(): lax.dynamic_index_in_dim(payload, (lam_here + shift) % lam_count, 0, keep...]
    unnamed x11 -> x23, local copies, waits for them, and re-layouts: 3.52 us -> 7.38 us
    reshape x1 -> x2, local copies, waits for them, and re-layouts: 1.57 us -> 5.2 us  [on_device(): (contrib * scale).astype(jnp.float16)]
    concatenate x1 -> x0, other arithmetic: 2.59 us -> none  [on_device(): payload = jnp.concatenate([payload, info], axis=4)]
  transfers between devices with their start and end apart: 3 -> 9, of which waited for: 2 -> 3; matrix products, arithmetic and copies ran while one was open for 37% -> 39% of each run, Pallas kernels for 0% -> 0%
where the time goes in v10:
time: 129 us; the launch traced here: 128 us
  local copies, waits for them, and re-layouts  36.6 us (28%)
  starting transfers between devices  33.3 us (26%)
  waiting for transfers between devices  19.8 us (15%)
  other arithmetic  18.2 us (14%)
  Pallas kernels  11.5 us (9%)
  matrix products  6.34 us (5%)
  between operations  2.25 us (2%)
    ppermute x7, starting transfers between devices, on_device(): arrived.append(lax.ppermute(outgoing, 'lam', ring))  15.6 us
    pallas_call x1, Pallas kernels, final_contract(): pl.pallas_call(contract_kernel, grid=(occ_share,), in_specs=[pl.BlockSpec...  11.5 us
    ppermute x7, waiting for transfers between devices, on_device(): arrived.append(lax.ppermute(outgoing, 'lam', ring))  10.9 us
    gather x1, local copies, waits for them, and re-layouts, on_device(): vir_rows = jnp.take(virtual_coef, both_index[1], axis=0)  9.86 us
    all_to_all x1, starting transfers between devices, on_device(): lax.all_to_all(mixed, 'pair', split_axis=2, concat_axis=1, tiled=True)  9.17 us
    all_to_all x1, waiting for transfers between devices, on_device(): lax.all_to_all(mixed, 'pair', split_axis=2, concat_axis=1, tiled=True)  8.9 us
    all_to_all x1, starting transfers between devices, on_device(): lax.all_to_all(index_copies, 'pair', split_axis=0, concat_axis=0, tiled=T...  8.59 us
    unnamed x23, local copies, waits for them, and re-layouts  7.38 us
  transfers between devices with their start and end apart: 9, of which 3 were waited for; matrix products, arithmetic and copies ran while one was open for 39% of the time, Pallas kernels for 0%

profile of v10, /device:TPU:1, one launch (start us, length us, event | category | flops | bytes accessed | tf_op | source)
XLA Modules:
  0.0 127.9 jit_solution(9687957622305020564)
XLA Ops:
  1.5 8.6 %all-to-all-start.1 = ((s32[32,1,128]{2,1,0:T(1,128)}), s32[32,1,128]{2,1,0:T(1,128)S(1)}, u32[]{:S(2)}, u32[]{:S(2)}) async-start(s32[32,1,128]{2,1,0:T(1,128)} %reshape.236), calls=%async_computation.1 | async-start | bytes 32768 | tf_op jit(solution)/shard_map/all_to_all | solution.py:58
  15.0 4.9 %abs_reduce_fusion = (f32[]{:T(128)}, f32[8,16,4,1024]{3,1,2,0:T(8,128)}) fusion(bf16[1,8,4,64,1024]{4,3,2,1,0:T(8,128)(2,1)} %param.12, bf16[8,64,16]{1,2,0:T(8,128)(2,1)S(1)} %gather_fusion, pred[8]{0:T(512)(128)(4,1)S(1)} %get-tuple-element.45, pred[8]{0:T(512)(128)(4,1)S(1)} %get-tuple-element.46), kind=kOutput, calls=%fused_computation.16 | convolution fusion | flops 68173824 | bytes 6307860 | tf_op jit(solution)/shard_map/tmj,tkms->jtks/dot_general | solution.py:70
  21.9 2.8 %fusion.4 = f16[16,8,4,1024]{3,0,2,1:T(8,128)(2,1)} fusion(f32[8,16,4,1024]{3,1,2,0:T(8,128)} %get-tuple-element.42, f32[]{:T(128)S(6)} %exp2.15), kind=kLoop, calls=%fused_computation.20 | loop fusion | flops 1048576 | bytes 3145732 | tf_op jit(solution)/shard_map/convert_element_type | solution.py:75
  24.7 2.4 %reshape.184 = f16[8,2,8,4,1024]{4,1,0,3,2:T(2,128)(2,1)} reshape(f16[16,8,4,1024]{3,0,2,1:T(8,128)(2,1)} %fusion.4) | data formatting | bytes 2097152 | tf_op jit(solution)/shard_map/reshape | solution.py:75
  27.1 2.8 %copy.20 = f16[8,2,8,4,1024]{4,2,0,3,1:T(8,128)(2,1)} copy(f16[8,2,8,4,1024]{4,1,0,3,2:T(2,128)(2,1)} %reshape.184) | data formatting | bytes 2097152 | tf_op jit(solution)/shard_map/reshape | solution.py:75
  30.1 1.8 %fusion.15 = (f16[2,8,4,1152]{3,1,2,0:T(8,128)(2,1)}, f16[2,8,4,1152]{3,1,2,0:T(8,128)(2,1)}) fusion(s32[]{:T(128)S(6)} %select_n.137, f16[8,2,8,4,128]{4,2,0,3,1:T(8,128)(2,1)S(1)} %broadcast_in_dim.64, f16[8,2,8,4,1024]{4,2,0,3,1:T(8,128)(2,1)} %copy.20, s32[]{:T(128)S(6)} %select_n.135), kind=kLoop, calls=%fused_computation.46 | loop fusion | flops 147456 | bytes 1474568 | tf_op jit(solution)/shard_map/jit(dynamic_index_in_dim)/squeeze | solution.py:91
  31.8 6.0 %collective-permute-start.5 = (f16[2,8,4,1152]{3,1,2,0:T(8,128)(2,1)}, f16[2,8,4,1152]{3,1,2,0:T(8,128)(2,1)}, u32[]{:S(2)}, u32[]{:S(2)}) collective-permute-start(f16[2,8,4,1152]{3,1,2,0:T(8,128)(2,1)} %get-tuple-element.37), channel_id=1, source_target_pairs={{0,6},{1,7},{2,0},{3,1},{4,2},{5,3},{6,4},{7,5},{8,14},{9,15},{10,... | collective-permute-start | bytes 442376 | tf_op jit(solution)/shard_map/ppermute | solution.py:93
  38.6 2.2 %fusion.21 = (f16[2,8,4,1152]{3,1,2,0:T(8,128)(2,1)}, f16[8,2,8,4,1152]{4,2,0,3,1:T(8,128)(2,1)}, f16[2,8,4,1152]{3,1,2,0:T(8,128)(2,1)}, f16[2,8,4,1152]{3,1,2,...) fusion(s32[]{:T(128)S(6)} %select_n.139, ...), kind=kLoop, calls=%fused_computation.52 | loop fusion | flops 442367 | bytes 2064408 | tf_op jit(solution)/shard_map/jit(dynamic_index_in_dim)/squeeze | solution.py:91
  41.3 1.2 collective-permute-start
  42.5 1.9 %collective-permute-start.1 = (f16[2,8,4,1152]{3,1,2,0:T(8,128)(2,1)}, f16[2,8,4,1152]{3,1,2,0:T(8,128)(2,1)}, u32[]{:S(2)}, u32[]{:S(2)}) collective-permute-start(f16[2,8,4,1152]{3,1,2,0:T(8,128)(2,1)} %get-tuple-element.34), channel_id=1, source_target_pairs={{0,2},{1,3},{2,4},{3,5},{4,6},{5,7},{6,0},{7,1},{8,10},{9,11},{10,... | collective-permute-start | bytes 442376 | tf_op jit(solution)/shard_map/ppermute | solution.py:93
  46.3 6.2 %gather_fusion.1 = bf16[2048,16]{1,0:T(8,128)(2,1)S(1)} fusion(bf16[1024,16]{1,0:T(8,128)(2,1)S(1)} %copy.24, s32[2048]{0:T(1024)S(1)} %get-tuple-element.44), kind=kCustom, calls=%fused_computation.1 | custom fusion | bytes 139264 | tf_op jit(solution)/shard_map/jit(_take)/gather | solution.py:114
  52.7 9.9 %gather_fusion.2 = bf16[2048,1280]{1,0:T(8,128)(2,1)} fusion(bf16[1024,1280]{1,0:T(8,128)(2,1)S(1)} %copy-done, s32[2048]{0:T(1024)S(1)} %get-tuple-element.43), kind=kCustom, calls=%fused_computation.2 | custom fusion | bytes 10493952 | tf_op jit(solution)/shard_map/jit(_take)/gather | solution.py:115
  62.6 5.5 %broadcast_select_fusion.vir_ref = bf16[2048,1280]{1,0:T(8,128)(2,1)} fusion(bf16[2048,1280]{1,0:T(8,128)(2,1)} %gather_fusion.2, pred[2048]{0:T(1024)(128)(4,1)S(1)} %compare_and_fusion), kind=kLoop, calls=%fused_computation.3 | loop fusion | flops 2621440 | bytes 10487808 | tf_op jit(solution)/shard_map/jit(_take)/select_n | solution.py:115
  68.0 2.2 %collective-permute-start.2 = (f16[2,8,4,1152]{3,1,2,0:T(8,128)(2,1)S(1)}, f16[2,8,4,1152]{3,1,2,0:T(8,128)(2,1)S(1)}, u32[]{:S(2)}, u32[]{:S(2)}) collective-permute-start(f16[2,8,4,1152]{3,1,2,0:T(8,128)(2,1)S(1)} %copy-done.3), channel_id=1, source_target_pairs={{0,3},{1,4},{2,5},{3,6},{4,7},{5,0},{6,1},{7,2},{8,11},{9,12},{10,... | collective-permute-start | bytes 442376 | tf_op jit(solution)/shard_map/ppermute | solution.py:93
  71.2 3.1 %collective-permute-start.3 = (f16[2,8,4,1152]{3,1,2,0:T(8,128)(2,1)S(1)}, f16[2,8,4,1152]{3,1,2,0:T(8,128)(2,1)S(1)}, u32[]{:S(2)}, u32[]{:S(2)}) collective-permute-start(f16[2,8,4,1152]{3,1,2,0:T(8,128)(2,1)S(1)} %copy-done.2), channel_id=1, source_target_pairs={{0,4},{1,5},{2,6},{3,7},{4,0},{5,1},{6,2},{7,3},{8,12},{9,13},{10,... | collective-permute-start | bytes 442376 | tf_op jit(solution)/shard_map/ppermute | solution.py:93
  75.2 5.7 %collective-permute-done.2 = f16[2,8,4,1152]{3,1,2,0:T(8,128)(2,1)S(1)} collective-permute-done((f16[2,8,4,1152]{3,1,2,0:T(8,128)(2,1)S(1)}, f16[2,8,4,1152]{3,1,2,0:T(8,128)(2,1)S(1)}, u32[]{:S(2)}, u32[]{:S(2)}) %collective-permute-start.2) | collective-permute-done | bytes 147488 | tf_op jit(solution)/shard_map/ppermute | solution.py:93
  81.0 5.1 %collective-permute-done.3 = f16[2,8,4,1152]{3,1,2,0:T(8,128)(2,1)S(1)} collective-permute-done((f16[2,8,4,1152]{3,1,2,0:T(8,128)(2,1)S(1)}, f16[2,8,4,1152]{3,1,2,0:T(8,128)(2,1)S(1)}, u32[]{:S(2)}, u32[]{:S(2)}) %collective-permute-start.3) | collective-permute-done | bytes 147488 | tf_op jit(solution)/shard_map/ppermute | solution.py:93
  91.9 1.3 reshape.185
  93.2 1.1 reshape.234
  94.3 9.2 %all-to-all-start = ((bf16[32,2,2560]{2,1,0:T(2,128)(2,1)}), bf16[32,2,2560]{2,1,0:T(2,128)(2,1)}, u32[]{:S(2)}, u32[]{:S(2)}) async-start(bf16[32,2,2560]{2,1,0:T(2,128)(2,1)} %reshape.234), calls=%async_computation | async-start | bytes 655360 | tf_op jit(solution)/shard_map/all_to_all | solution.py:110
  104.2 8.9 %all-to-all-done = bf16[32,2,2560]{2,1,0:T(2,128)(2,1)} async-done(((bf16[32,2,2560]{2,1,0:T(2,128)(2,1)}), bf16[32,2,2560]{2,1,0:T(2,128)(2,1)}, u32[]{:S(2)}, u32[]{:S(2)}) %all-to-all-start) | async-done | bytes 327712 | tf_op jit(solution)/shard_map/all_to_all | solution.py:110
  113.1 1.4 %reshape.235 = bf16[32,40,2,64]{3,2,1,0:T(2,128)(2,1)S(1)} reshape(bf16[32,2,2560]{2,1,0:T(2,128)(2,1)} %all-to-all-done) | data formatting | bytes 655360
  115.2 1.3 reshape.186
  116.4 11.5 %shard_map.82 = f32[2,40,20480]{2,1,0:T(8,128)} custom-call(bf16[2,40,2048]{2,1,0:T(8,128)(2,1)} %bitcast.102, f32[16,2048]{1,0:T(8,128)} %convert_bitcast_fusion.occ_ref, bf16[2048,1280]{1,0:T(8,128)(2,1)} %broadcast_select_fusion.vir_ref), custom_call_target="tpu_custom_call" | custom-call | tf_op jit(solution)/shard_map/pallas_call | solution.py:29
  (69 shorter events, 18.8 us)
Async XLA Ops:
  0.0 52.7 %copy-start = (bf16[1024,1280]{1,0:T(8,128)(2,1)S(1)}, bf16[1024,1280]{1,0:T(8,128)(2,1)}, u32[]{:S(2)}) copy-start(bf16[1024,1280]{1,0:T(8,128)(2,1)} %param.19) | copy-start | bytes 7864324
  1.5 43.0 %all-to-all-start.1 = ((s32[32,1,128]{2,1,0:T(1,128)}), s32[32,1,128]{2,1,0:T(1,128)S(1)}, u32[]{:S(2)}, u32[]{:S(2)}) async-start(s32[32,1,128]{2,1,0:T(1,128)} %reshape.236), calls=%async_computation.1 | async-start | bytes 32768 | tf_op jit(solution)/shard_map/all_to_all | solution.py:58
  15.0 5.5 %copy-start.5 = (s32[1,8]{1,0:T(1,128)S(1)}, s32[1,8]{1,0:T(1,128)}, u32[]{:S(2)}) copy-start(s32[1,8]{1,0:T(1,128)} %param.13) | copy-start | bytes 100
  31.8 12.5 %copy-start.4 = (bf16[1024,16]{0,1:T(8,128)(2,1)S(1)}, bf16[1024,16]{0,1:T(8,128)(2,1)}, u32[]{:S(2)}) copy-start(bf16[1024,16]{0,1:T(8,128)(2,1)} %param.18) | copy-start | bytes 98308
  31.8 55.3 %collective-permute-start.5 = (f16[2,8,4,1152]{3,1,2,0:T(8,128)(2,1)}, f16[2,8,4,1152]{3,1,2,0:T(8,128)(2,1)}, u32[]{:S(2)}, u32[]{:S(2)}) collective-permute-start(f16[2,8,4,1152]{3,1,2,0:T(8,128)(2,1)} %get-tuple-element.37), channel_id=1, source_target_pairs={{0,6},{1,7},{2,0},{3,1},{4,2},{5,3},{6,4},{7,5},{8,14},{9,15},{10,... | collective-permute-start | bytes 442376 | tf_op jit(solution)/shard_map/ppermute | solution.py:93
  37.9 48.3 %collective-permute-start.4 = (f16[2,8,4,1152]{3,1,2,0:T(8,128)(2,1)}, f16[2,8,4,1152]{3,1,2,0:T(8,128)(2,1)}, u32[]{:S(2)}, u32[]{:S(2)}) collective-permute-start(f16[2,8,4,1152]{3,1,2,0:T(8,128)(2,1)} %get-tuple-element.38), channel_id=1, source_target_pairs={{0,5},{1,6},{2,7},{3,0},{4,1},{5,2},{6,3},{7,4},{8,13},{9,14},{10,... | collective-permute-start | bytes 442376 | tf_op jit(solution)/shard_map/ppermute | solution.py:93
  40.8 47.2 %collective-permute-start.6 = (f16[2,8,4,1152]{3,1,2,0:T(8,128)(2,1)}, f16[2,8,4,1152]{3,1,2,0:T(8,128)(2,1)}, u32[]{:S(2)}, u32[]{:S(2)}) collective-permute-start(f16[2,8,4,1152]{3,1,2,0:T(8,128)(2,1)} %get-tuple-element.31), channel_id=1, source_target_pairs={{0,7},{1,0},{2,1},{3,2},{4,3},{5,4},{6,5},{7,6},{8,15},{9,8},{10,9... | collective-permute-start | bytes 442376 | tf_op jit(solution)/shard_map/ppermute | solution.py:93
  41.3 26.7 %collective-permute-start = (f16[2,8,4,1152]{3,1,2,0:T(8,128)(2,1)}, f16[2,8,4,1152]{3,1,2,0:T(8,128)(2,1)}, u32[]{:S(2)}, u32[]{:S(2)}) collective-permute-start(f16[2,8,4,1152]{3,1,2,0:T(8,128)(2,1)} %get-tuple-element.33), channel_id=1, source_target_pairs={{0,1},{1,2},{2,3},{3,4},{4,5},{5,6},{6,7},{7,0},{8,9},{9,10},{10,1... | collective-permute-start | bytes 442376 | tf_op jit(solution)/shard_map/ppermute | solution.py:93
  42.5 28.7 %collective-permute-start.1 = (f16[2,8,4,1152]{3,1,2,0:T(8,128)(2,1)}, f16[2,8,4,1152]{3,1,2,0:T(8,128)(2,1)}, u32[]{:S(2)}, u32[]{:S(2)}) collective-permute-start(f16[2,8,4,1152]{3,1,2,0:T(8,128)(2,1)} %get-tuple-element.34), channel_id=1, source_target_pairs={{0,2},{1,3},{2,4},{3,5},{4,6},{5,7},{6,0},{7,1},{8,10},{9,11},{10,... | collective-permute-start | bytes 442376 | tf_op jit(solution)/shard_map/ppermute | solution.py:93
  62.5 5.5 %copy-start.3 = (f16[2,8,4,1152]{3,1,2,0:T(8,128)(2,1)S(1)}, f16[2,8,4,1152]{3,1,2,0:T(8,128)(2,1)}, u32[]{:S(2)}) copy-start(f16[2,8,4,1152]{3,1,2,0:T(8,128)(2,1)} %get-tuple-element.35) | copy-start | bytes 442372
  62.5 7.7 %copy-start.1 = (f16[8,2,8,4,1152]{4,2,0,3,1:T(8,128)(2,1)S(1)}, f16[8,2,8,4,1152]{4,2,0,3,1:T(8,128)(2,1)}, u32[]{:S(2)}) copy-start(f16[8,2,8,4,1152]{4,2,0,3,1:T(8,128)(2,1)} %get-tuple-element.32) | copy-start | bytes 3538948
  62.6 8.6 %copy-start.2 = (f16[2,8,4,1152]{3,1,2,0:T(8,128)(2,1)S(1)}, f16[2,8,4,1152]{3,1,2,0:T(8,128)(2,1)}, u32[]{:S(2)}) copy-start(f16[2,8,4,1152]{3,1,2,0:T(8,128)(2,1)} %get-tuple-element.36) | copy-start | bytes 442372
  68.0 12.9 %collective-permute-start.2 = (f16[2,8,4,1152]{3,1,2,0:T(8,128)(2,1)S(1)}, f16[2,8,4,1152]{3,1,2,0:T(8,128)(2,1)S(1)}, u32[]{:S(2)}, u32[]{:S(2)}) collective-permute-start(f16[2,8,4,1152]{3,1,2,0:T(8,128)(2,1)S(1)} %copy-done.3), channel_id=1, source_target_pairs={{0,3},{1,4},{2,5},{3,6},{4,7},{5,0},{6,1},{7,2},{8,11},{9,12},{10,... | collective-permute-start | bytes 442376 | tf_op jit(solution)/shard_map/ppermute | solution.py:93
  71.2 14.9 %collective-permute-start.3 = (f16[2,8,4,1152]{3,1,2,0:T(8,128)(2,1)S(1)}, f16[2,8,4,1152]{3,1,2,0:T(8,128)(2,1)S(1)}, u32[]{:S(2)}, u32[]{:S(2)}) collective-permute-start(f16[2,8,4,1152]{3,1,2,0:T(8,128)(2,1)S(1)} %copy-done.2), channel_id=1, source_target_pairs={{0,4},{1,5},{2,6},{3,7},{4,0},{5,1},{6,2},{7,3},{8,12},{9,13},{10,... | collective-permute-start | bytes 442376 | tf_op jit(solution)/shard_map/ppermute | solution.py:93
  94.3 18.8 %all-to-all-start = ((bf16[32,2,2560]{2,1,0:T(2,128)(2,1)}), bf16[32,2,2560]{2,1,0:T(2,128)(2,1)}, u32[]{:S(2)}, u32[]{:S(2)}) async-start(bf16[32,2,2560]{2,1,0:T(2,128)(2,1)} %reshape.234), calls=%async_computation | async-start | bytes 655360 | tf_op jit(solution)/shard_map/all_to_all | solution.py:110

commit v11 on v9

--- a/solution.py
+++ b/solution.py
@@ -11,11 +11,12 @@
     occ_total = occ_ref.shape[0]
     vir_total = vir_ref.shape[1]
     mixed_block = mixed_ref[0].astype(jnp.float32)
-    for i in range(occ_total):
-        stack_ref[i * vir_share : (i + 1) * vir_share, :] = mixed_block * occ_ref[i : i + 1, :]
-    product = jnp.dot(
-        stack_ref[...].astype(jnp.bfloat16), vir_ref[...], preferred_element_type=jnp.float32
-    )
+    for i in range(0, occ_total, 2):
+        pair_rows = jnp.concatenate(
+            [mixed_block * occ_ref[i : i + 1, :], mixed_block * occ_ref[i + 1 : i + 2, :]], axis=0
+        )
+        stack_ref[i * vir_share : (i + 2) * vir_share, :] = pair_rows.astype(jnp.bfloat16)
+    product = jnp.dot(stack_ref[...], vir_ref[...], preferred_element_type=jnp.float32)
     for i in range(occ_total):
         out_ref[0, :, i * vir_total : (i + 1) * vir_total] = product[
             i * vir_share : (i + 1) * vir_share, :
@@ -36,7 +37,7 @@
         ],
         out_specs=pl.BlockSpec((1, vir_share, occ_total * vir_total), lambda n: (n, 0, 0)),
         out_shape=jax.ShapeDtypeStruct((occ_share, vir_share, occ_total * vir_total), jnp.float32),
-        scratch_shapes=[pltpu.VMEM((occ_total * vir_share, total_rows), jnp.float32)],
+        scratch_shapes=[pltpu.VMEM((occ_total * vir_share, total_rows), jnp.bfloat16)],
         interpret=interpret,
     )(mixed_t, occ_t, vir_rows)
 

time: 108 us -> 108 us (level)
  no operation moved by 1% of the time
where the time goes in v11:
time: 108 us
  local copies, waits for them, and re-layouts  28.1 us (26%)
  starting transfers between devices  24.4 us (23%)
  waiting for transfers between devices  17.7 us (16%)
  other arithmetic  16.2 us (15%)
  Pallas kernels  11.5 us (11%)
  matrix products  7.62 us (7%)
  between operations  2.24 us (2%)
    pallas_call x1, Pallas kernels, final_contract(): pl.pallas_call(contract_kernel, grid=(occ_share,), in_specs=[pl.BlockSpec...  11.5 us
    gather x1, local copies, waits for them, and re-layouts, on_device(): vir_rows = jnp.take(virtual_coef, both_index[1], axis=0)  9.85 us
    all_to_all x1, waiting for transfers between devices, on_device(): lax.all_to_all(mixed, 'pair', split_axis=2, concat_axis=1, tiled=True)  8.92 us
    all_to_all x1, waiting for transfers between devices, on_device(): lax.all_to_all(payload, 'lam', split_axis=0, concat_axis=0, tiled=True)  8.79 us
    all_to_all x1, starting transfers between devices, on_device(): lax.all_to_all(index_copies, 'pair', split_axis=0, concat_axis=0, tiled=T...  8.59 us
    all_to_all x1, starting transfers between devices, on_device(): lax.all_to_all(payload, 'lam', split_axis=0, concat_axis=0, tiled=True)  8.2 us
    all_to_all x1, starting transfers between devices, on_device(): lax.all_to_all(mixed, 'pair', split_axis=2, concat_axis=1, tiled=True)  7.6 us
    gather x2, local copies, waits for them, and re-layouts, on_device(): occ_rows = jnp.take(occupied_coef, both_index[0], axis=0)  6.36 us
  transfers between devices with their start and end apart: 3, of which 2 were waited for; matrix products, arithmetic and copies ran while one was open for 37% of the time, Pallas kernels for 0%

profile of v11, /device:TPU:1, one launch (start us, length us, event | category | flops | bytes accessed | tf_op | source)
XLA Modules:
  0.0 107.8 jit_solution(5113812566268063783)
XLA Ops:
  0.0 0.8 pad_add_fusion
  0.8 0.7 reshape.236
  1.5 8.6 %all-to-all-start.2 = ((s32[32,1,128]{2,1,0:T(1,128)}), s32[32,1,128]{2,1,0:T(1,128)S(1)}, u32[]{:S(2)}, u32[]{:S(2)}) async-start(s32[32,1,128]{2,1,0:T(1,128)} %reshape.236), calls=%async_computation.2 | async-start | bytes 32768 | tf_op jit(solution)/shard_map/all_to_all | solution.py:59
  13.4 0.9 reshape.183
  14.9 4.9 %abs_reduce_fusion = (f32[]{:T(128)}, f32[8,16,4,1024]{3,1,2,0:T(8,128)}) fusion(bf16[1,8,4,64,1024]{4,3,2,1,0:T(8,128)(2,1)} %param.12, bf16[8,64,16]{1,2,0:T(8,128)(2,1)S(1)} %gather_fusion, pred[8]{0:T(512)(128)(4,1)S(1)} %get-tuple-element.35, pred[8]{0:T(512)(128)(4,1)S(1)} %get-tuple-element.36), kind=kOutput, calls=%fused_computation.8 | convolution fusion | flops 68173824 | bytes 6307860 | tf_op jit(solution)/shard_map/tmj,tkms->jtks/dot_general | solution.py:71
  21.8 1.9 %fusion.4 = f16[16,8,4,1024]{3,0,2,1:T(8,128)(2,1)S(1)} fusion(f32[8,16,4,1024]{3,1,2,0:T(8,128)} %get-tuple-element.34, f32[]{:T(128)S(6)} %exp2.15), kind=kLoop, calls=%fused_computation.13 | loop fusion | flops 1048576 | bytes 3145732 | tf_op jit(solution)/shard_map/convert_element_type | solution.py:76
  23.7 1.6 %copy.37 = f16[16,8,4,1024]{3,1,2,0:T(8,128)(2,1)} copy(f16[16,8,4,1024]{3,0,2,1:T(8,128)(2,1)S(1)} %fusion.4) | data formatting | bytes 2097152 | tf_op jit(solution)/shard_map/reshape | solution.py:76
  25.4 2.6 %pad_maximum_fusion = f16[8,2,8,4,1152]{4,2,3,1,0:T(8,128)(2,1)} fusion(f16[8,2,8,4,128]{4,2,3,1,0:T(8,128)(2,1)S(1)} %broadcast_in_dim.64, f16[8,2,8,4,1024]{4,2,3,1,0:T(8,128)(2,1)} %bitcast.74), kind=kLoop, calls=%fused_computation.11 | loop fusion | flops 589824 | bytes 2359296 | tf_op jit(solution)/shard_map/concatenate | solution.py:87
  28.2 8.2 %all-to-all-start = ((f16[8,2,8,4,1152]{4,2,3,1,0:T(8,128)(2,1)}), f16[8,2,8,4,1152]{4,2,3,1,0:T(8,128)(2,1)}, u32[]{:S(2)}, u32[]{:S(2)}) async-start(f16[8,2,8,4,1152]{4,2,3,1,0:T(8,128)(2,1)} %pad_maximum_fusion), calls=%async_computation | async-start | bytes 2359296 | tf_op jit(solution)/shard_map/all_to_all | solution.py:89
  36.9 0.7 reduce.31
  38.1 6.2 %gather_fusion.1 = bf16[2048,16]{1,0:T(8,128)(2,1)S(1)} fusion(bf16[1024,16]{1,0:T(8,128)(2,1)S(1)} %copy.32, s32[2048]{0:T(1024)S(1)} %broadcast_clamp_fusion.1), kind=kCustom, calls=%fused_computation.1 | custom fusion | bytes 139264 | tf_op jit(solution)/shard_map/jit(_take)/gather | solution.py:109
  44.5 9.9 %gather_fusion.2 = bf16[2048,1280]{1,0:T(8,128)(2,1)} fusion(bf16[1024,1280]{1,0:T(8,128)(2,1)S(1)} %copy-done, s32[2048]{0:T(1024)S(1)} %broadcast_clamp_fusion), kind=kCustom, calls=%fused_computation.2 | custom fusion | bytes 10493952 | tf_op jit(solution)/shard_map/jit(_take)/gather | solution.py:110
  54.4 5.4 %broadcast_select_fusion.vir_ref = bf16[2048,1280]{1,0:T(8,128)(2,1)} fusion(bf16[2048,1280]{1,0:T(8,128)(2,1)} %gather_fusion.2, pred[2048]{0:T(1024)(128)(4,1)S(1)} %compare_and_fusion), kind=kLoop, calls=%fused_computation.3 | loop fusion | flops 2621440 | bytes 10487808 | tf_op jit(solution)/shard_map/jit(_take)/select_n | solution.py:110
  59.7 8.8 %all-to-all-done = f16[8,2,8,4,1152]{4,2,3,1,0:T(8,128)(2,1)} async-done(((f16[8,2,8,4,1152]{4,2,3,1,0:T(8,128)(2,1)}), f16[8,2,8,4,1152]{4,2,3,1,0:T(8,128)(2,1)}, u32[]{:S(2)}, u32[]{:S(2)}) %all-to-all-start) | async-done | bytes 1179680 | tf_op jit(solution)/shard_map/all_to_all | solution.py:89
  68.5 0.7 fusion.13
  69.5 2.2 %fusion.3 = bf16[2,16,4,1024]{3,1,2,0:T(8,128)(2,1)S(1)} fusion(f16[8,2,8,4,1152]{4,2,3,1,0:T(8,128)(2,1)} %all-to-all-done, f32[8,8,128]{2,1,0:T(8,128)S(1)} %fusion.13, f32[8]{0:T(128)S(1)} %fusion.19), kind=kOutput, calls=%fused_computation.12 | convolution fusion | flops 100795392 | bytes 1343520 | tf_op jit(solution)/shard_map/ptg,pjtks->jgks/dot_general | solution.py:94
  72.5 0.9 copy.30
  73.4 1.3 %reshape.185 = bf16[2,64,32,40]{1,0,3,2:T(2,128)(2,1)S(1)} reshape(bf16[128,1280]{0,1:T(8,128)(2,1)} %copy.30) | data formatting | bytes 655360 | tf_op jit(solution)/shard_map/reshape | solution.py:104
  74.7 1.1 %reshape.234 = bf16[32,2,2560]{2,1,0:T(2,128)(2,1)} reshape(bf16[32,40,2,64]{3,2,1,0:T(2,128)(2,1)S(1)} %bitcast.75) | data formatting | bytes 655360
  75.8 7.6 %all-to-all-start.1 = ((bf16[32,2,2560]{2,1,0:T(2,128)(2,1)}), bf16[32,2,2560]{2,1,0:T(2,128)(2,1)}, u32[]{:S(2)}, u32[]{:S(2)}) async-start(bf16[32,2,2560]{2,1,0:T(2,128)(2,1)} %reshape.234), calls=%async_computation.1 | async-start | bytes 655360 | tf_op jit(solution)/shard_map/all_to_all | solution.py:105
  84.1 8.9 %all-to-all-done.1 = bf16[32,2,2560]{2,1,0:T(2,128)(2,1)} async-done(((bf16[32,2,2560]{2,1,0:T(2,128)(2,1)}), bf16[32,2,2560]{2,1,0:T(2,128)(2,1)}, u32[]{:S(2)}, u32[]{:S(2)}) %all-to-all-start.1) | async-done | bytes 327712 | tf_op jit(solution)/shard_map/all_to_all | solution.py:105
  93.0 1.4 %reshape.235 = bf16[32,40,2,64]{3,2,1,0:T(2,128)(2,1)S(1)} reshape(bf16[32,2,2560]{2,1,0:T(2,128)(2,1)} %all-to-all-done.1) | data formatting | bytes 655360
  95.1 1.3 %reshape.186 = bf16[2,2048,40]{1,2,0:T(8,128)(2,1)} reshape(bf16[2,32,64,1,40]{2,1,4,0,3:T(8,128)(2,1)S(1)} %copy.31) | data formatting | bytes 655360 | tf_op jit(solution)/shard_map/reshape | solution.py:107
  96.3 11.5 %shard_map.82 = f32[2,40,20480]{2,1,0:T(8,128)} custom-call(bf16[2,40,2048]{2,1,0:T(8,128)(2,1)} %bitcast.76, f32[16,2048]{1,0:T(8,128)} %convert_bitcast_fusion.occ_ref, bf16[2048,1280]{1,0:T(8,128)(2,1)} %broadcast_select_fusion.vir_ref), custom_call_target="tpu_custom_call" | custom-call | tf_op jit(solution)/shard_map/pallas_call | solution.py:30
  (43 shorter events, 7.7 us)
Async XLA Ops:
  0.0 44.5 %copy-start = (bf16[1024,1280]{1,0:T(8,128)(2,1)S(1)}, bf16[1024,1280]{1,0:T(8,128)(2,1)}, u32[]{:S(2)}) copy-start(bf16[1024,1280]{1,0:T(8,128)(2,1)} %param.19) | copy-start | bytes 7864324
  1.5 26.6 %all-to-all-start.2 = ((s32[32,1,128]{2,1,0:T(1,128)}), s32[32,1,128]{2,1,0:T(1,128)S(1)}, u32[]{:S(2)}, u32[]{:S(2)}) async-start(s32[32,1,128]{2,1,0:T(1,128)} %reshape.236), calls=%async_computation.2 | async-start | bytes 32768 | tf_op jit(solution)/shard_map/all_to_all | solution.py:59
  14.9 5.6 %copy-start.2 = (s32[1,8]{1,0:T(1,128)S(1)}, s32[1,8]{1,0:T(1,128)}, u32[]{:S(2)}) copy-start(s32[1,8]{1,0:T(1,128)} %param.13) | copy-start | bytes 100
  23.7 4.3 %copy-start.1 = (bf16[1024,16]{0,1:T(8,128)(2,1)S(1)}, bf16[1024,16]{0,1:T(8,128)(2,1)}, u32[]{:S(2)}) copy-start(bf16[1024,16]{0,1:T(8,128)(2,1)} %param.18) | copy-start | bytes 98308
  28.2 40.4 %all-to-all-start = ((f16[8,2,8,4,1152]{4,2,3,1,0:T(8,128)(2,1)}), f16[8,2,8,4,1152]{4,2,3,1,0:T(8,128)(2,1)}, u32[]{:S(2)}, u32[]{:S(2)}) async-start(f16[8,2,8,4,1152]{4,2,3,1,0:T(8,128)(2,1)} %pad_maximum_fusion), calls=%async_computation | async-start | bytes 2359296 | tf_op jit(solution)/shard_map/all_to_all | solution.py:89
  75.8 17.2 %all-to-all-start.1 = ((bf16[32,2,2560]{2,1,0:T(2,128)(2,1)}), bf16[32,2,2560]{2,1,0:T(2,128)(2,1)}, u32[]{:S(2)}, u32[]{:S(2)}) async-start(bf16[32,2,2560]{2,1,0:T(2,128)(2,1)} %reshape.234), calls=%async_computation.1 | async-start | bytes 655360 | tf_op jit(solution)/shard_map/all_to_all | solution.py:105

commit v12 on v9

--- a/solution.py
+++ b/solution.py
@@ -65,7 +65,7 @@
     lam_list = tile_lam[0]
     live = jnp.arange(slot_count) < tile_count[0, 0]
     occ_blocks = occupied_coef.reshape(basis_count // tile_depth, tile_depth, occ_total)
-    occ_slot = jnp.take(occ_blocks, lam_list, axis=0)
+    occ_slot = jnp.take(occ_blocks, lam_list, axis=0, mode="clip")
     occ_slot = jnp.where(live[:, None, None], occ_slot, jnp.zeros((), occ_slot.dtype))
     contrib = jnp.einsum("tmj,tkms->jtks", occ_slot, tile_data, preferred_element_type=jnp.float32)
 
@@ -105,8 +105,8 @@
     total_rows = received.shape[1]
     mixed_rows = received.reshape(occ_share, total_rows, vir_share)
 
-    occ_rows = jnp.take(occupied_coef, both_index[0], axis=0)
-    vir_rows = jnp.take(virtual_coef, both_index[1], axis=0)
+    occ_rows = jnp.take(occupied_coef, both_index[0], axis=0, mode="clip")
+    vir_rows = jnp.take(virtual_coef, both_index[1], axis=0, mode="clip")
     mixed_t = jnp.transpose(mixed_rows, (0, 2, 1))
     occ_t = jnp.transpose(occ_rows).astype(jnp.float32)
     return final_contract(mixed_t, occ_t, vir_rows)

time: 108 us -> 108 us (level)
  other arithmetic: 16.2 us -> 10.4 us
  waiting for transfers between devices: 17.7 us -> 23 us
    select_n x4 -> x0, other arithmetic: 6.05 us -> none  [the longest x2 5.38 us: on_device(): vir_rows = jnp.take(virtual_coef, both_index[1], axis=0)]
    all_to_all x1, waiting for transfers between devices: 8.79 us -> 14 us  [on_device(): lax.all_to_all(payload, 'lam', split_axis=0, concat_axis=0, tiled=True)]
  transfers between devices with their start and end apart: 3 -> 3, of which waited for: 2 -> 2; matrix products, arithmetic and copies ran while one was open for 37% -> 32% of each run, Pallas kernels for 0% -> 0%
where the time goes in v12:
time: 108 us; the launch traced here: 107 us
  local copies, waits for them, and re-layouts  28.1 us (26%)
  starting transfers between devices  24.4 us (23%)
  waiting for transfers between devices  23 us (21%)
  Pallas kernels  11.5 us (11%)
  other arithmetic  10.4 us (10%)
  matrix products  7.58 us (7%)
  between operations  2.13 us (2%)
    all_to_all x1, waiting for transfers between devices, on_device(): lax.all_to_all(payload, 'lam', split_axis=0, concat_axis=0, tiled=True)  14 us
    pallas_call x1, Pallas kernels, final_contract(): pl.pallas_call(contract_kernel, grid=(occ_share,), in_specs=[pl.BlockSpec...  11.5 us
    gather x1, local copies, waits for them, and re-layouts, on_device(): vir_rows = jnp.take(virtual_coef, both_index[1], axis=0, mode='clip')  9.9 us
    all_to_all x1, waiting for transfers between devices, on_device(): lax.all_to_all(mixed, 'pair', split_axis=2, concat_axis=1, tiled=True)  8.93 us
    all_to_all x1, starting transfers between devices, on_device(): lax.all_to_all(index_copies, 'pair', split_axis=0, concat_axis=0, tiled=T...  8.59 us
    all_to_all x1, starting transfers between devices, on_device(): lax.all_to_all(payload, 'lam', split_axis=0, concat_axis=0, tiled=True)  8.19 us
    all_to_all x1, starting transfers between devices, on_device(): lax.all_to_all(mixed, 'pair', split_axis=2, concat_axis=1, tiled=True)  7.6 us
    gather x2, local copies, waits for them, and re-layouts, on_device(): occ_rows = jnp.take(occupied_coef, both_index[0], axis=0, mode='clip')  6.36 us
  transfers between devices with their start and end apart: 3, of which 2 were waited for; matrix products, arithmetic and copies ran while one was open for 32% of the time, Pallas kernels for 0%

profile of v12, /device:TPU:1, one launch (start us, length us, event | category | flops | bytes accessed | tf_op | source)
XLA Modules:
  0.0 107.0 jit_solution(7034187431967513297)
XLA Ops:
  0.0 0.8 pad_add_fusion
  1.5 8.6 %all-to-all-start.2 = ((s32[32,1,128]{2,1,0:T(1,128)}), s32[32,1,128]{2,1,0:T(1,128)S(1)}, u32[]{:S(2)}, u32[]{:S(2)}) async-start(s32[32,1,128]{2,1,0:T(1,128)} %reshape.134), calls=%async_computation.2 | async-start | bytes 32768 | tf_op jit(solution)/shard_map/all_to_all | solution.py:58
  10.1 0.7 compare_reduce_fusion.1
  12.8 0.9 reshape.84
  14.3 4.9 %abs_reduce_fusion = (f32[]{:T(128)}, f32[8,16,4,1024]{3,1,2,0:T(8,128)}) fusion(bf16[1,8,4,64,1024]{4,3,2,1,0:T(8,128)(2,1)} %param.12, bf16[8,64,16]{1,2,0:T(8,128)(2,1)S(1)} %gather_fusion, pred[8]{0:T(512)(128)(4,1)S(1)} %iota_compare_fusion.1), kind=kOutput, calls=%fused_computation.7 | convolution fusion | flops 68165632 | bytes 6307852 | tf_op jit(solution)/shard_map/tmj,tkms->jtks/dot_general | solution.py:70
  19.9 0.8 convert_select_fusion
  21.2 1.9 %fusion.4 = f16[16,8,4,1024]{3,0,2,1:T(8,128)(2,1)S(1)} fusion(f32[8,16,4,1024]{3,1,2,0:T(8,128)} %get-tuple-element.32, f32[]{:T(128)S(6)} %exp2.15), kind=kLoop, calls=%fused_computation.12 | loop fusion | flops 1048576 | bytes 3145732 | tf_op jit(solution)/shard_map/convert_element_type | solution.py:75
  23.1 1.6 %copy.37 = f16[16,8,4,1024]{3,1,2,0:T(8,128)(2,1)} copy(f16[16,8,4,1024]{3,0,2,1:T(8,128)(2,1)S(1)} %fusion.4) | data formatting | bytes 2097152 | tf_op jit(solution)/shard_map/reshape | solution.py:75
  24.8 2.6 %pad_maximum_fusion = f16[8,2,8,4,1152]{4,2,3,1,0:T(8,128)(2,1)} fusion(f16[8,2,8,4,128]{4,2,3,1,0:T(8,128)(2,1)S(1)} %broadcast_in_dim.45, f16[8,2,8,4,1024]{4,2,3,1,0:T(8,128)(2,1)} %bitcast.65), kind=kLoop, calls=%fused_computation.10 | loop fusion | flops 589824 | bytes 2359296 | tf_op jit(solution)/shard_map/concatenate | solution.py:86
  27.4 8.2 %all-to-all-start = ((f16[8,2,8,4,1152]{4,2,3,1,0:T(8,128)(2,1)}), f16[8,2,8,4,1152]{4,2,3,1,0:T(8,128)(2,1)}, u32[]{:S(2)}, u32[]{:S(2)}) async-start(f16[8,2,8,4,1152]{4,2,3,1,0:T(8,128)(2,1)} %pad_maximum_fusion), calls=%async_computation | async-start | bytes 2359296 | tf_op jit(solution)/shard_map/all_to_all | solution.py:88
  36.4 0.7 reduce.27
  37.4 6.2 %gather_fusion.1 = bf16[2048,16]{1,0:T(8,128)(2,1)S(1)} fusion(bf16[1024,16]{1,0:T(8,128)(2,1)S(1)} %copy.32, s32[2048]{0:T(1024)S(1)} %broadcast_clamp_fusion.1), kind=kCustom, calls=%fused_computation.1 | custom fusion | bytes 139264 | tf_op jit(solution)/shard_map/jit(_take)/gather | solution.py:108
  43.8 9.9 %gather_fusion.2 = bf16[2048,1280]{1,0:T(8,128)(2,1)} fusion(bf16[1024,1280]{1,0:T(8,128)(2,1)S(1)} %copy-done, s32[2048]{0:T(1024)S(1)} %broadcast_clamp_fusion), kind=kCustom, calls=%fused_computation.2 | custom fusion | bytes 10493952 | tf_op jit(solution)/shard_map/jit(_take)/gather | solution.py:109
  53.7 14.0 %all-to-all-done = f16[8,2,8,4,1152]{4,2,3,1,0:T(8,128)(2,1)} async-done(((f16[8,2,8,4,1152]{4,2,3,1,0:T(8,128)(2,1)}), f16[8,2,8,4,1152]{4,2,3,1,0:T(8,128)(2,1)}, u32[]{:S(2)}, u32[]{:S(2)}) %all-to-all-start) | async-done | bytes 1179680 | tf_op jit(solution)/shard_map/all_to_all | solution.py:88
  67.7 0.7 fusion.11
  68.7 2.2 %fusion.3 = bf16[2,16,4,1024]{3,1,2,0:T(8,128)(2,1)S(1)} fusion(f16[8,2,8,4,1152]{4,2,3,1,0:T(8,128)(2,1)} %all-to-all-done, f32[8,8,128]{2,1,0:T(8,128)S(1)} %fusion.11, f32[8]{0:T(128)S(1)} %fusion.16), kind=kOutput, calls=%fused_computation.11 | convolution fusion | flops 100795392 | bytes 1343520 | tf_op jit(solution)/shard_map/ptg,pjtks->jgks/dot_general | solution.py:93
  71.7 0.9 copy.30
  72.6 1.3 %reshape.86 = bf16[2,64,32,40]{1,0,3,2:T(2,128)(2,1)S(1)} reshape(bf16[128,1280]{0,1:T(8,128)(2,1)} %copy.30) | data formatting | bytes 655360 | tf_op jit(solution)/shard_map/reshape | solution.py:103
  73.9 1.1 %reshape.132 = bf16[32,2,2560]{2,1,0:T(2,128)(2,1)} reshape(bf16[32,40,2,64]{3,2,1,0:T(2,128)(2,1)S(1)} %bitcast.66) | data formatting | bytes 655360
  75.0 7.6 %all-to-all-start.1 = ((bf16[32,2,2560]{2,1,0:T(2,128)(2,1)}), bf16[32,2,2560]{2,1,0:T(2,128)(2,1)}, u32[]{:S(2)}, u32[]{:S(2)}) async-start(bf16[32,2,2560]{2,1,0:T(2,128)(2,1)} %reshape.132), calls=%async_computation.1 | async-start | bytes 655360 | tf_op jit(solution)/shard_map/all_to_all | solution.py:104
  83.3 8.9 %all-to-all-done.1 = bf16[32,2,2560]{2,1,0:T(2,128)(2,1)} async-done(((bf16[32,2,2560]{2,1,0:T(2,128)(2,1)}), bf16[32,2,2560]{2,1,0:T(2,128)(2,1)}, u32[]{:S(2)}, u32[]{:S(2)}) %all-to-all-start.1) | async-done | bytes 327712 | tf_op jit(solution)/shard_map/all_to_all | solution.py:104
  92.2 1.4 %reshape.133 = bf16[32,40,2,64]{3,2,1,0:T(2,128)(2,1)S(1)} reshape(bf16[32,2,2560]{2,1,0:T(2,128)(2,1)} %all-to-all-done.1) | data formatting | bytes 655360
  94.3 1.3 %reshape.87 = bf16[2,2048,40]{1,2,0:T(8,128)(2,1)} reshape(bf16[2,32,64,1,40]{2,1,4,0,3:T(8,128)(2,1)S(1)} %copy.31) | data formatting | bytes 655360 | tf_op jit(solution)/shard_map/reshape | solution.py:106
  95.5 11.5 %shard_map.82 = f32[2,40,20480]{2,1,0:T(8,128)} custom-call(bf16[2,40,2048]{2,1,0:T(8,128)(2,1)} %bitcast.67, f32[16,2048]{1,0:T(8,128)} %convert_bitcast_fusion.occ_ref, bf16[2048,1280]{1,0:T(8,128)(2,1)} %gather_fusion.2), custom_call_target="tpu_custom_call" | custom-call | tf_op jit(solution)/shard_map/pallas_call | solution.py:29
  (35 shorter events, 6.3 us)
Async XLA Ops:
  0.0 43.8 %copy-start = (bf16[1024,1280]{1,0:T(8,128)(2,1)S(1)}, bf16[1024,1280]{1,0:T(8,128)(2,1)}, u32[]{:S(2)}) copy-start(bf16[1024,1280]{1,0:T(8,128)(2,1)} %param.19) | copy-start | bytes 7864324
  1.5 25.8 %all-to-all-start.2 = ((s32[32,1,128]{2,1,0:T(1,128)}), s32[32,1,128]{2,1,0:T(1,128)S(1)}, u32[]{:S(2)}, u32[]{:S(2)}) async-start(s32[32,1,128]{2,1,0:T(1,128)} %reshape.134), calls=%async_computation.2 | async-start | bytes 32768 | tf_op jit(solution)/shard_map/all_to_all | solution.py:58
  14.3 5.6 %copy-start.2 = (s32[1,8]{1,0:T(1,128)S(1)}, s32[1,8]{1,0:T(1,128)}, u32[]{:S(2)}) copy-start(s32[1,8]{1,0:T(1,128)} %param.13) | copy-start | bytes 100
  24.7 10.9 %copy-start.1 = (bf16[1024,16]{0,1:T(8,128)(2,1)S(1)}, bf16[1024,16]{0,1:T(8,128)(2,1)}, u32[]{:S(2)}) copy-start(bf16[1024,16]{0,1:T(8,128)(2,1)} %param.18) | copy-start | bytes 98308
  27.4 40.3 %all-to-all-start = ((f16[8,2,8,4,1152]{4,2,3,1,0:T(8,128)(2,1)}), f16[8,2,8,4,1152]{4,2,3,1,0:T(8,128)(2,1)}, u32[]{:S(2)}, u32[]{:S(2)}) async-start(f16[8,2,8,4,1152]{4,2,3,1,0:T(8,128)(2,1)} %pad_maximum_fusion), calls=%async_computation | async-start | bytes 2359296 | tf_op jit(solution)/shard_map/all_to_all | solution.py:88
  75.0 17.2 %all-to-all-start.1 = ((bf16[32,2,2560]{2,1,0:T(2,128)(2,1)}), bf16[32,2,2560]{2,1,0:T(2,128)(2,1)}, u32[]{:S(2)}, u32[]{:S(2)}) async-start(bf16[32,2,2560]{2,1,0:T(2,128)(2,1)} %reshape.132), calls=%async_computation.1 | async-start | bytes 655360 | tf_op jit(solution)/shard_map/all_to_all | solution.py:104

commit v13 on v12

--- a/solution.py
+++ b/solution.py
@@ -90,24 +90,24 @@
     got_info = got[:, 0, :, 0, basis_count:].astype(jnp.float32)
     unscale = jnp.exp2(got_info[:, 0, block_count] - 13.0)
     got_hit = got_info[:, :, :block_count] * unscale[:, None, None]
+    got_data = got[..., :basis_count].astype(jnp.float32)
+    data_high = got_data.astype(jnp.bfloat16)
+    data_low = (got_data - data_high.astype(jnp.float32)).astype(jnp.bfloat16)
+    hit_weight = got_hit.astype(jnp.bfloat16)
     own_half = jnp.einsum(
-        "ptg,pjtks->jgks",
-        got_hit,
-        got[..., :basis_count].astype(jnp.float32),
-        precision=lax.Precision.HIGHEST,
-        preferred_element_type=jnp.float32,
-    ).reshape(occ_share, rows_here, basis_count)
+        "ptg,pjtks->jgks", hit_weight, data_high, preferred_element_type=jnp.float32
+    ) + jnp.einsum("ptg,pjtks->jgks", hit_weight, data_low, preferred_element_type=jnp.float32)
 
-    half_low = own_half.astype(jnp.bfloat16).reshape(occ_share * rows_here, basis_count)
-    mixed = jnp.dot(half_low, virtual_coef, preferred_element_type=jnp.float32)
-    mixed = mixed.astype(jnp.bfloat16).reshape(occ_share, rows_here, pair_count, vir_share)
-    received = lax.all_to_all(mixed, "pair", split_axis=2, concat_axis=1, tiled=True)
-    total_rows = received.shape[1]
-    mixed_rows = received.reshape(occ_share, total_rows, vir_share)
+    half_low = own_half.astype(jnp.bfloat16).reshape(occ_share, rows_here, basis_count)
+    mixed = jnp.einsum("sn,jrs->njr", virtual_coef, half_low, preferred_element_type=jnp.float32)
+    mixed = mixed.astype(jnp.bfloat16).reshape(pair_count, vir_share, occ_share, rows_here)
+    received = lax.all_to_all(mixed, "pair", split_axis=0, concat_axis=0, tiled=True)
+    mixed_t = jnp.transpose(received, (2, 1, 0, 3)).reshape(
+        occ_share, vir_share, pair_count * rows_here
+    )
 
     occ_rows = jnp.take(occupied_coef, both_index[0], axis=0, mode="clip")
     vir_rows = jnp.take(virtual_coef, both_index[1], axis=0, mode="clip")
-    mixed_t = jnp.transpose(mixed_rows, (0, 2, 1))
     occ_t = jnp.transpose(occ_rows).astype(jnp.float32)
     return final_contract(mixed_t, occ_t, vir_rows)
 

time: 108 us -> 110 us (1.019)
  matrix products: 7.58 us -> 9.41 us
    dot_general x2 -> x3, matrix products: 2.72 us -> 4.54 us  [the longest x1 1.67 us: on_device(): jnp.einsum('ptg,pjtks->jgks', hit_weight, data_low, preferred_element_typ...]
    unnamed x11, local copies, waits for them, and re-layouts: 3.52 us -> 4.62 us
  transfers between devices with their start and end apart: 3 -> 3, of which waited for: 2 -> 2; matrix products, arithmetic and copies ran while one was open for 32% -> 31% of each run, Pallas kernels for 0% -> 0%
where the time goes in v13:
time: 110 us
  local copies, waits for them, and re-layouts  28.8 us (26%)
  starting transfers between devices  24.4 us (22%)
  waiting for transfers between devices  23 us (21%)
  Pallas kernels  11.5 us (10%)
  other arithmetic  10.4 us (9%)
  matrix products  9.41 us (9%)
  between operations  2.13 us (2%)
    all_to_all x1, waiting for transfers between devices, on_device(): lax.all_to_all(payload, 'lam', split_axis=0, concat_axis=0, tiled=True)  14 us
    pallas_call x1, Pallas kernels, final_contract(): pl.pallas_call(contract_kernel, grid=(occ_share,), in_specs=[pl.BlockSpec...  11.5 us
    gather x1, local copies, waits for them, and re-layouts, on_device(): vir_rows = jnp.take(virtual_coef, both_index[1], axis=0, mode='clip')  9.9 us
    all_to_all x1, waiting for transfers between devices, on_device(): lax.all_to_all(mixed, 'pair', split_axis=0, concat_axis=0, tiled=True)  8.93 us
    all_to_all x1, starting transfers between devices, on_device(): lax.all_to_all(index_copies, 'pair', split_axis=0, concat_axis=0, tiled=T...  8.59 us
    all_to_all x1, starting transfers between devices, on_device(): lax.all_to_all(payload, 'lam', split_axis=0, concat_axis=0, tiled=True)  8.19 us
    all_to_all x1, starting transfers between devices, on_device(): lax.all_to_all(mixed, 'pair', split_axis=0, concat_axis=0, tiled=True)  7.6 us
    gather x2, local copies, waits for them, and re-layouts, on_device(): occ_rows = jnp.take(occupied_coef, both_index[0], axis=0, mode='clip')  6.36 us
  transfers between devices with their start and end apart: 3, of which 2 were waited for; matrix products, arithmetic and copies ran while one was open for 31% of the time, Pallas kernels for 0%

profile of v13, /device:TPU:1, one launch (start us, length us, event | category | flops | bytes accessed | tf_op | source)
XLA Modules:
  0.0 109.6 jit_solution(1837128239368239371)
XLA Ops:
  0.0 0.8 pad_add_fusion
  1.5 8.6 %all-to-all-start.2 = ((s32[32,1,128]{2,1,0:T(1,128)}), s32[32,1,128]{2,1,0:T(1,128)S(1)}, u32[]{:S(2)}, u32[]{:S(2)}) async-start(s32[32,1,128]{2,1,0:T(1,128)} %reshape.135), calls=%async_computation.2 | async-start | bytes 32768 | tf_op jit(solution)/shard_map/all_to_all | solution.py:58
  12.8 0.9 reshape.82
  14.3 4.9 %abs_reduce_fusion = (f32[]{:T(128)}, f32[8,16,4,1024]{3,1,2,0:T(8,128)}) fusion(bf16[1,8,4,64,1024]{4,3,2,1,0:T(8,128)(2,1)} %param.12, bf16[8,64,16]{1,2,0:T(8,128)(2,1)S(1)} %gather_fusion, pred[8]{0:T(512)(128)(4,1)S(1)} %iota_compare_fusion.1), kind=kOutput, calls=%fused_computation.13 | convolution fusion | flops 68165632 | bytes 6307852 | tf_op jit(solution)/shard_map/tmj,tkms->jtks/dot_general | solution.py:70
  19.9 0.8 convert_select_fusion
  21.2 1.9 %fusion.14 = f16[16,8,4,1024]{3,0,2,1:T(8,128)(2,1)S(1)} fusion(f32[8,16,4,1024]{3,1,2,0:T(8,128)} %get-tuple-element.32, f32[]{:T(128)S(6)} %exp2.15), kind=kLoop, calls=%fused_computation.20 | loop fusion | flops 1048576 | bytes 3145732 | tf_op jit(solution)/shard_map/convert_element_type | solution.py:75
  23.1 1.6 %copy.42 = f16[16,8,4,1024]{3,1,2,0:T(8,128)(2,1)} copy(f16[16,8,4,1024]{3,0,2,1:T(8,128)(2,1)S(1)} %fusion.14) | data formatting | bytes 2097152 | tf_op jit(solution)/shard_map/reshape | solution.py:75
  24.8 2.6 %pad_maximum_fusion = f16[8,2,8,4,1152]{4,2,3,1,0:T(8,128)(2,1)} fusion(f16[8,2,8,4,128]{4,2,3,1,0:T(8,128)(2,1)S(1)} %broadcast_in_dim.45, f16[8,2,8,4,1024]{4,2,3,1,0:T(8,128)(2,1)} %bitcast.71), kind=kLoop, calls=%fused_computation.18 | loop fusion | flops 589824 | bytes 2359296 | tf_op jit(solution)/shard_map/concatenate | solution.py:86
  27.4 8.2 %all-to-all-start = ((f16[8,2,8,4,1152]{4,2,3,1,0:T(8,128)(2,1)}), f16[8,2,8,4,1152]{4,2,3,1,0:T(8,128)(2,1)}, u32[]{:S(2)}, u32[]{:S(2)}) async-start(f16[8,2,8,4,1152]{4,2,3,1,0:T(8,128)(2,1)} %pad_maximum_fusion), calls=%async_computation | async-start | bytes 2359296 | tf_op jit(solution)/shard_map/all_to_all | solution.py:88
  36.4 0.7 reduce.27
  37.4 6.2 %gather_fusion.1 = bf16[2048,16]{1,0:T(8,128)(2,1)S(1)} fusion(bf16[1024,16]{1,0:T(8,128)(2,1)S(1)} %copy.36, s32[2048]{0:T(1024)S(1)} %broadcast_clamp_fusion.1), kind=kCustom, calls=%fused_computation.1 | custom fusion | bytes 139264 | tf_op jit(solution)/shard_map/jit(_take)/gather | solution.py:109
  43.8 9.9 %gather_fusion.2 = bf16[2048,1280]{1,0:T(8,128)(2,1)} fusion(bf16[1024,1280]{1,0:T(8,128)(2,1)S(1)} %copy-done, s32[2048]{0:T(1024)S(1)} %broadcast_clamp_fusion), kind=kCustom, calls=%fused_computation.2 | custom fusion | bytes 10493952 | tf_op jit(solution)/shard_map/jit(_take)/gather | solution.py:110
  53.7 14.0 %all-to-all-done = f16[8,2,8,4,1152]{4,2,3,1,0:T(8,128)(2,1)} async-done(((f16[8,2,8,4,1152]{4,2,3,1,0:T(8,128)(2,1)}), f16[8,2,8,4,1152]{4,2,3,1,0:T(8,128)(2,1)}, u32[]{:S(2)}, u32[]{:S(2)}) %all-to-all-start) | async-done | bytes 1179680 | tf_op jit(solution)/shard_map/all_to_all | solution.py:88
  68.7 1.7 %convolution_bitcast_fusion = f32[2,4,1024,16]{2,3,1,0:T(8,128)S(1)} fusion(f32[8,8,128]{2,1,0:T(8,128)S(1)} %fusion.24, f32[8]{0:T(128)S(1)} %fusion.28, f16[8,2,8,4,1152]{4,2,3,1,0:T(8,128)(2,1)} %all-to-all-done), kind=kOutput, calls=%fused_computation.14 | convolution fusion | flops 19400704 | bytes 1605664 | tf_op jit(solution)/shard_map/ptg,pjtks->jgks/dot_general | solution.py:99
  70.4 1.6 %fusion.13 = bf16[2,16,4,1024]{3,1,2,0:T(8,128)(2,1)S(1)} fusion(f32[2,4,1024,16]{2,3,1,0:T(8,128)S(1)} %convolution_bitcast_fusion, f32[8,8,128]{2,1,0:T(8,128)S(1)} %fusion.24, f32[8]{0:T(128)S(1)} %fusion.28, f16[8,2,8,4,1152]{4,2,3,1,0:T(8,128)(2,1)} %all-to-all-done), kind=kOutput, calls=%fused_computation.19 | convolution fusion | flops 18089984 | bytes 1867808 | tf_op jit(solution)/shard_map/ptg,pjtks->jgks/dot_general | solution.py:97
  72.3 1.2 %fusion.7 = bf16[1280,2,64]{0,2,1:T(8,128)(2,1)} fusion(bf16[1024,1280]{1,0:T(8,128)(2,1)S(1)} %copy-done, bf16[2,64,1024]{2,0,1:T(2,128)(2,1)S(1)} %bitcast.74), kind=kOutput, calls=%fused_computation.10 | convolution fusion | flops 335708160 | bytes 3211264 | tf_op jit(solution)/shard_map/sn,jrs->njr/dot_general | solution.py:102
  73.5 1.3 %copy.33 = bf16[1280,2,64]{2,0,1:T(8,128)(2,1)S(1)} copy(bf16[1280,2,64]{0,2,1:T(8,128)(2,1)} %fusion.7) | data formatting | bytes 655360 | tf_op jit(solution)/shard_map/convert_element_type | solution.py:103
  74.8 0.9 copy.55
  75.7 2.2 %reshape.133 = bf16[32,2,2560]{2,1,0:T(2,128)(2,1)} reshape(bf16[32,2,40,64]{3,2,1,0:T(8,128)(2,1)} %bitcast.73) | data formatting | bytes 655360
  77.9 7.6 %all-to-all-start.1 = ((bf16[32,2,2560]{2,1,0:T(2,128)(2,1)}), bf16[32,2,2560]{2,1,0:T(2,128)(2,1)}, u32[]{:S(2)}, u32[]{:S(2)}) async-start(bf16[32,2,2560]{2,1,0:T(2,128)(2,1)} %reshape.133), calls=%async_computation.1 | async-start | bytes 655360 | tf_op jit(solution)/shard_map/all_to_all | solution.py:104
  86.2 8.9 %all-to-all-done.1 = bf16[32,2,2560]{2,1,0:T(2,128)(2,1)} async-done(((bf16[32,2,2560]{2,1,0:T(2,128)(2,1)}), bf16[32,2,2560]{2,1,0:T(2,128)(2,1)}, u32[]{:S(2)}, u32[]{:S(2)}) %all-to-all-start.1) | async-done | bytes 327712 | tf_op jit(solution)/shard_map/all_to_all | solution.py:104
  95.2 1.4 %reshape.134 = bf16[32,2,40,64]{3,2,1,0:T(8,128)(2,1)S(1)} reshape(bf16[32,2,2560]{2,1,0:T(2,128)(2,1)} %all-to-all-done.1) | data formatting | bytes 655360
  96.8 1.3 %reshape.86.mixed_ref = bf16[2,40,2048]{2,1,0:T(8,128)(2,1)} reshape(bf16[2,40,32,64]{3,2,1,0:T(8,128)(2,1)S(1)} %copy.35) | data formatting | bytes 655360 | tf_op jit(solution)/shard_map/reshape | solution.py:105
  98.1 11.5 %shard_map.82 = f32[2,40,20480]{2,1,0:T(8,128)} custom-call(bf16[2,40,2048]{2,1,0:T(8,128)(2,1)} %reshape.86.mixed_ref, f32[16,2048]{1,0:T(8,128)} %convert_bitcast_fusion.occ_ref, bf16[2048,1280]{1,0:T(8,128)(2,1)} %gather_fusion.2), custom_call_target="tpu_custom_call" | custom-call | tf_op jit(solution)/shard_map/pallas_call | solution.py:29
  (35 shorter events, 6.8 us)
Async XLA Ops:
  0.0 43.8 %copy-start = (bf16[1024,1280]{1,0:T(8,128)(2,1)S(1)}, bf16[1024,1280]{1,0:T(8,128)(2,1)}, u32[]{:S(2)}) copy-start(bf16[1024,1280]{1,0:T(8,128)(2,1)} %param.19) | copy-start | bytes 7864324
  1.5 25.9 %all-to-all-start.2 = ((s32[32,1,128]{2,1,0:T(1,128)}), s32[32,1,128]{2,1,0:T(1,128)S(1)}, u32[]{:S(2)}, u32[]{:S(2)}) async-start(s32[32,1,128]{2,1,0:T(1,128)} %reshape.135), calls=%async_computation.2 | async-start | bytes 32768 | tf_op jit(solution)/shard_map/all_to_all | solution.py:58
  14.3 5.6 %copy-start.2 = (s32[1,8]{1,0:T(1,128)S(1)}, s32[1,8]{1,0:T(1,128)}, u32[]{:S(2)}) copy-start(s32[1,8]{1,0:T(1,128)} %param.13) | copy-start | bytes 100
  24.8 10.8 %copy-start.1 = (bf16[1024,16]{0,1:T(8,128)(2,1)S(1)}, bf16[1024,16]{0,1:T(8,128)(2,1)}, u32[]{:S(2)}) copy-start(bf16[1024,16]{0,1:T(8,128)(2,1)} %param.18) | copy-start | bytes 98308
  27.4 40.3 %all-to-all-start = ((f16[8,2,8,4,1152]{4,2,3,1,0:T(8,128)(2,1)}), f16[8,2,8,4,1152]{4,2,3,1,0:T(8,128)(2,1)}, u32[]{:S(2)}, u32[]{:S(2)}) async-start(f16[8,2,8,4,1152]{4,2,3,1,0:T(8,128)(2,1)} %pad_maximum_fusion), calls=%async_computation | async-start | bytes 2359296 | tf_op jit(solution)/shard_map/all_to_all | solution.py:88
  77.9 17.2 %all-to-all-start.1 = ((bf16[32,2,2560]{2,1,0:T(2,128)(2,1)}), bf16[32,2,2560]{2,1,0:T(2,128)(2,1)}, u32[]{:S(2)}, u32[]{:S(2)}) async-start(bf16[32,2,2560]{2,1,0:T(2,128)(2,1)} %reshape.133), calls=%async_computation.1 | async-start | bytes 655360 | tf_op jit(solution)/shard_map/all_to_all | solution.py:104

commit v14 on v12

--- a/solution.py
+++ b/solution.py
@@ -94,7 +94,7 @@
         "ptg,pjtks->jgks",
         got_hit,
         got[..., :basis_count].astype(jnp.float32),
-        precision=lax.Precision.HIGHEST,
+        precision=lax.Precision.HIGH,
         preferred_element_type=jnp.float32,
     ).reshape(occ_share, rows_here, basis_count)
 

time: 108 us -> 107 us (level)
  no operation moved by 1% of the time
where the time goes in v14:
time: 107 us
  local copies, waits for them, and re-layouts  28.1 us (26%)
  starting transfers between devices  24.4 us (23%)
  waiting for transfers between devices  23 us (21%)
  Pallas kernels  11.5 us (11%)
  other arithmetic  10.4 us (10%)
  matrix products  7.33 us (7%)
  between operations  2.13 us (2%)
    all_to_all x1, waiting for transfers between devices, on_device(): lax.all_to_all(payload, 'lam', split_axis=0, concat_axis=0, tiled=True)  14 us
    pallas_call x1, Pallas kernels, final_contract(): pl.pallas_call(contract_kernel, grid=(occ_share,), in_specs=[pl.BlockSpec...  11.5 us
    gather x1, local copies, waits for them, and re-layouts, on_device(): vir_rows = jnp.take(virtual_coef, both_index[1], axis=0, mode='clip')  9.9 us
    all_to_all x1, waiting for transfers between devices, on_device(): lax.all_to_all(mixed, 'pair', split_axis=2, concat_axis=1, tiled=True)  8.93 us
    all_to_all x1, starting transfers between devices, on_device(): lax.all_to_all(index_copies, 'pair', split_axis=0, concat_axis=0, tiled=T...  8.59 us
    all_to_all x1, starting transfers between devices, on_device(): lax.all_to_all(payload, 'lam', split_axis=0, concat_axis=0, tiled=True)  8.19 us
    all_to_all x1, starting transfers between devices, on_device(): lax.all_to_all(mixed, 'pair', split_axis=2, concat_axis=1, tiled=True)  7.6 us
    gather x2, local copies, waits for them, and re-layouts, on_device(): occ_rows = jnp.take(occupied_coef, both_index[0], axis=0, mode='clip')  6.36 us
  transfers between devices with their start and end apart: 3, of which 2 were waited for; matrix products, arithmetic and copies ran while one was open for 32% of the time, Pallas kernels for 0%

profile of v14, /device:TPU:1, one launch (start us, length us, event | category | flops | bytes accessed | tf_op | source)
XLA Modules:
  0.0 106.7 jit_solution(5917871964066886144)
XLA Ops:
  0.0 0.8 pad_add_fusion
  1.5 8.6 %all-to-all-start.2 = ((s32[32,1,128]{2,1,0:T(1,128)}), s32[32,1,128]{2,1,0:T(1,128)S(1)}, u32[]{:S(2)}, u32[]{:S(2)}) async-start(s32[32,1,128]{2,1,0:T(1,128)} %reshape.134), calls=%async_computation.2 | async-start | bytes 32768 | tf_op jit(solution)/shard_map/all_to_all | solution.py:58
  10.1 0.7 compare_reduce_fusion.1
  12.8 0.9 reshape.84
  14.3 4.9 %abs_reduce_fusion = (f32[]{:T(128)}, f32[8,16,4,1024]{3,1,2,0:T(8,128)}) fusion(bf16[1,8,4,64,1024]{4,3,2,1,0:T(8,128)(2,1)} %param.12, bf16[8,64,16]{1,2,0:T(8,128)(2,1)S(1)} %gather_fusion, pred[8]{0:T(512)(128)(4,1)S(1)} %iota_compare_fusion.1), kind=kOutput, calls=%fused_computation.7 | convolution fusion | flops 68165632 | bytes 6307852 | tf_op jit(solution)/shard_map/tmj,tkms->jtks/dot_general | solution.py:70
  19.9 0.8 convert_select_fusion
  21.2 1.9 %fusion.4 = f16[16,8,4,1024]{3,0,2,1:T(8,128)(2,1)S(1)} fusion(f32[8,16,4,1024]{3,1,2,0:T(8,128)} %get-tuple-element.32, f32[]{:T(128)S(6)} %exp2.15), kind=kLoop, calls=%fused_computation.12 | loop fusion | flops 1048576 | bytes 3145732 | tf_op jit(solution)/shard_map/convert_element_type | solution.py:75
  23.1 1.6 %copy.37 = f16[16,8,4,1024]{3,1,2,0:T(8,128)(2,1)} copy(f16[16,8,4,1024]{3,0,2,1:T(8,128)(2,1)S(1)} %fusion.4) | data formatting | bytes 2097152 | tf_op jit(solution)/shard_map/reshape | solution.py:75
  24.8 2.6 %pad_maximum_fusion = f16[8,2,8,4,1152]{4,2,3,1,0:T(8,128)(2,1)} fusion(f16[8,2,8,4,128]{4,2,3,1,0:T(8,128)(2,1)S(1)} %broadcast_in_dim.45, f16[8,2,8,4,1024]{4,2,3,1,0:T(8,128)(2,1)} %bitcast.65), kind=kLoop, calls=%fused_computation.10 | loop fusion | flops 589824 | bytes 2359296 | tf_op jit(solution)/shard_map/concatenate | solution.py:86
  27.4 8.2 %all-to-all-start = ((f16[8,2,8,4,1152]{4,2,3,1,0:T(8,128)(2,1)}), f16[8,2,8,4,1152]{4,2,3,1,0:T(8,128)(2,1)}, u32[]{:S(2)}, u32[]{:S(2)}) async-start(f16[8,2,8,4,1152]{4,2,3,1,0:T(8,128)(2,1)} %pad_maximum_fusion), calls=%async_computation | async-start | bytes 2359296 | tf_op jit(solution)/shard_map/all_to_all | solution.py:88
  36.4 0.7 reduce.27
  37.4 6.2 %gather_fusion.1 = bf16[2048,16]{1,0:T(8,128)(2,1)S(1)} fusion(bf16[1024,16]{1,0:T(8,128)(2,1)S(1)} %copy.32, s32[2048]{0:T(1024)S(1)} %broadcast_clamp_fusion.1), kind=kCustom, calls=%fused_computation.1 | custom fusion | bytes 139264 | tf_op jit(solution)/shard_map/jit(_take)/gather | solution.py:108
  43.8 9.9 %gather_fusion.2 = bf16[2048,1280]{1,0:T(8,128)(2,1)} fusion(bf16[1024,1280]{1,0:T(8,128)(2,1)S(1)} %copy-done, s32[2048]{0:T(1024)S(1)} %broadcast_clamp_fusion), kind=kCustom, calls=%fused_computation.2 | custom fusion | bytes 10493952 | tf_op jit(solution)/shard_map/jit(_take)/gather | solution.py:109
  53.7 14.0 %all-to-all-done = f16[8,2,8,4,1152]{4,2,3,1,0:T(8,128)(2,1)} async-done(((f16[8,2,8,4,1152]{4,2,3,1,0:T(8,128)(2,1)}), f16[8,2,8,4,1152]{4,2,3,1,0:T(8,128)(2,1)}, u32[]{:S(2)}, u32[]{:S(2)}) %all-to-all-start) | async-done | bytes 1179680 | tf_op jit(solution)/shard_map/all_to_all | solution.py:88
  67.7 0.7 fusion.11
  68.7 1.9 %fusion.3 = bf16[2,16,4,1024]{3,1,2,0:T(8,128)(2,1)S(1)} fusion(f16[8,2,8,4,1152]{4,2,3,1,0:T(8,128)(2,1)} %all-to-all-done, f32[8,8,128]{2,1,0:T(8,128)S(1)} %fusion.11, f32[8]{0:T(128)S(1)} %fusion.16), kind=kOutput, calls=%fused_computation.11 | convolution fusion | flops 50463744 | bytes 1343520 | tf_op jit(solution)/shard_map/ptg,pjtks->jgks/dot_general | solution.py:93
  71.4 0.9 copy.30
  72.3 1.3 %reshape.86 = bf16[2,64,32,40]{1,0,3,2:T(2,128)(2,1)S(1)} reshape(bf16[128,1280]{0,1:T(8,128)(2,1)} %copy.30) | data formatting | bytes 655360 | tf_op jit(solution)/shard_map/reshape | solution.py:103
  73.6 1.1 %reshape.132 = bf16[32,2,2560]{2,1,0:T(2,128)(2,1)} reshape(bf16[32,40,2,64]{3,2,1,0:T(2,128)(2,1)S(1)} %bitcast.66) | data formatting | bytes 655360
  74.7 7.6 %all-to-all-start.1 = ((bf16[32,2,2560]{2,1,0:T(2,128)(2,1)}), bf16[32,2,2560]{2,1,0:T(2,128)(2,1)}, u32[]{:S(2)}, u32[]{:S(2)}) async-start(bf16[32,2,2560]{2,1,0:T(2,128)(2,1)} %reshape.132), calls=%async_computation.1 | async-start | bytes 655360 | tf_op jit(solution)/shard_map/all_to_all | solution.py:104
  83.0 8.9 %all-to-all-done.1 = bf16[32,2,2560]{2,1,0:T(2,128)(2,1)} async-done(((bf16[32,2,2560]{2,1,0:T(2,128)(2,1)}), bf16[32,2,2560]{2,1,0:T(2,128)(2,1)}, u32[]{:S(2)}, u32[]{:S(2)}) %all-to-all-start.1) | async-done | bytes 327712 | tf_op jit(solution)/shard_map/all_to_all | solution.py:104
  91.9 1.4 %reshape.133 = bf16[32,40,2,64]{3,2,1,0:T(2,128)(2,1)S(1)} reshape(bf16[32,2,2560]{2,1,0:T(2,128)(2,1)} %all-to-all-done.1) | data formatting | bytes 655360
  94.0 1.3 %reshape.87 = bf16[2,2048,40]{1,2,0:T(8,128)(2,1)} reshape(bf16[2,32,64,1,40]{2,1,4,0,3:T(8,128)(2,1)S(1)} %copy.31) | data formatting | bytes 655360 | tf_op jit(solution)/shard_map/reshape | solution.py:106
  95.3 11.5 %shard_map.82 = f32[2,40,20480]{2,1,0:T(8,128)} custom-call(bf16[2,40,2048]{2,1,0:T(8,128)(2,1)} %bitcast.67, f32[16,2048]{1,0:T(8,128)} %convert_bitcast_fusion.occ_ref, bf16[2048,1280]{1,0:T(8,128)(2,1)} %gather_fusion.2), custom_call_target="tpu_custom_call" | custom-call | tf_op jit(solution)/shard_map/pallas_call | solution.py:29
  (35 shorter events, 6.3 us)
Async XLA Ops:
  0.0 43.8 %copy-start = (bf16[1024,1280]{1,0:T(8,128)(2,1)S(1)}, bf16[1024,1280]{1,0:T(8,128)(2,1)}, u32[]{:S(2)}) copy-start(bf16[1024,1280]{1,0:T(8,128)(2,1)} %param.19) | copy-start | bytes 7864324
  1.5 25.8 %all-to-all-start.2 = ((s32[32,1,128]{2,1,0:T(1,128)}), s32[32,1,128]{2,1,0:T(1,128)S(1)}, u32[]{:S(2)}, u32[]{:S(2)}) async-start(s32[32,1,128]{2,1,0:T(1,128)} %reshape.134), calls=%async_computation.2 | async-start | bytes 32768 | tf_op jit(solution)/shard_map/all_to_all | solution.py:58
  14.3 5.6 %copy-start.2 = (s32[1,8]{1,0:T(1,128)S(1)}, s32[1,8]{1,0:T(1,128)}, u32[]{:S(2)}) copy-start(s32[1,8]{1,0:T(1,128)} %param.13) | copy-start | bytes 100
  24.7 10.9 %copy-start.1 = (bf16[1024,16]{0,1:T(8,128)(2,1)S(1)}, bf16[1024,16]{0,1:T(8,128)(2,1)}, u32[]{:S(2)}) copy-start(bf16[1024,16]{0,1:T(8,128)(2,1)} %param.18) | copy-start | bytes 98308
  27.4 40.3 %all-to-all-start = ((f16[8,2,8,4,1152]{4,2,3,1,0:T(8,128)(2,1)}), f16[8,2,8,4,1152]{4,2,3,1,0:T(8,128)(2,1)}, u32[]{:S(2)}, u32[]{:S(2)}) async-start(f16[8,2,8,4,1152]{4,2,3,1,0:T(8,128)(2,1)} %pad_maximum_fusion), calls=%async_computation | async-start | bytes 2359296 | tf_op jit(solution)/shard_map/all_to_all | solution.py:88
  74.7 17.2 %all-to-all-start.1 = ((bf16[32,2,2560]{2,1,0:T(2,128)(2,1)}), bf16[32,2,2560]{2,1,0:T(2,128)(2,1)}, u32[]{:S(2)}, u32[]{:S(2)}) async-start(bf16[32,2,2560]{2,1,0:T(2,128)(2,1)} %reshape.132), calls=%async_computation.1 | async-start | bytes 655360 | tf_op jit(solution)/shard_map/all_to_all | solution.py:104

commit v15 on v14

--- a/solution.py
+++ b/solution.py
@@ -76,9 +76,14 @@
         lam_count, occ_share, slot_count, tile_rows, basis_count
     )
     hit = (pair_list[:, None] == jnp.arange(block_count)[None, :]) & live[:, None]
-    info = jnp.zeros((slot_count, 128), jnp.float32)
-    info = info.at[:, :block_count].set(hit.astype(jnp.float32))
-    info = info.at[:, block_count].set(exponent)
+    info = jnp.concatenate(
+        [
+            hit.astype(jnp.float32),
+            jnp.broadcast_to(exponent, (slot_count, 1)),
+            jnp.zeros((slot_count, 128 - block_count - 1), jnp.float32),
+        ],
+        axis=1,
+    )
     info = jnp.broadcast_to(
         info.astype(jnp.float16)[None, None, :, None, :],
         (lam_count, occ_share, slot_count, tile_rows, 128),

time: 107 us -> 103 us (0.963)
  other arithmetic: 10.4 us -> 7.77 us
    another operation x3 -> x1, other arithmetic: 2.11 us -> 0.73 us
    concatenate x1, other arithmetic: 2.55 us -> 1.33 us  [on_device(): payload = jnp.concatenate([payload, info], axis=4)]
    unnamed x11 -> x9, local copies, waits for them, and re-layouts: 3.52 us -> 3.51 us
  transfers between devices with their start and end apart: 3 -> 3, of which waited for: 2 -> 2; matrix products, arithmetic and copies ran while one was open for 32% -> 30% of each run, Pallas kernels for 0% -> 0%
where the time goes in v15:
time: 103 us
  local copies, waits for them, and re-layouts  27.2 us (26%)
  starting transfers between devices  24.4 us (24%)
  waiting for transfers between devices  23 us (22%)
  Pallas kernels  11.5 us (11%)
  other arithmetic  7.77 us (8%)
  matrix products  7.29 us (7%)
  between operations  1.49 us (1%)
    all_to_all x1, waiting for transfers between devices, on_device(): lax.all_to_all(payload, 'lam', split_axis=0, concat_axis=0, tiled=True)  14 us
    pallas_call x1, Pallas kernels, final_contract(): pl.pallas_call(contract_kernel, grid=(occ_share,), in_specs=[pl.BlockSpec...  11.5 us
    gather x1, local copies, waits for them, and re-layouts, on_device(): vir_rows = jnp.take(virtual_coef, both_index[1], axis=0, mode='clip')  9.9 us
    all_to_all x1, waiting for transfers between devices, on_device(): lax.all_to_all(mixed, 'pair', split_axis=2, concat_axis=1, tiled=True)  8.93 us
    all_to_all x1, starting transfers between devices, on_device(): lax.all_to_all(index_copies, 'pair', split_axis=0, concat_axis=0, tiled=T...  8.59 us
    all_to_all x1, starting transfers between devices, on_device(): lax.all_to_all(payload, 'lam', split_axis=0, concat_axis=0, tiled=True)  8.19 us
    all_to_all x1, starting transfers between devices, on_device(): lax.all_to_all(mixed, 'pair', split_axis=2, concat_axis=1, tiled=True)  7.6 us
    gather x2, local copies, waits for them, and re-layouts, on_device(): occ_rows = jnp.take(occupied_coef, both_index[0], axis=0, mode='clip')  6.36 us
  transfers between devices with their start and end apart: 3, of which 2 were waited for; matrix products, arithmetic and copies ran while one was open for 30% of the time, Pallas kernels for 0%

profile of v15, /device:TPU:1, one launch (start us, length us, event | category | flops | bytes accessed | tf_op | source)
XLA Modules:
  0.0 102.5 jit_solution(12835607258625860863)
XLA Ops:
  0.0 0.8 pad_add_fusion
  0.8 0.7 reshape.114
  1.5 8.6 %all-to-all-start.2 = ((s32[32,1,128]{2,1,0:T(1,128)}), s32[32,1,128]{2,1,0:T(1,128)S(1)}, u32[]{:S(2)}, u32[]{:S(2)}) async-start(s32[32,1,128]{2,1,0:T(1,128)} %reshape.114), calls=%async_computation.2 | async-start | bytes 32768 | tf_op jit(solution)/shard_map/all_to_all | solution.py:58
  11.5 0.9 reshape.63
  12.4 0.7 convert_convert_fusion
  13.7 4.8 %abs_reduce_fusion = (f32[]{:T(128)}, f32[8,16,4,1024]{3,1,2,0:T(8,128)}) fusion(bf16[1,8,4,64,1024]{4,3,2,1,0:T(8,128)(2,1)} %param.8, bf16[8,64,16]{1,2,0:T(8,128)(2,1)S(1)} %gather_fusion, pred[8]{0:T(512)(128)(4,1)S(1)} %iota_compare_fusion.1), kind=kOutput, calls=%fused_computation.7 | convolution fusion | flops 68165632 | bytes 6307852 | tf_op jit(solution)/shard_map/tmj,tkms->jtks/dot_general | solution.py:70
  19.1 1.9 %fusion.4 = f16[16,8,4,1024]{3,0,2,1:T(8,128)(2,1)S(1)} fusion(f32[8,16,4,1024]{3,1,2,0:T(8,128)} %get-tuple-element.8, f32[]{:T(128)S(6)} %exp2.15), kind=kLoop, calls=%fused_computation.12 | loop fusion | flops 1048576 | bytes 3145732 | tf_op jit(solution)/shard_map/convert_element_type | solution.py:75
  21.8 1.3 %pad_maximum_fusion = f16[8,2,8,4,1152]{4,2,3,1,0:T(8,128)(2,1)} fusion(f16[8,2,8,4,128]{4,2,3,1,0:T(8,128)(2,1)S(1)} %broadcast_in_dim.51, f16[8,2,8,4,1024]{4,2,3,1,0:T(8,128)(2,1)S(1)} %bitcast.66), kind=kLoop, calls=%fused_computation.10 | loop fusion | flops 589824 | bytes 2359296 | tf_op jit(solution)/shard_map/concatenate | solution.py:91
  23.2 8.2 %all-to-all-start = ((f16[8,2,8,4,1152]{4,2,3,1,0:T(8,128)(2,1)}), f16[8,2,8,4,1152]{4,2,3,1,0:T(8,128)(2,1)}, u32[]{:S(2)}, u32[]{:S(2)}) async-start(f16[8,2,8,4,1152]{4,2,3,1,0:T(8,128)(2,1)} %pad_maximum_fusion), calls=%async_computation | async-start | bytes 2359296 | tf_op jit(solution)/shard_map/all_to_all | solution.py:93
  32.1 0.7 reduce.11
  33.2 6.2 %gather_fusion.1 = bf16[2048,16]{1,0:T(8,128)(2,1)S(1)} fusion(bf16[1024,16]{1,0:T(8,128)(2,1)S(1)} %copy.32, s32[2048]{0:T(1024)S(1)} %broadcast_clamp_fusion.1), kind=kCustom, calls=%fused_computation.1 | custom fusion | bytes 139264 | tf_op jit(solution)/shard_map/jit(_take)/gather | solution.py:113
  39.6 9.9 %gather_fusion.2 = bf16[2048,1280]{1,0:T(8,128)(2,1)} fusion(bf16[1024,1280]{1,0:T(8,128)(2,1)S(1)} %copy-done, s32[2048]{0:T(1024)S(1)} %broadcast_clamp_fusion), kind=kCustom, calls=%fused_computation.2 | custom fusion | bytes 10493952 | tf_op jit(solution)/shard_map/jit(_take)/gather | solution.py:114
  49.5 14.0 %all-to-all-done = f16[8,2,8,4,1152]{4,2,3,1,0:T(8,128)(2,1)} async-done(((f16[8,2,8,4,1152]{4,2,3,1,0:T(8,128)(2,1)}), f16[8,2,8,4,1152]{4,2,3,1,0:T(8,128)(2,1)}, u32[]{:S(2)}, u32[]{:S(2)}) %all-to-all-start) | async-done | bytes 1179680 | tf_op jit(solution)/shard_map/all_to_all | solution.py:93
  63.5 0.7 fusion.11
  64.5 1.9 %fusion.3 = bf16[2,16,4,1024]{3,1,2,0:T(8,128)(2,1)S(1)} fusion(f16[8,2,8,4,1152]{4,2,3,1,0:T(8,128)(2,1)} %all-to-all-done, f32[8,8,128]{2,1,0:T(8,128)S(1)} %fusion.11, f32[8]{0:T(128)S(1)} %fusion.16), kind=kOutput, calls=%fused_computation.11 | convolution fusion | flops 50463744 | bytes 1343520 | tf_op jit(solution)/shard_map/ptg,pjtks->jgks/dot_general | solution.py:98
  67.2 0.9 copy.30
  68.1 1.3 %reshape.65 = bf16[2,64,32,40]{1,0,3,2:T(2,128)(2,1)S(1)} reshape(bf16[128,1280]{0,1:T(8,128)(2,1)} %copy.30) | data formatting | bytes 655360 | tf_op jit(solution)/shard_map/reshape | solution.py:108
  69.4 1.1 %reshape.112 = bf16[32,2,2560]{2,1,0:T(2,128)(2,1)} reshape(bf16[32,40,2,64]{3,2,1,0:T(2,128)(2,1)S(1)} %bitcast.67) | data formatting | bytes 655360
  70.5 7.6 %all-to-all-start.1 = ((bf16[32,2,2560]{2,1,0:T(2,128)(2,1)}), bf16[32,2,2560]{2,1,0:T(2,128)(2,1)}, u32[]{:S(2)}, u32[]{:S(2)}) async-start(bf16[32,2,2560]{2,1,0:T(2,128)(2,1)} %reshape.112), calls=%async_computation.1 | async-start | bytes 655360 | tf_op jit(solution)/shard_map/all_to_all | solution.py:109
  78.1 0.7 convert_bitcast_fusion.occ_ref
  78.8 8.9 %all-to-all-done.1 = bf16[32,2,2560]{2,1,0:T(2,128)(2,1)} async-done(((bf16[32,2,2560]{2,1,0:T(2,128)(2,1)}), bf16[32,2,2560]{2,1,0:T(2,128)(2,1)}, u32[]{:S(2)}, u32[]{:S(2)}) %all-to-all-start.1) | async-done | bytes 327712 | tf_op jit(solution)/shard_map/all_to_all | solution.py:109
  87.7 1.4 %reshape.113 = bf16[32,40,2,64]{3,2,1,0:T(2,128)(2,1)S(1)} reshape(bf16[32,2,2560]{2,1,0:T(2,128)(2,1)} %all-to-all-done.1) | data formatting | bytes 655360
  89.8 1.3 %reshape.66 = bf16[2,2048,40]{1,2,0:T(8,128)(2,1)} reshape(bf16[2,32,64,1,40]{2,1,4,0,3:T(8,128)(2,1)S(1)} %copy.31) | data formatting | bytes 655360 | tf_op jit(solution)/shard_map/reshape | solution.py:111
  91.0 11.5 %shard_map.82 = f32[2,40,20480]{2,1,0:T(8,128)} custom-call(bf16[2,40,2048]{2,1,0:T(8,128)(2,1)} %bitcast.68, f32[16,2048]{1,0:T(8,128)} %convert_bitcast_fusion.occ_ref, bf16[2048,1280]{1,0:T(8,128)(2,1)} %gather_fusion.2), custom_call_target="tpu_custom_call" | custom-call | tf_op jit(solution)/shard_map/pallas_call | solution.py:29
  (31 shorter events, 5.0 us)
Async XLA Ops:
  0.0 39.6 %copy-start = (bf16[1024,1280]{1,0:T(8,128)(2,1)S(1)}, bf16[1024,1280]{1,0:T(8,128)(2,1)}, u32[]{:S(2)}) copy-start(bf16[1024,1280]{1,0:T(8,128)(2,1)} %param.15) | copy-start | bytes 7864324
  1.5 21.6 %all-to-all-start.2 = ((s32[32,1,128]{2,1,0:T(1,128)}), s32[32,1,128]{2,1,0:T(1,128)S(1)}, u32[]{:S(2)}, u32[]{:S(2)}) async-start(s32[32,1,128]{2,1,0:T(1,128)} %reshape.114), calls=%async_computation.2 | async-start | bytes 32768 | tf_op jit(solution)/shard_map/all_to_all | solution.py:58
  21.6 9.7 %copy-start.1 = (bf16[1024,16]{0,1:T(8,128)(2,1)S(1)}, bf16[1024,16]{0,1:T(8,128)(2,1)}, u32[]{:S(2)}) copy-start(bf16[1024,16]{0,1:T(8,128)(2,1)} %param.14) | copy-start | bytes 98308
  23.2 40.3 %all-to-all-start = ((f16[8,2,8,4,1152]{4,2,3,1,0:T(8,128)(2,1)}), f16[8,2,8,4,1152]{4,2,3,1,0:T(8,128)(2,1)}, u32[]{:S(2)}, u32[]{:S(2)}) async-start(f16[8,2,8,4,1152]{4,2,3,1,0:T(8,128)(2,1)} %pad_maximum_fusion), calls=%async_computation | async-start | bytes 2359296 | tf_op jit(solution)/shard_map/all_to_all | solution.py:93
  70.5 17.2 %all-to-all-start.1 = ((bf16[32,2,2560]{2,1,0:T(2,128)(2,1)}), bf16[32,2,2560]{2,1,0:T(2,128)(2,1)}, u32[]{:S(2)}, u32[]{:S(2)}) async-start(bf16[32,2,2560]{2,1,0:T(2,128)(2,1)} %reshape.112), calls=%async_computation.1 | async-start | bytes 655360 | tf_op jit(solution)/shard_map/all_to_all | solution.py:109

commit v16 on v15

--- a/solution.py
+++ b/solution.py
@@ -53,10 +53,12 @@
     vir_share = vir_total // pair_count
 
     index_copies = jnp.broadcast_to(
-        jnp.stack([mu_index, nu_index])[None], (pair_count, 2, rows_here)
+        jnp.concatenate([mu_index, nu_index])[None], (pair_count, 2 * rows_here)
     )
     both_index = lax.all_to_all(index_copies, "pair", split_axis=0, concat_axis=0, tiled=True)
-    both_index = jnp.transpose(both_index, (1, 0, 2)).reshape(2, pair_count * rows_here)
+    both_index = jnp.stack(
+        [both_index[:, :rows_here].reshape(-1), both_index[:, rows_here:].reshape(-1)]
+    )
 
     tile_data = integrals[0]
     slot_count, tile_rows, tile_depth, _ = tile_data.shape

time: 103 us -> 103 us (level)
  waiting for transfers between devices: 23 us -> 24.4 us
    all_to_all x1, waiting for transfers between devices: 14 us -> 15.4 us  [on_device(): lax.all_to_all(payload, 'lam', split_axis=0, concat_axis=0, tiled=True)]
    unnamed x9 -> x7, local copies, waits for them, and re-layouts: 3.51 us -> 2.73 us
  transfers between devices with their start and end apart: 3 -> 3, of which waited for: 2 -> 2; matrix products, arithmetic and copies ran while one was open for 30% -> 28% of each run, Pallas kernels for 0% -> 0%
where the time goes in v16:
time: 103 us
  local copies, waits for them, and re-layouts  26.4 us (26%)
  starting transfers between devices  24.4 us (24%)
  waiting for transfers between devices  24.4 us (24%)
  Pallas kernels  11.5 us (11%)
  matrix products  7.29 us (7%)
  other arithmetic  7.11 us (7%)
  between operations  1.47 us (1%)
    all_to_all x1, waiting for transfers between devices, on_device(): lax.all_to_all(payload, 'lam', split_axis=0, concat_axis=0, tiled=True)  15.4 us
    pallas_call x1, Pallas kernels, final_contract(): pl.pallas_call(contract_kernel, grid=(occ_share,), in_specs=[pl.BlockSpec...  11.5 us
    gather x1, local copies, waits for them, and re-layouts, on_device(): vir_rows = jnp.take(virtual_coef, both_index[1], axis=0, mode='clip')  9.93 us
    all_to_all x1, waiting for transfers between devices, on_device(): lax.all_to_all(mixed, 'pair', split_axis=2, concat_axis=1, tiled=True)  8.93 us
    all_to_all x1, starting transfers between devices, on_device(): lax.all_to_all(index_copies, 'pair', split_axis=0, concat_axis=0, tiled=T...  8.59 us
    all_to_all x1, starting transfers between devices, on_device(): lax.all_to_all(payload, 'lam', split_axis=0, concat_axis=0, tiled=True)  8.19 us
    all_to_all x1, starting transfers between devices, on_device(): lax.all_to_all(mixed, 'pair', split_axis=2, concat_axis=1, tiled=True)  7.6 us
    gather x2, local copies, waits for them, and re-layouts, on_device(): occ_rows = jnp.take(occupied_coef, both_index[0], axis=0, mode='clip')  6.36 us
  transfers between devices with their start and end apart: 3, of which 2 were waited for; matrix products, arithmetic and copies ran while one was open for 28% of the time, Pallas kernels for 0%

profile of v16, /device:TPU:1, one launch (start us, length us, event | category | flops | bytes accessed | tf_op | source)
XLA Modules:
  0.0 102.5 jit_solution(4506133258153868616)
XLA Ops:
  0.0 0.9 pad_add_fusion
  1.5 8.6 %all-to-all-start.2 = ((s32[32,1,128]{2,1,0:T(1,128)}), s32[32,1,128]{2,1,0:T(1,128)S(1)}, u32[]{:S(2)}, u32[]{:S(2)}) async-start(s32[32,1,128]{2,1,0:T(1,128)} %broadcast_in_dim.52), calls=%async_computation.2 | async-start | bytes 32768 | tf_op jit(solution)/shard_map/all_to_all | solution.py:58
  10.8 0.7 pad_clamp_fusion
  11.4 0.9 reshape.63
  12.3 0.7 convert_convert_fusion
  13.6 4.8 %abs_reduce_fusion = (f32[]{:T(128)}, f32[8,16,4,1024]{3,1,2,0:T(8,128)}) fusion(bf16[1,8,4,64,1024]{4,3,2,1,0:T(8,128)(2,1)} %param.8, bf16[8,64,16]{1,2,0:T(8,128)(2,1)S(1)} %gather_fusion, pred[8]{0:T(512)(128)(4,1)S(1)} %iota_compare_fusion.1), kind=kOutput, calls=%fused_computation.7 | convolution fusion | flops 68165632 | bytes 6307852 | tf_op jit(solution)/shard_map/tmj,tkms->jtks/dot_general | solution.py:72
  19.1 1.9 %fusion.4 = f16[16,8,4,1024]{3,0,2,1:T(8,128)(2,1)S(1)} fusion(f32[8,16,4,1024]{3,1,2,0:T(8,128)} %get-tuple-element.8, f32[]{:T(128)S(6)} %exp2.15), kind=kLoop, calls=%fused_computation.12 | loop fusion | flops 1048576 | bytes 3145732 | tf_op jit(solution)/shard_map/convert_element_type | solution.py:77
  21.0 0.6 copy.37
  21.8 1.3 %pad_maximum_fusion = f16[8,2,8,4,1152]{4,2,3,1,0:T(8,128)(2,1)} fusion(f16[8,2,8,4,128]{4,2,3,1,0:T(8,128)(2,1)S(1)} %broadcast_in_dim.51, f16[8,2,8,4,1024]{4,2,3,1,0:T(8,128)(2,1)S(1)} %bitcast.64), kind=kLoop, calls=%fused_computation.10 | loop fusion | flops 589824 | bytes 2359296 | tf_op jit(solution)/shard_map/concatenate | solution.py:93
  23.1 8.2 %all-to-all-start = ((f16[8,2,8,4,1152]{4,2,3,1,0:T(8,128)(2,1)}), f16[8,2,8,4,1152]{4,2,3,1,0:T(8,128)(2,1)}, u32[]{:S(2)}, u32[]{:S(2)}) async-start(f16[8,2,8,4,1152]{4,2,3,1,0:T(8,128)(2,1)} %pad_maximum_fusion), calls=%async_computation | async-start | bytes 2359296 | tf_op jit(solution)/shard_map/all_to_all | solution.py:95
  31.7 6.2 %gather_fusion.1 = bf16[2048,16]{1,0:T(8,128)(2,1)S(1)} fusion(bf16[1024,16]{1,0:T(8,128)(2,1)S(1)} %copy.32, s32[2048]{0:T(1024)S(1)} %broadcast_clamp_fusion.1), kind=kCustom, calls=%fused_computation.1 | custom fusion | bytes 139264 | tf_op jit(solution)/shard_map/jit(_take)/gather | solution.py:115
  38.1 9.9 %gather_fusion.2 = bf16[2048,1280]{1,0:T(8,128)(2,1)} fusion(bf16[1024,1280]{1,0:T(8,128)(2,1)S(1)} %copy-done, s32[2048]{0:T(1024)S(1)} %broadcast_clamp_fusion), kind=kCustom, calls=%fused_computation.2 | custom fusion | bytes 10493952 | tf_op jit(solution)/shard_map/jit(_take)/gather | solution.py:116
  48.1 15.4 %all-to-all-done = f16[8,2,8,4,1152]{4,2,3,1,0:T(8,128)(2,1)} async-done(((f16[8,2,8,4,1152]{4,2,3,1,0:T(8,128)(2,1)}), f16[8,2,8,4,1152]{4,2,3,1,0:T(8,128)(2,1)}, u32[]{:S(2)}, u32[]{:S(2)}) %all-to-all-start) | async-done | bytes 1179680 | tf_op jit(solution)/shard_map/all_to_all | solution.py:95
  63.5 0.7 fusion.11
  64.4 1.9 %fusion.3 = bf16[2,16,4,1024]{3,1,2,0:T(8,128)(2,1)S(1)} fusion(f16[8,2,8,4,1152]{4,2,3,1,0:T(8,128)(2,1)} %all-to-all-done, f32[8,8,128]{2,1,0:T(8,128)S(1)} %fusion.11, f32[8]{0:T(128)S(1)} %fusion.16), kind=kOutput, calls=%fused_computation.11 | convolution fusion | flops 50463744 | bytes 1343520 | tf_op jit(solution)/shard_map/ptg,pjtks->jgks/dot_general | solution.py:100
  67.2 0.9 copy.30
  68.1 1.3 %reshape.65 = bf16[2,64,32,40]{1,0,3,2:T(2,128)(2,1)S(1)} reshape(bf16[128,1280]{0,1:T(8,128)(2,1)} %copy.30) | data formatting | bytes 655360 | tf_op jit(solution)/shard_map/reshape | solution.py:110
  69.4 1.1 %reshape.100 = bf16[32,2,2560]{2,1,0:T(2,128)(2,1)} reshape(bf16[32,40,2,64]{3,2,1,0:T(2,128)(2,1)S(1)} %bitcast.65) | data formatting | bytes 655360
  70.5 7.6 %all-to-all-start.1 = ((bf16[32,2,2560]{2,1,0:T(2,128)(2,1)}), bf16[32,2,2560]{2,1,0:T(2,128)(2,1)}, u32[]{:S(2)}, u32[]{:S(2)}) async-start(bf16[32,2,2560]{2,1,0:T(2,128)(2,1)} %reshape.100), calls=%async_computation.1 | async-start | bytes 655360 | tf_op jit(solution)/shard_map/all_to_all | solution.py:111
  78.1 0.7 convert_bitcast_fusion.occ_ref
  78.8 8.9 %all-to-all-done.1 = bf16[32,2,2560]{2,1,0:T(2,128)(2,1)} async-done(((bf16[32,2,2560]{2,1,0:T(2,128)(2,1)}), bf16[32,2,2560]{2,1,0:T(2,128)(2,1)}, u32[]{:S(2)}, u32[]{:S(2)}) %all-to-all-start.1) | async-done | bytes 327712 | tf_op jit(solution)/shard_map/all_to_all | solution.py:111
  87.7 1.4 %reshape.101 = bf16[32,40,2,64]{3,2,1,0:T(2,128)(2,1)S(1)} reshape(bf16[32,2,2560]{2,1,0:T(2,128)(2,1)} %all-to-all-done.1) | data formatting | bytes 655360
  89.8 1.3 %reshape.66 = bf16[2,2048,40]{1,2,0:T(8,128)(2,1)} reshape(bf16[2,32,64,1,40]{2,1,4,0,3:T(8,128)(2,1)S(1)} %copy.31) | data formatting | bytes 655360 | tf_op jit(solution)/shard_map/reshape | solution.py:113
  91.0 11.5 %shard_map.82 = f32[2,40,20480]{2,1,0:T(8,128)} custom-call(bf16[2,40,2048]{2,1,0:T(8,128)(2,1)} %bitcast.66, f32[16,2048]{1,0:T(8,128)} %convert_bitcast_fusion.occ_ref, bf16[2048,1280]{1,0:T(8,128)(2,1)} %gather_fusion.2), custom_call_target="tpu_custom_call" | custom-call | tf_op jit(solution)/shard_map/pallas_call | solution.py:29
  (27 shorter events, 3.6 us)
Async XLA Ops:
  0.0 38.1 %copy-start = (bf16[1024,1280]{1,0:T(8,128)(2,1)S(1)}, bf16[1024,1280]{1,0:T(8,128)(2,1)}, u32[]{:S(2)}) copy-start(bf16[1024,1280]{1,0:T(8,128)(2,1)} %param.15) | copy-start | bytes 7864324
  1.5 21.6 %all-to-all-start.2 = ((s32[32,1,128]{2,1,0:T(1,128)}), s32[32,1,128]{2,1,0:T(1,128)S(1)}, u32[]{:S(2)}, u32[]{:S(2)}) async-start(s32[32,1,128]{2,1,0:T(1,128)} %broadcast_in_dim.52), calls=%async_computation.2 | async-start | bytes 32768 | tf_op jit(solution)/shard_map/all_to_all | solution.py:58
  21.6 9.7 %copy-start.1 = (bf16[1024,16]{0,1:T(8,128)(2,1)S(1)}, bf16[1024,16]{0,1:T(8,128)(2,1)}, u32[]{:S(2)}) copy-start(bf16[1024,16]{0,1:T(8,128)(2,1)} %param.14) | copy-start | bytes 98308
  23.1 40.3 %all-to-all-start = ((f16[8,2,8,4,1152]{4,2,3,1,0:T(8,128)(2,1)}), f16[8,2,8,4,1152]{4,2,3,1,0:T(8,128)(2,1)}, u32[]{:S(2)}, u32[]{:S(2)}) async-start(f16[8,2,8,4,1152]{4,2,3,1,0:T(8,128)(2,1)} %pad_maximum_fusion), calls=%async_computation | async-start | bytes 2359296 | tf_op jit(solution)/shard_map/all_to_all | solution.py:95
  70.5 17.2 %all-to-all-start.1 = ((bf16[32,2,2560]{2,1,0:T(2,128)(2,1)}), bf16[32,2,2560]{2,1,0:T(2,128)(2,1)}, u32[]{:S(2)}, u32[]{:S(2)}) async-start(bf16[32,2,2560]{2,1,0:T(2,128)(2,1)} %reshape.100), calls=%async_computation.1 | async-start | bytes 655360 | tf_op jit(solution)/shard_map/all_to_all | solution.py:111

commit v17 on v15

--- a/solution.py
+++ b/solution.py
@@ -26,17 +26,18 @@
     occ_share, vir_share, total_rows = mixed_t.shape
     occ_total = occ_t.shape[0]
     vir_total = vir_rows.shape[1]
+    occ_step = occ_total // 2
     return pl.pallas_call(
         contract_kernel,
-        grid=(occ_share,),
+        grid=(occ_share, 2),
         in_specs=[
-            pl.BlockSpec((1, vir_share, total_rows), lambda n: (n, 0, 0)),
-            pl.BlockSpec((occ_total, total_rows), lambda n: (0, 0)),
-            pl.BlockSpec((total_rows, vir_total), lambda n: (0, 0)),
+            pl.BlockSpec((1, vir_share, total_rows), lambda n, h: (n, 0, 0)),
+            pl.BlockSpec((occ_step, total_rows), lambda n, h: (h, 0)),
+            pl.BlockSpec((total_rows, vir_total), lambda n, h: (0, 0)),
         ],
-        out_specs=pl.BlockSpec((1, vir_share, occ_total * vir_total), lambda n: (n, 0, 0)),
+        out_specs=pl.BlockSpec((1, vir_share, occ_step * vir_total), lambda n, h: (n, 0, h)),
         out_shape=jax.ShapeDtypeStruct((occ_share, vir_share, occ_total * vir_total), jnp.float32),
-        scratch_shapes=[pltpu.VMEM((occ_total * vir_share, total_rows), jnp.float32)],
+        scratch_shapes=[pltpu.VMEM((occ_step * vir_share, total_rows), jnp.float32)],
         interpret=interpret,
     )(mixed_t, occ_t, vir_rows)
 

time: 103 us -> 103 us (level)
  no operation moved by 1% of the time
where the time goes in v17:
time: 103 us; the launch traced here: 102 us
  local copies, waits for them, and re-layouts  27.2 us (26%)
  starting transfers between devices  24.4 us (24%)
  waiting for transfers between devices  23 us (22%)
  Pallas kernels  11.3 us (11%)
  other arithmetic  7.77 us (8%)
  matrix products  7.29 us (7%)
  between operations  1.49 us (1%)
    all_to_all x1, waiting for transfers between devices, on_device(): lax.all_to_all(payload, 'lam', split_axis=0, concat_axis=0, tiled=True)  14 us
    pallas_call x1, Pallas kernels, final_contract(): pl.pallas_call(contract_kernel, grid=(occ_share, 2), in_specs=[pl.BlockSp...  11.3 us
    gather x1, local copies, waits for them, and re-layouts, on_device(): vir_rows = jnp.take(virtual_coef, both_index[1], axis=0, mode='clip')  9.9 us
    all_to_all x1, waiting for transfers between devices, on_device(): lax.all_to_all(mixed, 'pair', split_axis=2, concat_axis=1, tiled=True)  8.93 us
    all_to_all x1, starting transfers between devices, on_device(): lax.all_to_all(index_copies, 'pair', split_axis=0, concat_axis=0, tiled=T...  8.59 us
    all_to_all x1, starting transfers between devices, on_device(): lax.all_to_all(payload, 'lam', split_axis=0, concat_axis=0, tiled=True)  8.19 us
    all_to_all x1, starting transfers between devices, on_device(): lax.all_to_all(mixed, 'pair', split_axis=2, concat_axis=1, tiled=True)  7.6 us
    gather x2, local copies, waits for them, and re-layouts, on_device(): occ_rows = jnp.take(occupied_coef, both_index[0], axis=0, mode='clip')  6.36 us
  transfers between devices with their start and end apart: 3, of which 2 were waited for; matrix products, arithmetic and copies ran while one was open for 30% of the time, Pallas kernels for 0%

profile of v17, /device:TPU:1, one launch (start us, length us, event | category | flops | bytes accessed | tf_op | source)
XLA Modules:
  0.0 102.4 jit_solution(7758449869393732716)
XLA Ops:
  0.0 0.8 pad_add_fusion
  0.8 0.7 reshape.114
  1.5 8.6 %all-to-all-start.2 = ((s32[32,1,128]{2,1,0:T(1,128)}), s32[32,1,128]{2,1,0:T(1,128)S(1)}, u32[]{:S(2)}, u32[]{:S(2)}) async-start(s32[32,1,128]{2,1,0:T(1,128)} %reshape.114), calls=%async_computation.2 | async-start | bytes 32768 | tf_op jit(solution)/shard_map/all_to_all | solution.py:59
  11.5 0.9 reshape.63
  12.4 0.7 convert_convert_fusion
  13.7 4.8 %abs_reduce_fusion = (f32[]{:T(128)}, f32[8,16,4,1024]{3,1,2,0:T(8,128)}) fusion(bf16[1,8,4,64,1024]{4,3,2,1,0:T(8,128)(2,1)} %param.8, bf16[8,64,16]{1,2,0:T(8,128)(2,1)S(1)} %gather_fusion, pred[8]{0:T(512)(128)(4,1)S(1)} %iota_compare_fusion.1), kind=kOutput, calls=%fused_computation.7 | convolution fusion | flops 68165632 | bytes 6307852 | tf_op jit(solution)/shard_map/tmj,tkms->jtks/dot_general | solution.py:71
  19.1 1.9 %fusion.4 = f16[16,8,4,1024]{3,0,2,1:T(8,128)(2,1)S(1)} fusion(f32[8,16,4,1024]{3,1,2,0:T(8,128)} %get-tuple-element.8, f32[]{:T(128)S(6)} %exp2.15), kind=kLoop, calls=%fused_computation.12 | loop fusion | flops 1048576 | bytes 3145732 | tf_op jit(solution)/shard_map/convert_element_type | solution.py:76
  21.8 1.3 %pad_maximum_fusion = f16[8,2,8,4,1152]{4,2,3,1,0:T(8,128)(2,1)} fusion(f16[8,2,8,4,128]{4,2,3,1,0:T(8,128)(2,1)S(1)} %broadcast_in_dim.51, f16[8,2,8,4,1024]{4,2,3,1,0:T(8,128)(2,1)S(1)} %bitcast.66), kind=kLoop, calls=%fused_computation.10 | loop fusion | flops 589824 | bytes 2359296 | tf_op jit(solution)/shard_map/concatenate | solution.py:92
  23.2 8.2 %all-to-all-start = ((f16[8,2,8,4,1152]{4,2,3,1,0:T(8,128)(2,1)}), f16[8,2,8,4,1152]{4,2,3,1,0:T(8,128)(2,1)}, u32[]{:S(2)}, u32[]{:S(2)}) async-start(f16[8,2,8,4,1152]{4,2,3,1,0:T(8,128)(2,1)} %pad_maximum_fusion), calls=%async_computation | async-start | bytes 2359296 | tf_op jit(solution)/shard_map/all_to_all | solution.py:94
  32.1 0.7 reduce.11
  33.2 6.2 %gather_fusion.1 = bf16[2048,16]{1,0:T(8,128)(2,1)S(1)} fusion(bf16[1024,16]{1,0:T(8,128)(2,1)S(1)} %copy.32, s32[2048]{0:T(1024)S(1)} %broadcast_clamp_fusion.1), kind=kCustom, calls=%fused_computation.1 | custom fusion | bytes 139264 | tf_op jit(solution)/shard_map/jit(_take)/gather | solution.py:114
  39.6 9.9 %gather_fusion.2 = bf16[2048,1280]{1,0:T(8,128)(2,1)} fusion(bf16[1024,1280]{1,0:T(8,128)(2,1)S(1)} %copy-done, s32[2048]{0:T(1024)S(1)} %broadcast_clamp_fusion), kind=kCustom, calls=%fused_computation.2 | custom fusion | bytes 10493952 | tf_op jit(solution)/shard_map/jit(_take)/gather | solution.py:115
  49.5 14.0 %all-to-all-done = f16[8,2,8,4,1152]{4,2,3,1,0:T(8,128)(2,1)} async-done(((f16[8,2,8,4,1152]{4,2,3,1,0:T(8,128)(2,1)}), f16[8,2,8,4,1152]{4,2,3,1,0:T(8,128)(2,1)}, u32[]{:S(2)}, u32[]{:S(2)}) %all-to-all-start) | async-done | bytes 1179680 | tf_op jit(solution)/shard_map/all_to_all | solution.py:94
  63.5 0.7 fusion.11
  64.5 1.9 %fusion.3 = bf16[2,16,4,1024]{3,1,2,0:T(8,128)(2,1)S(1)} fusion(f16[8,2,8,4,1152]{4,2,3,1,0:T(8,128)(2,1)} %all-to-all-done, f32[8,8,128]{2,1,0:T(8,128)S(1)} %fusion.11, f32[8]{0:T(128)S(1)} %fusion.16), kind=kOutput, calls=%fused_computation.11 | convolution fusion | flops 50463744 | bytes 1343520 | tf_op jit(solution)/shard_map/ptg,pjtks->jgks/dot_general | solution.py:99
  67.2 0.9 copy.30
  68.1 1.3 %reshape.65 = bf16[2,64,32,40]{1,0,3,2:T(2,128)(2,1)S(1)} reshape(bf16[128,1280]{0,1:T(8,128)(2,1)} %copy.30) | data formatting | bytes 655360 | tf_op jit(solution)/shard_map/reshape | solution.py:109
  69.4 1.1 %reshape.112 = bf16[32,2,2560]{2,1,0:T(2,128)(2,1)} reshape(bf16[32,40,2,64]{3,2,1,0:T(2,128)(2,1)S(1)} %bitcast.67) | data formatting | bytes 655360
  70.5 7.6 %all-to-all-start.1 = ((bf16[32,2,2560]{2,1,0:T(2,128)(2,1)}), bf16[32,2,2560]{2,1,0:T(2,128)(2,1)}, u32[]{:S(2)}, u32[]{:S(2)}) async-start(bf16[32,2,2560]{2,1,0:T(2,128)(2,1)} %reshape.112), calls=%async_computation.1 | async-start | bytes 655360 | tf_op jit(solution)/shard_map/all_to_all | solution.py:110
  78.1 0.7 convert_bitcast_fusion.occ_ref
  78.8 8.9 %all-to-all-done.1 = bf16[32,2,2560]{2,1,0:T(2,128)(2,1)} async-done(((bf16[32,2,2560]{2,1,0:T(2,128)(2,1)}), bf16[32,2,2560]{2,1,0:T(2,128)(2,1)}, u32[]{:S(2)}, u32[]{:S(2)}) %all-to-all-start.1) | async-done | bytes 327712 | tf_op jit(solution)/shard_map/all_to_all | solution.py:110
  87.7 1.4 %reshape.113 = bf16[32,40,2,64]{3,2,1,0:T(2,128)(2,1)S(1)} reshape(bf16[32,2,2560]{2,1,0:T(2,128)(2,1)} %all-to-all-done.1) | data formatting | bytes 655360
  89.8 1.3 %reshape.66 = bf16[2,2048,40]{1,2,0:T(8,128)(2,1)} reshape(bf16[2,32,64,1,40]{2,1,4,0,3:T(8,128)(2,1)S(1)} %copy.31) | data formatting | bytes 655360 | tf_op jit(solution)/shard_map/reshape | solution.py:112
  91.0 11.3 %shard_map.82 = f32[2,40,20480]{2,1,0:T(8,128)} custom-call(bf16[2,40,2048]{2,1,0:T(8,128)(2,1)} %bitcast.68, f32[16,2048]{1,0:T(8,128)} %convert_bitcast_fusion.occ_ref, bf16[2048,1280]{1,0:T(8,128)(2,1)} %gather_fusion.2), custom_call_target="tpu_custom_call" | custom-call | tf_op jit(solution)/shard_map/pallas_call | solution.py:30
  (31 shorter events, 5.0 us)
Async XLA Ops:
  0.0 39.6 %copy-start = (bf16[1024,1280]{1,0:T(8,128)(2,1)S(1)}, bf16[1024,1280]{1,0:T(8,128)(2,1)}, u32[]{:S(2)}) copy-start(bf16[1024,1280]{1,0:T(8,128)(2,1)} %param.15) | copy-start | bytes 7864324
  1.5 21.6 %all-to-all-start.2 = ((s32[32,1,128]{2,1,0:T(1,128)}), s32[32,1,128]{2,1,0:T(1,128)S(1)}, u32[]{:S(2)}, u32[]{:S(2)}) async-start(s32[32,1,128]{2,1,0:T(1,128)} %reshape.114), calls=%async_computation.2 | async-start | bytes 32768 | tf_op jit(solution)/shard_map/all_to_all | solution.py:59
  21.6 9.7 %copy-start.1 = (bf16[1024,16]{0,1:T(8,128)(2,1)S(1)}, bf16[1024,16]{0,1:T(8,128)(2,1)}, u32[]{:S(2)}) copy-start(bf16[1024,16]{0,1:T(8,128)(2,1)} %param.14) | copy-start | bytes 98308
  23.2 40.3 %all-to-all-start = ((f16[8,2,8,4,1152]{4,2,3,1,0:T(8,128)(2,1)}), f16[8,2,8,4,1152]{4,2,3,1,0:T(8,128)(2,1)}, u32[]{:S(2)}, u32[]{:S(2)}) async-start(f16[8,2,8,4,1152]{4,2,3,1,0:T(8,128)(2,1)} %pad_maximum_fusion), calls=%async_computation | async-start | bytes 2359296 | tf_op jit(solution)/shard_map/all_to_all | solution.py:94
  70.5 17.2 %all-to-all-start.1 = ((bf16[32,2,2560]{2,1,0:T(2,128)(2,1)}), bf16[32,2,2560]{2,1,0:T(2,128)(2,1)}, u32[]{:S(2)}, u32[]{:S(2)}) async-start(bf16[32,2,2560]{2,1,0:T(2,128)(2,1)} %reshape.112), calls=%async_computation.1 | async-start | bytes 655360 | tf_op jit(solution)/shard_map/all_to_all | solution.py:110
